TPU v7x, 512 devices: a whole 4x8x8 slice. The times are simulated.
512 devices in a mesh: row: 16 (over z_hi, x), col: 32 (over y, z_lo, core).
Axes of the slice: x: 4, y: 8, z: 8 (z_hi: 4, z_lo: 2; z = z_hi * 2 + z_lo), core: 2. Of those that a mesh axis runs over, the one named last changes fastest.
Arguments:
- slab: float32 [16384, 16384], P('row', 'col'), may hold values from -3 to 3
- u_codes: bfloat16 [2, 32, 512, 384], P(None, 'row', 'col'), may hold values from -0.8984375 to 0.8984375
- v_codes: bfloat16 [2, 32, 1024, 384], P(None, 'row', 'col'), may hold values from -0.1875 to 0.1875
- u_scale: float32 [2, 32, 384], replicated, may hold values from 0.5 to 2.5
- v_scale: float32 [2, 32, 384], replicated, may hold values from 0.5 to 2.5
- ranks: int32 [2, 32], replicated, may hold values from 64 to 384, as said below
- d_inverse: float32 [2, 2, 2, 512], replicated, may hold values from -0.6 to 2, as said below
Outputs:
- updated: float32 [16384, 16384], P('row', 'col')
Inputs may be any that keep to these rules, and one draw needn't show every extreme that they name: `ranks`: every rank is one of 64, 128, 256 and 384; every panel has a tile of rank 384. `d_inverse`: each 2 x 2 block is symmetric positive definite, its diagonal entries between 0.5 and 2, its off-diagonal entry under 0.3 times the root of their product in magnitude.
All inputs are finite; a program needn't handle non-finite values.
Results may differ from a plain program's by a relative error of at most 0.0042.
Values may be sent and summed in bfloat16 or wider, within the bound.
No kernel may reach another device: no remote copies, remote signals or barrier semaphores. Data moves between devices by JAX's collectives and lax.ppermute only.
A program may use at most 128 MiB of HBM per device.

v0:
```python
import jax
import jax.numpy as jnp
from jax import lax
from jax.sharding import PartitionSpec as P


def from_root(block, axis, owner):
    block = jnp.where(lax.axis_index(axis) == owner, block, jnp.zeros_like(block))
    return lax.psum(block, axis)


def column_weight(u_scale_k, v_scale_k, ranks_k):
    position = lax.broadcasted_iota(jnp.int32, u_scale_k.shape, 1)
    return jnp.where(position < ranks_k[:, None], u_scale_k * v_scale_k, jnp.float32(0.0))


def apply_inverse(d_block, codes):
    shape = codes.shape
    pairs = codes.reshape(shape[:-2] + (shape[-2] // 2, 2, shape[-1]))
    even = pairs[..., 0, :].astype(jnp.float32)
    odd = pairs[..., 1, :].astype(jnp.float32)
    first = d_block[0, 0][:, None] * even + d_block[0, 1][:, None] * odd
    second = d_block[1, 0][:, None] * even + d_block[1, 1][:, None] * odd
    return jnp.stack([first, second], axis=-2).reshape(shape).astype(jnp.bfloat16)


def tile_update(width, row_u, row_v, row_weight, col_scaled, col_weight, col_u):
    inner = lax.dot_general(
        row_v, col_scaled, (((0,), (0,)), ((), ())), preferred_element_type=jnp.float32
    )
    core = (row_weight[:width, None] * inner * col_weight[None, :]).astype(jnp.bfloat16)
    left = jnp.dot(row_u, core, preferred_element_type=jnp.float32).astype(jnp.bfloat16)
    return lax.dot_general(
        left, col_u, (((1,), (1,)), ((), ())), preferred_element_type=jnp.float32
    )


def panel_update(slab_rows, row_u, row_v, col_u, col_v, d_block, weight_all, first_tile, column):
    per_row = row_u.shape[0]
    rank_most = row_u.shape[-1]
    col_scaled = apply_inverse(d_block, col_v)
    row_weight = lax.dynamic_slice_in_dim(weight_all, first_tile, per_row, 0)
    col_weight = lax.dynamic_index_in_dim(weight_all, column, 0, keepdims=False)

    def one_tile(items):
        tile_u, tile_v, tile_weight = items
        return tile_update(rank_most, tile_u, tile_v, tile_weight, col_scaled, col_weight, col_u)

    update = lax.map(one_tile, (row_u, row_v, row_weight))
    return slab_rows - update.reshape(slab_rows.shape)


def deliver_columns(pick_u, pick_v, owner_row, consume, state):
    col_u, col_v = (from_root(pick_u, "row", owner_row), from_root(pick_v, "row", owner_row))
    result = consume(col_u, col_v, state)
    return result


def local(slab, u_codes, v_codes, u_scale, v_scale, ranks, d_inverse):
    per_row = lax.axis_size("col") // lax.axis_size("row")
    column = lax.axis_index("col")
    owner_row = column // per_row
    offset = column % per_row
    first_tile = lax.axis_index("row") * per_row
    panels = u_codes.shape[0]
    for k in range(panels):
        row_u, row_v = (
            lax.all_gather(u_codes[k], "col", axis=1, tiled=True),
            lax.all_gather(v_codes[k], "col", axis=1, tiled=True),
        )
        pick_u = lax.dynamic_index_in_dim(row_u, offset, 0, keepdims=False)
        pick_v = lax.dynamic_index_in_dim(row_v, offset, 0, keepdims=False)
        weight_all = column_weight(u_scale[k], v_scale[k], ranks[k])

        def consume_one(col_u, col_v, slab_now):
            return panel_update(
                slab_now, row_u, row_v, col_u, col_v, d_inverse[k], weight_all, first_tile, column
            )

        slab = deliver_columns(pick_u, pick_v, owner_row, consume_one, slab)
    return slab


def solution(mesh):
    in_specs = (
        P("row", "col"),
        P(None, "row", "col", None),
        P(None, "row", "col", None),
        P(),
        P(),
        P(),
        P(),
    )
    out_specs = P("row", "col")
    return jax.shard_map(local, mesh=mesh, in_specs=in_specs, out_specs=out_specs, check_vma=False)
```

profile of v0, /device:TPU:16, one launch (start us, length us, event | category | flops | bytes accessed | tf_op | source)
XLA Modules:
  0.0 381.7 jit_solution(7517112665492828945)
XLA Ops:
  6.5 1.5 fusion.34
  8.0 0.0 all-gather.7.cloned.1.call-update
  8.0 0.0 all-gather.9.cloned.1.call-start
  8.1 0.7 all-gather.9.cloned.1.call-update
  8.8 0.0 all-reduce.3.cloned.1.call-start
  8.8 0.8 fusion.35
  9.6 33.7 %all-gather = bf16[1,2,512,384]{3,2,1,0:T(8,128)(2,1)S(1)} all-gather(bf16[1,2,16,384]{3,2,1,0:T(8,128)(2,1)S(1)} %get-tuple-element.135), channel_id=2, replica_groups=mesh['row'=16,'col'=32] {'col'}, dimensions={2}, use_global_device_ids=true | all-gather | bytes 811008 | tf_op jit(solution)/shard_map/all_gather | solution.py:68
  43.4 0.8 select_bitcast_fusion.1
  44.2 34.9 %all-gather.2 = bf16[1,2,512,384]{3,2,1,0:T(8,128)(2,1)S(1)} all-gather(bf16[1,2,16,384]{3,2,1,0:T(8,128)(2,1)S(1)} %get-tuple-element.136), channel_id=4, replica_groups=mesh['row'=16,'col'=32] {'col'}, dimensions={2}, use_global_device_ids=true | all-gather | bytes 811008 | tf_op jit(solution)/shard_map/all_gather | solution.py:68
  79.0 0.8 select_bitcast_fusion
  79.8 0.7 all-gather.7.cloned.1.call-done
  80.5 69.1 %all-gather.9.cloned.1.call-done = bf16[1,2,1024,384]{3,2,1,0:T(8,128)(2,1)} async-done(((bf16[1,2,32,384]{3,2,1,0:T(8,128)(2,1)}), bf16[1,2,1024,384]{3,2,1,0:T(8,128)(2,1)}) %all-gather.9.cloned.1.call-update) | async-done | bytes 1572880 | tf_op jit(solution)/shard_map/all_gather | solution.py:69
  149.6 2.4 dynamic-slice_select_fusion
  152.0 2.2 reshape.104
  154.2 1.0 copy.10
  155.2 0.3 reshape.102
  155.5 0.0 copy-start.7
  155.5 0.0 copy-start.4
  155.5 0.0 copy-start.5
  155.5 0.0 copy-start.6
  155.5 1.0 copy.8
  156.5 0.0 all-reduce.3.cloned.1.call-update
  156.6 0.0 copy-done.7
  156.6 0.1 bitcast_select_fusion.1
  156.8 189.8 %all-reduce.3.cloned.1.call-done = (bf16[512,2,384]{2,0,1:T(8,128)(2,1)}, bf16[512,384]{1,0:T(8,128)(2,1)}, bf16[512,2,384]{2,0,1:T(8,128)(2,1)}, bf16[512,384]{1,0:T(8,128)(2,1)}) async-done(((bf16[512,2,384]{2,0,1:T(8,128)(2,1)}, bf16[512,384]{1,0:T(8,128)(2,1)}, bf16[512,2,384]{2,0,1:T(8,128)(2,1)}, bf16[512,384]{1,0:T(8,128)(2,1)}), (bf16[512,2,384]{2,0,1:T(8,128)(2,1)}, bf16[512,384]{1,0:T(8,128)(2,1)}, ...) | async-done | bytes 2359312 | tf_op jit(solution)/shard_map/psum | solution.py:9
  346.7 1.5 fusion.29
  348.1 0.1 pad_maximum_fusion.1
  348.2 0.8 copy.11
  349.1 1.2 convert_element_type.45
  350.2 0.3 fusion.25
  350.6 0.1 pad_maximum_fusion
  350.7 0.8 copy.9
  351.5 0.0 copy-start.3
  351.5 1.2 convert_element_type.42
  352.7 1.6 broadcast.49.clone
  354.4 6.9 %while.21 = (s32[]{:T(128)}, f32[2,512,512]{2,1,0:T(8,128)}, bf16[2,512,384]{2,1,0:T(8,128)(2,1)S(1)}, f32[2,384]{1,0:T(2,128)S(1)}, bf16[2,1024,384]{2,1,0:T(8,...) while((s32[]{:T(128)}, f32[2,512,512]{2,1,0:T(8,128)}, ...), condition=%wide.region_7.8_spmd, body=%wide.region_6.7_spmd.sunk | while | flops 654950400 | bytes 4004973 | solution.py:49
  354.4 1.7 fusion.70
  356.1 1.7 fusion.71
  357.8 1.7 fusion.70
  359.6 1.7 fusion.71
  361.3 0.2 broadcast.49.clone.1
  361.6 0.7 copy-done
  362.3 8.8 %while.20 = (s32[]{:T(128)}, f32[2,512,512]{2,1,0:T(8,128)S(1)}, bf16[2,512,384]{2,1,0:T(8,128)(2,1)S(1)}, f32[2,384]{1,0:T(2,128)S(1)}, bf16[2,1024,384]{2,1,0:...) while((s32[]{:T(128)}, f32[2,512,512]{2,1,0:T(8,128)S(1)}, ...), condition=%wide.region_3.4_spmd, body=%wide.region_2.3_spmd.sunk | while | flops 654950400 | bytes 4004973 | solution.py:49
  362.3 2.7 fusion.63
  365.0 1.7 fusion.64
  366.7 2.7 fusion.63
  369.4 1.7 fusion.64
  371.1 4.1 %bitcast_subtract_fusion = f32[1024,512]{1,0:T(8,128)} fusion(f32[2,512,512]{2,1,0:T(8,128)} %get-tuple-element.90, f32[1024,512]{1,0:T(8,128)} %param.11, f32[2,512,512]{2,1,0:T(8,128)S(1)} %get-tuple-element.89), kind=kLoop, calls=%fused_computation.26 | loop fusion | flops 1048576 | bytes 8388608 | tf_op jit(solution)/shard_map/sub | solution.py:50
  (21 shorter events, 0.2 us)
Async XLA Ops:
  6.5 74.0 %all-gather.7.cloned.1.call-start = ((), (), s32[]{:S(2)}) async-start(), calls=%async_computation | async-start | bytes 1622016 | tf_op jit(solution)/shard_map/all_gather | solution.py:69
  8.0 141.6 %all-gather.9.cloned.1.call-start = ((), (), s32[]{:S(2)}) async-start(), calls=%async_computation.1 | async-start | bytes 1622016 | tf_op jit(solution)/shard_map/all_gather | solution.py:69
  8.8 337.9 %all-reduce.3.cloned.1.call-start = ((), (), s32[]{:S(2)}) async-start(), calls=%async_computation.2 | async-start | bytes 4718592 | tf_op jit(solution)/shard_map/psum | solution.py:9
  155.5 1.1 copy-start.7
  155.5 1.1 copy-start.4
  155.5 1.1 copy-start.5
  155.5 1.3 copy-start.6
  348.1 2.1 copy-start.2
  351.5 2.9 copy-start.1
  351.5 2.8 copy-start.3
  361.3 1.0 copy-start
Sparse Core Ops, SparseCore 0:
  9.4 70.9 all-gather.6
  82.6 67.0 all-gather.8
  156.7 189.9 all-reduce.2
where the time goes:
time: 382 us
  waiting for transfers between devices  260 us (68%)
  blocking collectives  68.6 us (18%)
  matrix products  15.6 us (4%)
  local copies, waits for them, and re-layouts  13.5 us (4%)
  between operations  13.3 us (3%)
  other arithmetic  10.1 us (3%)
    psum x1, waiting for transfers between devices, from_root(): return lax.psum(block, axis)  190 us
    all_gather x2, waiting for transfers between devices, local(): lax.all_gather(v_codes[k], 'col', axis=1, tiled=True)  69.8 us
    all_gather x2, blocking collectives, local(): lax.all_gather(u_codes[k], 'col', axis=1, tiled=True)  68.6 us
    dot_general x4, matrix products, tile_update(): lax.dot_general(row_v, col_scaled, (((0,), (0,)), ((), ())), preferred_el...  8.82 us
  transfers between devices with their start and end apart: 3, of which 3 were waited for; matrix products, arithmetic and copies ran while one was open for 1% of the time, Pallas kernels for 0%

commit v1 on v0

v1 whole, which is shorter than its diff:
```python
import jax
import jax.numpy as jnp
from jax import lax
from jax.sharding import PartitionSpec as P


def column_weight(u_scale_k, v_scale_k, ranks_k):
    position = lax.broadcasted_iota(jnp.int32, u_scale_k.shape, 1)
    return jnp.where(position < ranks_k[:, None], u_scale_k * v_scale_k, jnp.float32(0.0))


def apply_inverse(d_block, codes):
    shape = codes.shape
    pairs = codes.reshape(shape[:-2] + (shape[-2] // 2, 2, shape[-1]))
    even = pairs[..., 0, :].astype(jnp.float32)
    odd = pairs[..., 1, :].astype(jnp.float32)
    first = d_block[0, 0][:, None] * even + d_block[0, 1][:, None] * odd
    second = d_block[1, 0][:, None] * even + d_block[1, 1][:, None] * odd
    return jnp.stack([first, second], axis=-2).reshape(shape).astype(jnp.bfloat16)


def local(slab, u_codes, v_codes, u_scale, v_scale, ranks, d_inverse):
    panels, per_row, u_rows, rank_most = u_codes.shape
    v_rows = v_codes.shape[2]
    n_col = lax.axis_size("col")
    column = lax.axis_index("col")
    first_tile = lax.axis_index("row") * per_row
    both = u_rows + v_rows

    shard = jnp.concatenate([u_codes, v_codes], axis=2)

    row_all = lax.all_gather(shard, "col", axis=2, tiled=True)
    row_all = row_all.reshape(panels, per_row, n_col, both, rank_most)
    row_u = row_all[:, :, :, :u_rows].reshape(panels, per_row, n_col * u_rows, rank_most)
    row_v = row_all[:, :, :, u_rows:].reshape(panels, per_row, n_col * v_rows, rank_most)

    every_tile = lax.all_gather(shard, "row", axis=1, tiled=True)
    col_all = lax.all_to_all(every_tile, "col", 1, 2, tiled=True)
    col_all = col_all.reshape(panels, n_col, both, rank_most)
    col_u = col_all[:, :, :u_rows].reshape(panels, n_col * u_rows, rank_most)
    col_v = col_all[:, :, u_rows:].reshape(panels, n_col * v_rows, rank_most)

    weight = jnp.stack(
        [column_weight(u_scale[k], v_scale[k], ranks[k]) for k in range(panels)]
    )
    row_weight = lax.dynamic_slice_in_dim(weight, first_tile, per_row, 1)
    col_weight = lax.dynamic_index_in_dim(weight, column, 1, keepdims=False)
    col_scaled = jnp.stack([apply_inverse(d_inverse[k], col_v[k]) for k in range(panels)])

    inner = jnp.einsum("kibr,kbq->kirq", row_v, col_scaled, preferred_element_type=jnp.float32)
    core = (row_weight[:, :, :, None] * inner * col_weight[:, None, None, :]).astype(jnp.bfloat16)
    left = jnp.einsum("kimr,kirq->kimq", row_u, core, preferred_element_type=jnp.float32)
    left = left.astype(jnp.bfloat16)
    update = jnp.einsum("kimq,knq->imn", left, col_u, preferred_element_type=jnp.float32)
    return slab - update.reshape(slab.shape)


def solution(mesh):
    in_specs = (
        P("row", "col"),
        P(None, "row", "col", None),
        P(None, "row", "col", None),
        P(),
        P(),
        P(),
        P(),
    )
    out_specs = P("row", "col")
    return jax.shard_map(local, mesh=mesh, in_specs=in_specs, out_specs=out_specs, check_vma=False)
```

time: 382 us -> 202 us (0.53)
  the two profiles are of different devices: /device:TPU:16 before, /device:TPU:1 now
where the time goes in v1:
time: 202 us
  waiting for transfers between devices  149 us (74%)
  local copies, waits for them, and re-layouts  17.8 us (9%)
  between operations  13.6 us (7%)
  matrix products  10.4 us (5%)
  starting transfers between devices  9.07 us (4%)
    all_to_all x1, waiting for transfers between devices, local(): col_all = lax.all_to_all(every_tile, 'col', 1, 2, tiled=True)  73.7 us
    all_gather x1, waiting for transfers between devices, local(): every_tile = lax.all_gather(shard, 'row', axis=1, tiled=True)  73.3 us
    all_to_all x1, starting transfers between devices, local(): col_all = lax.all_to_all(every_tile, 'col', 1, 2, tiled=True)  9.03 us
    dot_general x1, matrix products, local(): jnp.einsum('kimr,kirq->kimq', row_u, core, preferred_element_type=jnp.flo...  6.03 us
    another operation x2, local copies, waits for them, and re-layouts, apply_inverse(): pairs = codes.reshape(shape[:-2] + (shape[-2] // 2, 2, shape[-1]))  4.49 us
    dot_general x1, matrix products, local(): jnp.einsum('kimq,knq->imn', left, col_u, preferred_element_type=jnp.float32)  4.4 us
  transfers between devices with their start and end apart: 3, of which 3 were waited for; matrix products, arithmetic and copies ran while one was open for 7% of the time, Pallas kernels for 0%

profile of v1, /device:TPU:1, one launch (start us, length us, event | category | flops | bytes accessed | tf_op | source)
XLA Modules:
  0.0 201.7 jit_solution(8519008060118880257)
XLA Ops:
  6.5 0.0 all-gather.5.cloned.1.call-start
  6.5 0.9 pad_maximum_fusion.2
  7.5 0.7 copy.41
  8.1 0.0 all-gather.5.cloned.1.call-update
  8.1 0.0 all-gather.3.cloned.1.call-start
  8.2 0.7 all-gather.3.cloned.1.call-update
  8.9 0.0 copy-start.4
  8.9 0.0 copy-start.1
  8.9 0.0 copy-start.2
  8.9 0.0 copy-start.3
  8.9 73.3 %all-gather.5.cloned.1.call-done = bf16[2,32,48,384]{3,2,0,1:T(8,128)(2,1)} async-done(((bf16[2,2,48,384]{3,2,0,1:T(8,128)(2,1)}), bf16[2,32,48,384]{3,2,0,1:T(8,128)(2,1)}) %all-gather.5.cloned.1.call-update) | async-done | bytes 2359312 | tf_op jit(solution)/shard_map/all_gather | solution.py:37
  82.2 9.0 %all-to-all-start = ((bf16[2,32,48,384]{3,2,0,1:T(8,128)(2,1)}), bf16[2,32,48,384]{3,2,0,1:T(8,128)(2,1)S(1)}, u32[]{:S(2)}, u32[]{:S(2)}) async-start(bf16[2,32,48,384]{3,2,0,1:T(8,128)(2,1)} %all-gather.5.cloned.1.call-done), calls=%async_computation | async-start | bytes 4718592 | tf_op jit(solution)/shard_map/all_to_all | solution.py:38
  91.3 0.0 copy-done.4
  91.3 0.0 copy-done.1
  91.3 0.0 copy-done.2
  91.3 0.1 multiply_select_fusion
  91.4 0.0 copy-done.3
  91.5 73.7 %all-to-all-done = bf16[2,32,48,384]{3,2,0,1:T(8,128)(2,1)S(1)} async-done(((bf16[2,32,48,384]{3,2,0,1:T(8,128)(2,1)}), bf16[2,32,48,384]{3,2,0,1:T(8,128)(2,1)S(1)}, u32[]{:S(2)}, u32[]{:S(2)}) %all-to-all-start) | async-done | bytes 2359328 | tf_op jit(solution)/shard_map/all_to_all | solution.py:38
  165.2 1.3 fusion.14
  166.5 2.2 %reshape_squeeze.7 = bf16[512,2,384]{2,1,0:T(2,128)(2,1)S(1)} reshape(bf16[1,32,32,384]{3,2,0,1:T(8,128)(2,1)} %get-tuple-element.6) | data formatting | bytes 1572864 | tf_op jit(solution)/shard_map/reshape;squeeze | solution.py:14
  168.7 1.1 fusion.16
  169.8 0.3 fusion.7
  170.1 0.1 pad_maximum_fusion.1
  170.2 0.8 copy.36
  171.0 1.2 convert_element_type.57
  172.2 2.3 %reshape_squeeze.6 = bf16[512,2,384]{2,1,0:T(2,128)(2,1)S(1)} reshape(bf16[1,32,32,384]{3,2,0,1:T(8,128)(2,1)} %get-tuple-element.5) | data formatting | bytes 1572864 | tf_op jit(solution)/shard_map/reshape;squeeze | solution.py:14
  174.6 1.1 fusion.15
  175.7 0.3 fusion.3
  176.0 0.1 pad_maximum_fusion
  176.1 0.8 copy.33
  176.9 1.2 convert_element_type.54
  178.1 0.1 slice.127
  178.2 0.1 copy.38
  178.3 1.1 all-gather.3.cloned.1.call-done
  179.4 2.8 %copy.30 = bf16[2,2,1536,384]{3,2,1,0:T(8,128)(2,1)S(1)} copy(bf16[2,2,1536,384]{3,2,0,1:T(8,128)(2,1)} %all-gather.3.cloned.1.call-done) | data formatting | bytes 9437184 | tf_op jit(solution)/shard_map/all_gather | solution.py:32
  182.2 0.2 slice.111
  182.4 0.0 copy-start
  182.4 2.0 %slice.112 = bf16[2,2,32,32,384]{4,3,2,1,0:T(8,128)(2,1)} slice(bf16[2,2,32,48,384]{4,3,2,1,0:T(8,128)(2,1)S(1)} %bitcast.48), slice={[0:2], [0:2], [0:32], [16:48], [0:384]} | slice | bytes 6291456 | tf_op jit(solution)/shard_map/slice | solution.py:35
  184.4 0.0 copy-done
  184.4 6.0 %convolution_convert_fusion = bf16[2,2,512,384]{3,2,1,0:T(8,128)(2,1)} fusion(bf16[2,2,512,384]{3,2,1,0:T(8,128)(2,1)S(1)} %bitcast.51, bf16[2,2,1024,384]{3,2,1,0:T(8,128)(2,1)} %bitcast.50, bf16[1,1024,384]{2,1,0:T(8,128)(2,1)S(1)} %copy-done, bf16[1,1024,384]{2,1,0:T(8,128)(2,1)} %convert_element_type.54, f32[2,384]{1,0:T(2,128)S(1)} %bitcast.61, ...), kind=kOutput, calls=%fused_computation.2 | convolution fusion | flops 1815281664 | bytes 7873536 | tf_op jit(solution)/shard_map/kimr,kirq->kimq/dot_general | solution.py:52
  190.4 4.4 %bitcast_subtract_fusion = f32[1024,512]{1,0:T(8,128)} fusion(f32[1024,512]{1,0:T(8,128)} %param.7, bf16[1024,2,384]{2,0,1:T(8,128)(2,1)} %bitcast.52, bf16[2,512,384]{2,1,0:T(8,128)(2,1)S(1)} %bitcast.49), kind=kOutput, calls=%fused_computation.1 | convolution fusion | flops 805830656 | bytes 6553600 | tf_op jit(solution)/shard_map/kimq,knq->imn/dot_general | solution.py:54
  (6 shorter events, 0.1 us)
Async XLA Ops:
  6.5 75.7 %all-gather.5.cloned.1.call-start = ((), (), s32[]{:S(2)}) async-start(), calls=%async_computation.2 | async-start | bytes 2506752 | tf_op jit(solution)/shard_map/all_gather | solution.py:37
  8.1 171.2 %all-gather.3.cloned.1.call-start = ((), (), s32[]{:S(2)}) async-start(), calls=%async_computation.1 | async-start | bytes 4866048 | tf_op jit(solution)/shard_map/all_gather | solution.py:32
  8.9 82.4 %copy-start.4 = (s32[2,32]{1,0:T(2,128)S(1)}, s32[2,32]{1,0:T(2,128)}, u32[]{:S(2)}) copy-start(s32[2,32]{1,0:T(2,128)} %param.12) | copy-start | bytes 772
  8.9 82.4 %copy-start.1 = (f32[2,32,384]{2,1,0:T(8,128)S(1)}, f32[2,32,384]{2,1,0:T(8,128)}, u32[]{:S(2)}) copy-start(f32[2,32,384]{2,1,0:T(8,128)} %param.11) | copy-start | bytes 294916
  8.9 82.4 %copy-start.2 = (f32[2,32,384]{2,1,0:T(8,128)S(1)}, f32[2,32,384]{2,1,0:T(8,128)}, u32[]{:S(2)}) copy-start(f32[2,32,384]{2,1,0:T(8,128)} %param.10) | copy-start | bytes 294916
  8.9 82.5 %copy-start.3 = (f32[2,2,2,512]{3,2,1,0:T(2,128)S(1)}, f32[2,2,2,512]{3,2,1,0:T(2,128)}, u32[]{:S(2)}) copy-start(f32[2,2,2,512]{3,2,1,0:T(2,128)} %param.13) | copy-start | bytes 49156
  82.2 83.0 %all-to-all-start = ((bf16[2,32,48,384]{3,2,0,1:T(8,128)(2,1)}), bf16[2,32,48,384]{3,2,0,1:T(8,128)(2,1)S(1)}, u32[]{:S(2)}, u32[]{:S(2)}) async-start(bf16[2,32,48,384]{3,2,0,1:T(8,128)(2,1)} %all-gather.5.cloned.1.call-done), calls=%async_computation | async-start | bytes 4718592 | tf_op jit(solution)/shard_map/all_to_all | solution.py:38
  182.4 2.0 %copy-start = (bf16[1,1024,384]{2,1,0:T(8,128)(2,1)S(1)}, bf16[1,1024,384]{2,1,0:T(8,128)(2,1)}, u32[]{:S(2)}) copy-start(bf16[1,1024,384]{2,1,0:T(8,128)(2,1)} %convert_element_type.57) | copy-start | bytes 2359300
Sparse Core Ops, SparseCore 0:
  10.4 71.8 all-gather.4
  84.3 95.0 all-gather.2

commit v2 on v1

v2 whole, which is shorter than its diff:
```python
import jax
import jax.numpy as jnp
from jax import lax
from jax.sharding import PartitionSpec as P


def column_weight(u_scale_k, v_scale_k, ranks_k):
    position = lax.broadcasted_iota(jnp.int32, u_scale_k.shape, 1)
    return jnp.where(position < ranks_k[:, None], u_scale_k * v_scale_k, jnp.float32(0.0))


def local(slab, u_codes, v_codes, u_scale, v_scale, ranks, d_inverse):
    panels, per_row, u_rows, rank_most = u_codes.shape
    v_rows = v_codes.shape[2]
    n_col = lax.axis_size("col")
    column = lax.axis_index("col")
    first_tile = lax.axis_index("row") * per_row
    tile_order = n_col * u_rows

    shard = jnp.concatenate([u_codes, v_codes], axis=2).transpose(1, 0, 2, 3)

    row_all = lax.all_gather(shard, "col", axis=0, tiled=False)
    row_u = row_all[:, :, :, :u_rows]
    row_v = row_all[:, :, :, u_rows:]

    every_tile = lax.all_gather(shard, "row", axis=0, tiled=True)
    col_all = lax.all_to_all(every_tile, "col", 0, 0, tiled=True)
    col_u = col_all[:, :, :u_rows].transpose(1, 0, 2, 3).reshape(panels, tile_order, rank_most)
    col_v = col_all[:, :, u_rows:]

    weight = jnp.stack(
        [column_weight(u_scale[k], v_scale[k], ranks[k]) for k in range(panels)]
    )
    row_weight = lax.dynamic_slice_in_dim(weight, first_tile, per_row, 1)
    col_weight = lax.dynamic_index_in_dim(weight, column, 1, keepdims=False)

    half = v_rows // 2
    d_blocks = d_inverse.reshape(panels, 2, 2, n_col, half).transpose(1, 2, 3, 0, 4)[..., None]
    pairs = col_v.reshape(n_col, panels, half, 2, rank_most)
    even = pairs[..., 0, :].astype(jnp.float32)
    odd = pairs[..., 1, :].astype(jnp.float32)
    first = d_blocks[0, 0] * even + d_blocks[0, 1] * odd
    second = d_blocks[1, 0] * even + d_blocks[1, 1] * odd
    col_scaled = jnp.stack([first, second], axis=-2).reshape(col_v.shape).astype(jnp.bfloat16)

    inner = jnp.einsum("cikbr,ckbq->kirq", row_v, col_scaled, preferred_element_type=jnp.float32)
    core = (row_weight[:, :, :, None] * inner * col_weight[:, None, None, :]).astype(jnp.bfloat16)
    left = jnp.einsum("cikmr,kirq->kicmq", row_u, core, preferred_element_type=jnp.float32)
    left = left.astype(jnp.bfloat16)
    update = jnp.einsum("kicmq,knq->icmn", left, col_u, preferred_element_type=jnp.float32)
    return slab - update.reshape(slab.shape)


def solution(mesh):
    in_specs = (
        P("row", "col"),
        P(None, "row", "col", None),
        P(None, "row", "col", None),
        P(),
        P(),
        P(),
        P(),
    )
    out_specs = P("row", "col")
    return jax.shard_map(local, mesh=mesh, in_specs=in_specs, out_specs=out_specs, check_vma=False)
```

time: 202 us -> 195 us (0.965)
  local copies, waits for them, and re-layouts: 17.8 us -> 2.73 us
  waiting for transfers between devices: 149 us -> 158 us
    all_gather x2, waiting for transfers between devices: 74.4 us -> 83.5 us  [the longest x1 73.3 us: local(): every_tile = lax.all_gather(shard, 'row', axis=0, tiled=True)]
    slice x8 -> x2, local copies, waits for them, and re-layouts: 5.85 us -> 0.46 us  [the longest x1 0.28 us: local(): col_v = col_all[:, :, u_rows:]]
    another operation x4 -> x1, local copies, waits for them, and re-layouts: 6.11 us -> 0.92 us  [local(): jnp.stack([first, second], axis=-2).reshape(col_v.shape)]
    all_gather x1 -> x0, local copies, waits for them, and re-layouts: 2.81 us -> none  [local(): row_all = lax.all_gather(shard, 'col', axis=2, tiled=True)]
    convert_element_type x2 -> x0, local copies, waits for them, and re-layouts: 2.37 us -> none  [apply_inverse(): jnp.stack([first, second], axis=-2).reshape(shape).astype(jnp.bfloat16)]
    dot_general x2 -> x3, matrix products: 10.4 us -> 8.85 us  [the longest x1 3.74 us: local(): jnp.einsum('cikbr,ckbq->kirq', row_v, col_scaled, preferred_element_type=...]
  transfers between devices with their start and end apart: 3 -> 3, of which waited for: 3 -> 3; matrix products, arithmetic and copies ran while one was open for 7% -> 2% of each run, Pallas kernels for 0% -> 0%
where the time goes in v2:
time: 195 us
  waiting for transfers between devices  158 us (81%)
  between operations  13.6 us (7%)
  starting transfers between devices  9.07 us (5%)
  matrix products  8.85 us (5%)
  other arithmetic  3.11 us (2%)
  local copies, waits for them, and re-layouts  2.73 us (1%)
    all_to_all x1, waiting for transfers between devices, local(): col_all = lax.all_to_all(every_tile, 'col', 0, 0, tiled=True)  73.6 us
    all_gather x1, waiting for transfers between devices, local(): every_tile = lax.all_gather(shard, 'row', axis=0, tiled=True)  73.3 us
    all_gather x1, waiting for transfers between devices, local(): row_all = lax.all_gather(shard, 'col', axis=0, tiled=False)  10.2 us
    all_to_all x1, starting transfers between devices, local(): col_all = lax.all_to_all(every_tile, 'col', 0, 0, tiled=True)  9.03 us
  transfers between devices with their start and end apart: 3, of which 3 were waited for; matrix products, arithmetic and copies ran while one was open for 2% of the time, Pallas kernels for 0%

profile of v2, /device:TPU:1, one launch (start us, length us, event | category | flops | bytes accessed | tf_op | source)
XLA Modules:
  0.0 195.2 jit_solution(14058793312024910637)
XLA Ops:
  6.5 0.0 all-gather.4.cloned.1.call-start
  6.5 1.6 copy_bitcast_fusion
  8.1 0.0 all-gather.4.cloned.1.call-update
  8.1 0.0 all-gather.6.cloned.1.call-start
  8.2 0.7 all-gather.6.cloned.1.call-update
  8.9 0.0 copy-start.4
  8.9 0.0 copy-start.1
  8.9 0.0 copy-start.2
  8.9 0.0 copy-start.3
  8.9 73.3 %all-gather.4.cloned.1.call-done = bf16[32,2,48,384]{3,2,1,0:T(8,128)(2,1)} async-done(((bf16[2,2,48,384]{3,2,1,0:T(8,128)(2,1)}), bf16[32,2,48,384]{3,2,1,0:T(8,128)(2,1)}) %all-gather.4.cloned.1.call-update) | async-done | bytes 2359312 | tf_op jit(solution)/shard_map/all_gather | solution.py:26
  82.2 9.0 %all-to-all-start = ((bf16[32,2,48,384]{3,2,1,0:T(8,128)(2,1)}), bf16[32,2,48,384]{3,2,1,0:T(8,128)(2,1)S(1)}, u32[]{:S(2)}, u32[]{:S(2)}) async-start(bf16[32,2,48,384]{3,2,1,0:T(8,128)(2,1)} %all-gather.4.cloned.1.call-done), calls=%async_computation | async-start | bytes 4718592 | tf_op jit(solution)/shard_map/all_to_all | solution.py:27
  91.3 0.0 copy-done.4
  91.3 0.0 copy-done.1
  91.3 0.0 copy-done.2
  91.3 0.1 multiply_select_fusion
  91.4 0.0 copy-done.3
  91.4 0.1 reshape.84
  91.7 73.6 %all-to-all-done = bf16[32,2,48,384]{3,2,1,0:T(8,128)(2,1)S(1)} async-done(((bf16[32,2,48,384]{3,2,1,0:T(8,128)(2,1)}), bf16[32,2,48,384]{3,2,1,0:T(8,128)(2,1)S(1)}, u32[]{:S(2)}, u32[]{:S(2)}) %all-to-all-start) | async-done | bytes 2359328 | tf_op jit(solution)/shard_map/all_to_all | solution.py:27
  165.3 0.3 slice.73
  165.6 0.9 copy.74
  166.5 0.1 slice_bitcast_fusion
  166.6 0.1 copy.63
  166.7 0.2 fusion.16
  166.9 1.3 fusion.5
  168.2 0.2 pad_maximum_fusion
  168.3 0.9 copy.61
  169.3 10.2 %all-gather.6.cloned.1.call-done = bf16[64,2,48,384]{3,2,1,0:T(8,128)(2,1)} async-done(((bf16[2,2,48,384]{3,2,1,0:T(8,128)(2,1)}), bf16[64,2,48,384]{3,2,1,0:T(8,128)(2,1)}) %all-gather.6.cloned.1.call-update) | async-done | bytes 4718608 | tf_op jit(solution)/shard_map/all_gather | solution.py:22
  179.4 3.7 %fusion = f32[2,2,384,384,1]{3,2,0,1,4:T(8,128)S(1)} fusion(bf16[32,2,2,48,384]{4,3,2,1,0:T(8,128)(2,1)} %bitcast.55, bf16[32,2,32,384,1]{3,0,2,1,4:T(8,128)(2,1)S(1)} %bitcast.51), kind=kOutput, calls=%fused_computation | convolution fusion | flops 1207959552 | bytes 7077888 | tf_op jit(solution)/shard_map/cikbr,ckbq->kirq/dot_general | solution.py:46
  183.2 0.0 copy-start
  183.2 2.8 %convolution_convert_fusion = bf16[2,2,32,16,384]{4,3,2,1,0:T(8,128)(2,1)S(1)} fusion(f32[2,2,384,384,1]{3,2,0,1,4:T(8,128)S(1)} %fusion, f32[2,384]{1,0:T(2,128)S(1)} %bitcast.54, f32[2,2,384]{2,1,0:T(2,128)S(1)} %fusion.14, bf16[32,2,2,48,384]{4,3,2,1,0:T(8,128)(2,1)} %bitcast.56), kind=kOutput, calls=%fused_computation.10 | convolution fusion | flops 606535680 | bytes 5514240 | tf_op jit(solution)/shard_map/cikmr,kirq->kicmq/dot_general | solution.py:48
  186.0 0.0 copy-done
  186.0 2.3 %bitcast_subtract_fusion = f32[1024,512]{1,0:T(8,128)} fusion(f32[1024,512]{1,0:T(8,128)S(1)} %copy-done, bf16[1024,2,384]{2,0,1:T(8,128)(2,1)S(1)} %bitcast.52, bf16[2,512,384]{2,1,0:T(8,128)(2,1)S(1)} %bitcast.50), kind=kOutput, calls=%fused_computation.5 | convolution fusion | flops 805830656 | bytes 6553600 | tf_op jit(solution)/shard_map/kicmq,knq->icmn/dot_general | solution.py:50
  (9 shorter events, 0.2 us)
Async XLA Ops:
  6.5 75.7 %all-gather.4.cloned.1.call-start = ((), (), s32[]{:S(2)}) async-start(), calls=%async_computation.1 | async-start | bytes 2506752 | tf_op jit(solution)/shard_map/all_gather | solution.py:26
  8.1 171.3 %all-gather.6.cloned.1.call-start = ((), (), s32[]{:S(2)}) async-start(), calls=%async_computation.2 | async-start | bytes 4866048 | tf_op jit(solution)/shard_map/all_gather | solution.py:22
  8.9 82.4 %copy-start.4 = (s32[2,32]{1,0:T(2,128)S(1)}, s32[2,32]{1,0:T(2,128)}, u32[]{:S(2)}) copy-start(s32[2,32]{1,0:T(2,128)} %param.12) | copy-start | bytes 772
  8.9 82.4 %copy-start.1 = (f32[2,32,384]{2,1,0:T(8,128)S(1)}, f32[2,32,384]{2,1,0:T(8,128)}, u32[]{:S(2)}) copy-start(f32[2,32,384]{2,1,0:T(8,128)} %param.11) | copy-start | bytes 294916
  8.9 82.4 %copy-start.2 = (f32[2,32,384]{2,1,0:T(8,128)S(1)}, f32[2,32,384]{2,1,0:T(8,128)}, u32[]{:S(2)}) copy-start(f32[2,32,384]{2,1,0:T(8,128)} %param.10) | copy-start | bytes 294916
  8.9 82.5 %copy-start.3 = (f32[2,2,2,512]{3,2,1,0:T(2,128)S(1)}, f32[2,2,2,512]{3,2,1,0:T(2,128)}, u32[]{:S(2)}) copy-start(f32[2,2,2,512]{3,2,1,0:T(2,128)} %param.13) | copy-start | bytes 49156
  82.2 83.1 %all-to-all-start = ((bf16[32,2,48,384]{3,2,1,0:T(8,128)(2,1)}), bf16[32,2,48,384]{3,2,1,0:T(8,128)(2,1)S(1)}, u32[]{:S(2)}, u32[]{:S(2)}) async-start(bf16[32,2,48,384]{3,2,1,0:T(8,128)(2,1)} %all-gather.4.cloned.1.call-done), calls=%async_computation | async-start | bytes 4718592 | tf_op jit(solution)/shard_map/all_to_all | solution.py:27
  183.2 2.8 %copy-start = (f32[1024,512]{1,0:T(8,128)S(1)}, f32[1024,512]{1,0:T(8,128)}, u32[]{:S(2)}) copy-start(f32[1024,512]{1,0:T(8,128)} %param.7) | copy-start | bytes 6291460
Sparse Core Ops, SparseCore 0:
  10.4 71.8 all-gather.3
  84.4 95.0 all-gather.5

commit v3 on v2

--- a/solution.py
+++ b/solution.py
@@ -23,7 +23,10 @@
     row_u = row_all[:, :, :, :u_rows]
     row_v = row_all[:, :, :, u_rows:]
 
-    every_tile = lax.all_gather(shard, "row", axis=0, tiled=True)
+    n_row = lax.axis_size("row")
+    spread = jnp.broadcast_to(shard[None], (n_row,) + shard.shape)
+    every_tile = lax.all_to_all(spread, "row", 0, 0, tiled=True)
+    every_tile = every_tile.reshape((n_row * per_row,) + shard.shape[1:])
     col_all = lax.all_to_all(every_tile, "col", 0, 0, tiled=True)
     col_u = col_all[:, :, :u_rows].transpose(1, 0, 2, 3).reshape(panels, tile_order, rank_most)
     col_v = col_all[:, :, u_rows:]

time: 195 us -> 181 us (0.928)
  waiting for transfers between devices: 158 us -> 124 us
  starting transfers between devices: 9.07 us -> 24 us
  local copies, waits for them, and re-layouts: 2.73 us -> 8.54 us
    all_gather x1 -> x0, waiting for transfers between devices: 73.3 us -> none  [local(): every_tile = lax.all_gather(shard, 'row', axis=0, tiled=True)]
    all_to_all x0 -> x1, waiting for transfers between devices: none -> 66 us  [local(): every_tile = lax.all_to_all(spread, 'row', 0, 0, tiled=True)]
    all_to_all x1, waiting for transfers between devices: 73.6 us -> 57.7 us  [local(): col_all = lax.all_to_all(every_tile, 'col', 0, 0, tiled=True)]
    all_to_all x0 -> x1, starting transfers between devices: none -> 13.4 us  [local(): every_tile = lax.all_to_all(spread, 'row', 0, 0, tiled=True)]
    all_gather x1, waiting for transfers between devices: 10.2 us -> 0.02 us  [local(): row_all = lax.all_gather(shard, 'col', axis=0, tiled=False)]
  transfers between devices with their start and end apart: 3 -> 3, of which waited for: 3 -> 2; matrix products, arithmetic and copies ran while one was open for 2% -> 4% of each run, Pallas kernels for 0% -> 0%
where the time goes in v3:
time: 181 us; the launch traced here: 180 us
  waiting for transfers between devices  124 us (69%)
  starting transfers between devices  24 us (13%)
  between operations  13.6 us (8%)
  matrix products  8.86 us (5%)
  local copies, waits for them, and re-layouts  8.54 us (5%)
    all_to_all x1, waiting for transfers between devices, local(): every_tile = lax.all_to_all(spread, 'row', 0, 0, tiled=True)  66 us
    all_to_all x1, waiting for transfers between devices, local(): col_all = lax.all_to_all(every_tile, 'col', 0, 0, tiled=True)  57.7 us
    all_to_all x1, starting transfers between devices, local(): every_tile = lax.all_to_all(spread, 'row', 0, 0, tiled=True)  13.4 us
    all_to_all x1, starting transfers between devices, local(): col_all = lax.all_to_all(every_tile, 'col', 0, 0, tiled=True)  10.5 us
    dot_general x1, matrix products, local(): jnp.einsum('cikbr,ckbq->kirq', row_v, col_scaled, preferred_element_type=...  3.74 us
  transfers between devices with their start and end apart: 3, of which 2 were waited for; matrix products, arithmetic and copies ran while one was open for 4% of the time, Pallas kernels for 0%

profile of v3, /device:TPU:1, one launch (start us, length us, event | category | flops | bytes accessed | tf_op | source)
XLA Modules:
  0.0 180.3 jit_solution(9627998132617958044)
XLA Ops:
  6.5 0.8 constant_dynamic-update-slice_fusion.1
  7.3 0.9 constant_dynamic-update-slice_fusion
  8.2 1.7 broadcast_in_dim.18
  10.0 13.4 %all-to-all-start = ((bf16[16,2,2,48,384]{4,3,1,2,0:T(8,128)(2,1)}), bf16[16,2,2,48,384]{4,3,1,2,0:T(8,128)(2,1)S(1)}, u32[]{:S(2)}, u32[]{:S(2)}) async-start(bf16[16,2,2,48,384]{4,3,1,2,0:T(8,128)(2,1)} %broadcast_in_dim.18), calls=%async_computation | async-start | bytes 4718592 | tf_op jit(solution)/shard_map/all_to_all | solution.py:28
  23.4 0.0 all-gather.3.cloned.1.call-start
  23.5 0.7 copy.90
  24.1 0.0 all-gather.3.cloned.1.call-update
  24.2 66.0 %all-to-all-done = bf16[16,2,2,48,384]{4,3,1,2,0:T(8,128)(2,1)S(1)} async-done(((bf16[16,2,2,48,384]{4,3,1,2,0:T(8,128)(2,1)}), bf16[16,2,2,48,384]{4,3,1,2,0:T(8,128)(2,1)S(1)}, u32[]{:S(2)}, u32[]{:S(2)}) %all-to-all-start) | async-done | bytes 2359328 | tf_op jit(solution)/shard_map/all_to_all | solution.py:28
  90.2 1.7 copy.52
  91.9 0.0 copy-start.4
  91.9 0.0 copy-start.1
  91.9 0.0 copy-start.2
  91.9 0.0 copy-start.3
  91.9 10.5 %all-to-all-start.1 = ((bf16[32,2,48,384]{3,2,1,0:T(8,128)(2,1)}), bf16[32,2,48,384]{3,2,1,0:T(8,128)(2,1)S(1)}, u32[]{:S(2)}, u32[]{:S(2)}) async-start(bf16[32,2,48,384]{3,2,1,0:T(8,128)(2,1)} %bitcast.52), calls=%async_computation.1 | async-start | bytes 4718592 | tf_op jit(solution)/shard_map/all_to_all | solution.py:30
  102.4 0.0 copy-done.4
  102.4 0.0 copy-done.1
  102.5 0.0 copy-done.2
  102.5 0.1 multiply_select_fusion
  102.6 0.0 copy-done.3
  102.6 0.1 reshape.88
  102.9 57.7 %all-to-all-done.1 = bf16[32,2,48,384]{3,2,1,0:T(8,128)(2,1)S(1)} async-done(((bf16[32,2,48,384]{3,2,1,0:T(8,128)(2,1)}), bf16[32,2,48,384]{3,2,1,0:T(8,128)(2,1)S(1)}, u32[]{:S(2)}, u32[]{:S(2)}) %all-to-all-start.1) | async-done | bytes 2359328 | tf_op jit(solution)/shard_map/all_to_all | solution.py:30
  160.6 0.3 slice.73
  160.9 0.9 copy.73
  161.8 0.1 slice_bitcast_fusion
  161.9 0.1 copy.61
  162.0 0.2 fusion.16
  162.2 1.3 fusion.5
  163.4 0.2 pad_maximum_fusion
  163.6 0.9 copy.59
  164.5 0.0 all-gather.3.cloned.1.call-done
  164.6 3.7 %fusion = f32[2,2,384,384,1]{3,2,0,1,4:T(8,128)S(1)} fusion(bf16[32,2,2,48,384]{4,3,2,1,0:T(8,128)(2,1)} %bitcast.61, bf16[32,2,32,384,1]{3,0,2,1,4:T(8,128)(2,1)S(1)} %bitcast.55), kind=kOutput, calls=%fused_computation | convolution fusion | flops 1207959552 | bytes 7077888 | tf_op jit(solution)/shard_map/cikbr,ckbq->kirq/dot_general | solution.py:49
  168.3 0.0 copy-start
  168.3 2.8 %convolution_convert_fusion = bf16[2,2,32,16,384]{4,3,2,1,0:T(8,128)(2,1)S(1)} fusion(f32[2,2,384,384,1]{3,2,0,1,4:T(8,128)S(1)} %fusion, f32[2,384]{1,0:T(2,128)S(1)} %bitcast.60, f32[2,2,384]{2,1,0:T(2,128)S(1)} %fusion.14, bf16[32,2,2,48,384]{4,3,2,1,0:T(8,128)(2,1)} %bitcast.62), kind=kOutput, calls=%fused_computation.10 | convolution fusion | flops 606535680 | bytes 5514240 | tf_op jit(solution)/shard_map/cikmr,kirq->kicmq/dot_general | solution.py:51
  171.1 0.0 copy-done
  171.1 2.3 %bitcast_subtract_fusion = f32[1024,512]{1,0:T(8,128)} fusion(f32[1024,512]{1,0:T(8,128)S(1)} %copy-done, bf16[1024,2,384]{2,0,1:T(8,128)(2,1)S(1)} %bitcast.56, bf16[2,512,384]{2,1,0:T(8,128)(2,1)S(1)} %bitcast.54), kind=kOutput, calls=%fused_computation.5 | convolution fusion | flops 805830656 | bytes 6553600 | tf_op jit(solution)/shard_map/kicmq,knq->icmn/dot_general | solution.py:53
  (9 shorter events, 0.2 us)
Async XLA Ops:
  10.0 80.2 %all-to-all-start = ((bf16[16,2,2,48,384]{4,3,1,2,0:T(8,128)(2,1)}), bf16[16,2,2,48,384]{4,3,1,2,0:T(8,128)(2,1)S(1)}, u32[]{:S(2)}, u32[]{:S(2)}) async-start(bf16[16,2,2,48,384]{4,3,1,2,0:T(8,128)(2,1)} %broadcast_in_dim.18), calls=%async_computation | async-start | bytes 4718592 | tf_op jit(solution)/shard_map/all_to_all | solution.py:28
  23.4 141.1 %all-gather.3.cloned.1.call-start = ((), (), s32[]{:S(2)}) async-start(), calls=%async_computation.2 | async-start | bytes 4866048 | tf_op jit(solution)/shard_map/all_gather | solution.py:22
  91.9 10.5 %copy-start.4 = (s32[2,32]{1,0:T(2,128)S(1)}, s32[2,32]{1,0:T(2,128)}, u32[]{:S(2)}) copy-start(s32[2,32]{1,0:T(2,128)} %param.12) | copy-start | bytes 772
  91.9 10.6 %copy-start.1 = (f32[2,32,384]{2,1,0:T(8,128)S(1)}, f32[2,32,384]{2,1,0:T(8,128)}, u32[]{:S(2)}) copy-start(f32[2,32,384]{2,1,0:T(8,128)} %param.11) | copy-start | bytes 294916
  91.9 10.6 %copy-start.2 = (f32[2,32,384]{2,1,0:T(8,128)S(1)}, f32[2,32,384]{2,1,0:T(8,128)}, u32[]{:S(2)}) copy-start(f32[2,32,384]{2,1,0:T(8,128)} %param.10) | copy-start | bytes 294916
  91.9 10.7 %copy-start.3 = (f32[2,2,2,512]{3,2,1,0:T(2,128)S(1)}, f32[2,2,2,512]{3,2,1,0:T(2,128)}, u32[]{:S(2)}) copy-start(f32[2,2,2,512]{3,2,1,0:T(2,128)} %param.13) | copy-start | bytes 49156
  91.9 68.7 %all-to-all-start.1 = ((bf16[32,2,48,384]{3,2,1,0:T(8,128)(2,1)}), bf16[32,2,48,384]{3,2,1,0:T(8,128)(2,1)S(1)}, u32[]{:S(2)}, u32[]{:S(2)}) async-start(bf16[32,2,48,384]{3,2,1,0:T(8,128)(2,1)} %bitcast.52), calls=%async_computation.1 | async-start | bytes 4718592 | tf_op jit(solution)/shard_map/all_to_all | solution.py:30
  168.3 2.8 %copy-start = (f32[1024,512]{1,0:T(8,128)S(1)}, f32[1024,512]{1,0:T(8,128)}, u32[]{:S(2)}) copy-start(f32[1024,512]{1,0:T(8,128)} %param.7) | copy-start | bytes 6291460
Sparse Core Ops, SparseCore 0:
  26.4 93.7 all-gather.2

commit v4 on v2

--- a/solution.py
+++ b/solution.py
@@ -1,7 +1,7 @@
 import jax
 import jax.numpy as jnp
 from jax import lax
-from jax.sharding import PartitionSpec as P
+from jax.sharding import Mesh, PartitionSpec as P
 
 
 def column_weight(u_scale_k, v_scale_k, ranks_k):
@@ -14,7 +14,7 @@
     v_rows = v_codes.shape[2]
     n_col = lax.axis_size("col")
     column = lax.axis_index("col")
-    first_tile = lax.axis_index("row") * per_row
+    first_tile = (lax.axis_index("zh") * lax.axis_size("x") + lax.axis_index("x")) * per_row
     tile_order = n_col * u_rows
 
     shard = jnp.concatenate([u_codes, v_codes], axis=2).transpose(1, 0, 2, 3)
@@ -23,7 +23,13 @@
     row_u = row_all[:, :, :, :u_rows]
     row_v = row_all[:, :, :, u_rows:]
 
-    every_tile = lax.all_gather(shard, "row", axis=0, tiled=True)
+    n_x = lax.axis_size("x")
+    n_z = lax.axis_size("zh")
+    spread = jnp.broadcast_to(shard[None], (n_x,) + shard.shape)
+    by_x = lax.all_to_all(spread, "x", 0, 0, tiled=True)
+    spread = jnp.broadcast_to(by_x[None], (n_z,) + by_x.shape)
+    every_tile = lax.all_to_all(spread, "zh", 0, 0, tiled=True)
+    every_tile = every_tile.reshape((n_z * n_x * per_row,) + shard.shape[1:])
     col_all = lax.all_to_all(every_tile, "col", 0, 0, tiled=True)
     col_u = col_all[:, :, :u_rows].transpose(1, 0, 2, 3).reshape(panels, tile_order, rank_most)
     col_v = col_all[:, :, u_rows:]
@@ -52,14 +58,18 @@
 
 
 def solution(mesh):
+    n_row, n_col = mesh.devices.shape
+    n_x = 4 if n_row % 4 == 0 else 1
+    split = Mesh(mesh.devices.reshape(n_row // n_x, n_x, n_col), ("zh", "x", "col"))
+    rows = ("zh", "x")
     in_specs = (
-        P("row", "col"),
-        P(None, "row", "col", None),
-        P(None, "row", "col", None),
+        P(rows, "col"),
+        P(None, rows, "col", None),
+        P(None, rows, "col", None),
         P(),
         P(),
         P(),
         P(),
     )
-    out_specs = P("row", "col")
-    return jax.shard_map(local, mesh=mesh, in_specs=in_specs, out_specs=out_specs, check_vma=False)
+    out_specs = P(rows, "col")
+    return jax.shard_map(local, mesh=split, in_specs=in_specs, out_specs=out_specs, check_vma=False)

time: 195 us -> 190 us (0.974)
  waiting for transfers between devices: 158 us -> 114 us
  starting transfers between devices: 9.07 us -> 31.2 us
  blocking collectives: 0 us -> 11.9 us
  local copies, waits for them, and re-layouts: 2.73 us -> 8.72 us
    all_gather x1 -> x0, waiting for transfers between devices: 73.3 us -> none  [local(): every_tile = lax.all_gather(shard, 'row', axis=0, tiled=True)]
    all_to_all x0 -> x1, waiting for transfers between devices: none -> 55.3 us  [local(): every_tile = lax.all_to_all(spread, 'zh', 0, 0, tiled=True)]
    all_to_all x1, waiting for transfers between devices: 73.6 us -> 58.4 us  [local(): col_all = lax.all_to_all(every_tile, 'col', 0, 0, tiled=True)]
    all_to_all x0 -> x1, blocking collectives: none -> 11.9 us  [local(): by_x = lax.all_to_all(spread, 'x', 0, 0, tiled=True)]
    all_to_all x0 -> x1, starting transfers between devices: none -> 11.7 us  [local(): every_tile = lax.all_to_all(spread, 'zh', 0, 0, tiled=True)]
    all_to_all x1, starting transfers between devices: 9.03 us -> 19.5 us  [local(): col_all = lax.all_to_all(every_tile, 'col', 0, 0, tiled=True)]
    all_gather x1, waiting for transfers between devices: 10.2 us -> 0.02 us  [local(): row_all = lax.all_gather(shard, 'col', axis=0, tiled=False)]
  transfers between devices with their start and end apart: 3 -> 3, of which waited for: 3 -> 2; matrix products, arithmetic and copies ran while one was open for 2% -> 4% of each run, Pallas kernels for 0% -> 0%
where the time goes in v4:
time: 190 us
  waiting for transfers between devices  114 us (60%)
  starting transfers between devices  31.2 us (16%)
  between operations  13.6 us (7%)
  blocking collectives  11.9 us (6%)
  matrix products  8.86 us (5%)
  local copies, waits for them, and re-layouts  8.72 us (5%)
    all_to_all x1, waiting for transfers between devices, local(): col_all = lax.all_to_all(every_tile, 'col', 0, 0, tiled=True)  58.4 us
    all_to_all x1, waiting for transfers between devices, local(): every_tile = lax.all_to_all(spread, 'zh', 0, 0, tiled=True)  55.3 us
    all_to_all x1, starting transfers between devices, local(): col_all = lax.all_to_all(every_tile, 'col', 0, 0, tiled=True)  19.5 us
    all_to_all x1, blocking collectives, local(): by_x = lax.all_to_all(spread, 'x', 0, 0, tiled=True)  11.9 us
    all_to_all x1, starting transfers between devices, local(): every_tile = lax.all_to_all(spread, 'zh', 0, 0, tiled=True)  11.7 us
  transfers between devices with their start and end apart: 3, of which 2 were waited for; matrix products, arithmetic and copies ran while one was open for 4% of the time, Pallas kernels for 0%

profile of v4, /device:TPU:1, one launch (start us, length us, event | category | flops | bytes accessed | tf_op | source)
XLA Modules:
  0.0 189.7 jit_solution(16438677925863964414)
XLA Ops:
  6.5 0.8 constant_dynamic-update-slice_fusion.1
  7.3 0.9 constant_dynamic-update-slice_fusion
  8.2 0.1 broadcast_in_dim.24
  8.3 11.9 %all_to_all.15 = bf16[4,2,2,48,384]{4,3,1,2,0:T(8,128)(2,1)S(1)} all-to-all(bf16[4,2,2,48,384]{4,3,1,2,0:T(8,128)(2,1)S(1)} %broadcast_in_dim.24), channel_id=1, replica_groups=mesh['zh'=4,'x'=4,'col'=32] {'x'}, dimensions={0} | all-to-all | bytes 1179648 | tf_op jit(solution)/shard_map/all_to_all | solution.py:29
  20.2 0.1 copy.55
  20.3 1.7 broadcast_in_dim.25
  22.0 11.7 %all-to-all-start.1 = ((bf16[4,4,2,2,48,384]{5,4,2,1,3,0:T(8,128)(2,1)}), bf16[4,4,2,2,48,384]{5,4,2,1,3,0:T(8,128)(2,1)S(1)}, u32[]{:S(2)}, u32[]{:S(2)}) async-start(bf16[4,4,2,2,48,384]{5,4,2,1,3,0:T(8,128)(2,1)} %broadcast_in_dim.25), calls=%async_computation.1 | async-start | bytes 4718592 | tf_op jit(solution)/shard_map/all_to_all | solution.py:31
  33.7 0.0 all-gather.3.cloned.1.call-start
  33.7 0.7 copy.94
  34.4 0.0 all-gather.3.cloned.1.call-update
  34.4 55.3 %all-to-all-done.1 = bf16[4,4,2,2,48,384]{5,4,2,1,3,0:T(8,128)(2,1)S(1)} async-done(((bf16[4,4,2,2,48,384]{5,4,2,1,3,0:T(8,128)(2,1)}), bf16[4,4,2,2,48,384]{5,4,2,1,3,0:T(8,128)(2,1)S(1)}, u32[]{:S(2)}, u32[]{:S(2)}) %all-to-all-start.1) | async-done | bytes 2359328 | tf_op jit(solution)/shard_map/all_to_all | solution.py:31
  89.7 1.8 copy.56
  91.6 0.0 copy-start.4
  91.6 0.0 copy-start.1
  91.6 0.0 copy-start.2
  91.6 0.0 copy-start.3
  91.6 19.5 %all-to-all-start.2 = ((bf16[32,2,48,384]{3,2,1,0:T(8,128)(2,1)}), bf16[32,2,48,384]{3,2,1,0:T(8,128)(2,1)S(1)}, u32[]{:S(2)}, u32[]{:S(2)}) async-start(bf16[32,2,48,384]{3,2,1,0:T(8,128)(2,1)} %bitcast.52), calls=%async_computation.2 | async-start | bytes 4718592 | tf_op jit(solution)/shard_map/all_to_all | solution.py:33
  111.1 0.0 copy-done.4
  111.1 0.0 copy-done.1
  111.1 0.0 copy-done.2
  111.2 0.1 multiply_select_fusion
  111.3 0.0 copy-done.3
  111.3 0.1 reshape.89
  111.6 58.4 %all-to-all-done.2 = bf16[32,2,48,384]{3,2,1,0:T(8,128)(2,1)S(1)} async-done(((bf16[32,2,48,384]{3,2,1,0:T(8,128)(2,1)}), bf16[32,2,48,384]{3,2,1,0:T(8,128)(2,1)S(1)}, u32[]{:S(2)}, u32[]{:S(2)}) %all-to-all-start.2) | async-done | bytes 2359328 | tf_op jit(solution)/shard_map/all_to_all | solution.py:33
  170.0 0.3 slice.73
  170.2 0.9 copy.77
  171.2 0.1 slice_bitcast_fusion
  171.3 0.1 copy.65
  171.3 0.2 fusion.16
  171.5 1.3 fusion.5
  172.8 0.2 pad_maximum_fusion
  173.0 0.9 copy.63
  173.9 0.0 all-gather.3.cloned.1.call-done
  173.9 3.7 %fusion = f32[2,2,384,384,1]{3,2,0,1,4:T(8,128)S(1)} fusion(bf16[32,2,2,48,384]{4,3,2,1,0:T(8,128)(2,1)} %bitcast.61, bf16[32,2,32,384,1]{3,0,2,1,4:T(8,128)(2,1)S(1)} %bitcast.55), kind=kOutput, calls=%fused_computation | convolution fusion | flops 1207959552 | bytes 7077888 | tf_op jit(solution)/shard_map/cikbr,ckbq->kirq/dot_general | solution.py:52
  177.7 0.0 copy-start
  177.7 2.8 %convolution_convert_fusion = bf16[2,2,32,16,384]{4,3,2,1,0:T(8,128)(2,1)S(1)} fusion(f32[2,2,384,384,1]{3,2,0,1,4:T(8,128)S(1)} %fusion, f32[2,384]{1,0:T(2,128)S(1)} %bitcast.60, f32[2,2,384]{2,1,0:T(2,128)S(1)} %fusion.14, bf16[32,2,2,48,384]{4,3,2,1,0:T(8,128)(2,1)} %bitcast.62), kind=kOutput, calls=%fused_computation.10 | convolution fusion | flops 606535680 | bytes 5514240 | tf_op jit(solution)/shard_map/cikmr,kirq->kicmq/dot_general | solution.py:54
  180.5 0.0 copy-done
  180.5 2.3 %bitcast_subtract_fusion = f32[1024,512]{1,0:T(8,128)} fusion(f32[1024,512]{1,0:T(8,128)S(1)} %copy-done, bf16[1024,2,384]{2,0,1:T(8,128)(2,1)S(1)} %bitcast.56, bf16[2,512,384]{2,1,0:T(8,128)(2,1)S(1)} %bitcast.54), kind=kOutput, calls=%fused_computation.5 | convolution fusion | flops 805830656 | bytes 6553600 | tf_op jit(solution)/shard_map/kicmq,knq->icmn/dot_general | solution.py:56
  (9 shorter events, 0.2 us)
Async XLA Ops:
  22.0 67.7 %all-to-all-start.1 = ((bf16[4,4,2,2,48,384]{5,4,2,1,3,0:T(8,128)(2,1)}), bf16[4,4,2,2,48,384]{5,4,2,1,3,0:T(8,128)(2,1)S(1)}, u32[]{:S(2)}, u32[]{:S(2)}) async-start(bf16[4,4,2,2,48,384]{5,4,2,1,3,0:T(8,128)(2,1)} %broadcast_in_dim.25), calls=%async_computation.1 | async-start | bytes 4718592 | tf_op jit(solution)/shard_map/all_to_all | solution.py:31
  33.7 140.2 %all-gather.3.cloned.1.call-start = ((), (), s32[]{:S(2)}) async-start(), calls=%async_computation.3 | async-start | bytes 4866048 | tf_op jit(solution)/shard_map/all_gather | solution.py:22
  91.6 19.6 %copy-start.4 = (s32[2,32]{1,0:T(2,128)S(1)}, s32[2,32]{1,0:T(2,128)}, u32[]{:S(2)}) copy-start(s32[2,32]{1,0:T(2,128)} %param.12) | copy-start | bytes 772
  91.6 19.6 %copy-start.1 = (f32[2,32,384]{2,1,0:T(8,128)S(1)}, f32[2,32,384]{2,1,0:T(8,128)}, u32[]{:S(2)}) copy-start(f32[2,32,384]{2,1,0:T(8,128)} %param.11) | copy-start | bytes 294916
  91.6 19.6 %copy-start.2 = (f32[2,32,384]{2,1,0:T(8,128)S(1)}, f32[2,32,384]{2,1,0:T(8,128)}, u32[]{:S(2)}) copy-start(f32[2,32,384]{2,1,0:T(8,128)} %param.10) | copy-start | bytes 294916
  91.6 19.7 %copy-start.3 = (f32[2,2,2,512]{3,2,1,0:T(2,128)S(1)}, f32[2,2,2,512]{3,2,1,0:T(2,128)}, u32[]{:S(2)}) copy-start(f32[2,2,2,512]{3,2,1,0:T(2,128)} %param.13) | copy-start | bytes 49156
  91.6 78.4 %all-to-all-start.2 = ((bf16[32,2,48,384]{3,2,1,0:T(8,128)(2,1)}), bf16[32,2,48,384]{3,2,1,0:T(8,128)(2,1)S(1)}, u32[]{:S(2)}, u32[]{:S(2)}) async-start(bf16[32,2,48,384]{3,2,1,0:T(8,128)(2,1)} %bitcast.52), calls=%async_computation.2 | async-start | bytes 4718592 | tf_op jit(solution)/shard_map/all_to_all | solution.py:33
  177.7 2.8 %copy-start = (f32[1024,512]{1,0:T(8,128)S(1)}, f32[1024,512]{1,0:T(8,128)}, u32[]{:S(2)}) copy-start(f32[1024,512]{1,0:T(8,128)} %param.7) | copy-start | bytes 6291460
Sparse Core Ops, SparseCore 0:
  36.7 94.6 all-gather.2

commit v5 on v3

--- a/solution.py
+++ b/solution.py
@@ -16,6 +16,7 @@
     column = lax.axis_index("col")
     first_tile = lax.axis_index("row") * per_row
     tile_order = n_col * u_rows
+    both = u_rows + v_rows
 
     shard = jnp.concatenate([u_codes, v_codes], axis=2).transpose(1, 0, 2, 3)
 
@@ -24,10 +25,12 @@
     row_v = row_all[:, :, :, u_rows:]
 
     n_row = lax.axis_size("row")
-    spread = jnp.broadcast_to(shard[None], (n_row,) + shard.shape)
+    flat = shard.reshape(per_row * panels * both, rank_most)
+    spread = jnp.broadcast_to(flat[None], (n_row,) + flat.shape)
     every_tile = lax.all_to_all(spread, "row", 0, 0, tiled=True)
-    every_tile = every_tile.reshape((n_row * per_row,) + shard.shape[1:])
+    every_tile = every_tile.reshape(n_row * per_row, panels * both, rank_most)
     col_all = lax.all_to_all(every_tile, "col", 0, 0, tiled=True)
+    col_all = col_all.reshape(n_col, panels, both, rank_most)
     col_u = col_all[:, :, :u_rows].transpose(1, 0, 2, 3).reshape(panels, tile_order, rank_most)
     col_v = col_all[:, :, u_rows:]
 

time: 181 us -> 179 us (0.989)
  local copies, waits for them, and re-layouts: 8.54 us -> 4.5 us
  transfers between devices with their start and end apart: 3 -> 3, of which waited for: 2 -> 2; matrix products, arithmetic and copies ran while one was open for 4% -> 2% of each run, Pallas kernels for 0% -> 0%
where the time goes in v5:
time: 179 us
  waiting for transfers between devices  125 us (70%)
  starting transfers between devices  24 us (13%)
  between operations  13.6 us (8%)
  matrix products  8.87 us (5%)
  local copies, waits for them, and re-layouts  4.5 us (3%)
  other arithmetic  3.12 us (2%)
    all_to_all x1, waiting for transfers between devices, local(): every_tile = lax.all_to_all(spread, 'row', 0, 0, tiled=True)  66.1 us
    all_to_all x1, waiting for transfers between devices, local(): col_all = lax.all_to_all(every_tile, 'col', 0, 0, tiled=True)  57.8 us
    all_to_all x1, starting transfers between devices, local(): every_tile = lax.all_to_all(spread, 'row', 0, 0, tiled=True)  13.5 us
    all_to_all x1, starting transfers between devices, local(): col_all = lax.all_to_all(every_tile, 'col', 0, 0, tiled=True)  10.5 us
    dot_general x1, matrix products, local(): jnp.einsum('cikbr,ckbq->kirq', row_v, col_scaled, preferred_element_type=...  3.75 us
  transfers between devices with their start and end apart: 3, of which 2 were waited for; matrix products, arithmetic and copies ran while one was open for 2% of the time, Pallas kernels for 0%

profile of v5, /device:TPU:1, one launch (start us, length us, event | category | flops | bytes accessed | tf_op | source)
XLA Modules:
  0.0 178.7 jit_solution(2855237512290172732)
XLA Ops:
  6.5 1.6 fusion.15
  8.1 1.8 broadcast_in_dim.20
  9.9 13.5 %all-to-all-start = ((bf16[16,192,384]{2,1,0:T(8,128)(2,1)}), bf16[16,192,384]{2,1,0:T(8,128)(2,1)}, u32[]{:S(2)}, u32[]{:S(2)}) async-start(bf16[16,192,384]{2,1,0:T(8,128)(2,1)} %broadcast_in_dim.20), calls=%async_computation | async-start | bytes 4718592 | tf_op jit(solution)/shard_map/all_to_all | solution.py:30
  23.4 0.0 all-gather.3.cloned.1.call-start
  23.4 0.7 all-gather.3.cloned.1.call-update
  24.1 66.1 %all-to-all-done = bf16[16,192,384]{2,1,0:T(8,128)(2,1)} async-done(((bf16[16,192,384]{2,1,0:T(8,128)(2,1)}), bf16[16,192,384]{2,1,0:T(8,128)(2,1)}, u32[]{:S(2)}, u32[]{:S(2)}) %all-to-all-start) | async-done | bytes 2359328 | tf_op jit(solution)/shard_map/all_to_all | solution.py:30
  90.2 0.0 copy-start.4
  90.2 0.0 copy-start.1
  90.2 0.0 copy-start.2
  90.2 0.0 copy-start.3
  90.2 10.5 %all-to-all-start.1 = ((bf16[32,96,384]{2,1,0:T(8,128)(2,1)}), bf16[32,96,384]{2,1,0:T(8,128)(2,1)S(1)}, u32[]{:S(2)}, u32[]{:S(2)}) async-start(bf16[32,96,384]{2,1,0:T(8,128)(2,1)} %bitcast.8), calls=%async_computation.1 | async-start | bytes 4718592 | tf_op jit(solution)/shard_map/all_to_all | solution.py:32
  100.7 0.0 copy-done.4
  100.8 0.0 copy-done.1
  100.8 0.0 copy-done.2
  100.8 0.1 multiply_select_fusion
  100.9 0.0 copy-done.3
  100.9 0.1 reshape.91
  101.2 57.8 %all-to-all-done.1 = bf16[32,96,384]{2,1,0:T(8,128)(2,1)S(1)} async-done(((bf16[32,96,384]{2,1,0:T(8,128)(2,1)}), bf16[32,96,384]{2,1,0:T(8,128)(2,1)S(1)}, u32[]{:S(2)}, u32[]{:S(2)}) %all-to-all-start.1) | async-done | bytes 2359328 | tf_op jit(solution)/shard_map/all_to_all | solution.py:32
  159.0 0.3 slice.73
  159.3 0.9 copy.40
  160.2 0.1 slice_bitcast_fusion
  160.3 0.1 copy.49
  160.4 0.2 fusion.14
  160.6 1.3 fusion.5
  161.9 0.2 pad_maximum_fusion
  162.0 0.9 copy.46
  163.0 0.0 all-gather.3.cloned.1.call-done
  163.0 3.7 %fusion = f32[2,2,384,384,1]{3,2,1,0,4:T(8,128)S(1)} fusion(bf16[32,2,32,384,1]{3,0,2,1,4:T(8,128)(2,1)S(1)} %bitcast.57, bf16[32,2,2,48,384]{4,3,2,1,0:T(8,128)(2,1)} %bitcast.62), kind=kOutput, calls=%fused_computation | convolution fusion | flops 1207959552 | bytes 7077888 | tf_op jit(solution)/shard_map/cikbr,ckbq->kirq/dot_general | solution.py:52
  166.7 0.0 copy-start
  166.8 2.8 %convolution_convert_fusion = bf16[2,2,32,16,384]{4,3,2,1,0:T(8,128)(2,1)S(1)} fusion(bf16[32,2,2,48,384]{4,3,2,1,0:T(8,128)(2,1)} %bitcast.63, f32[2,2,384,384,1]{3,2,1,0,4:T(8,128)S(1)} %fusion, f32[2,384]{1,0:T(2,128)S(1)} %bitcast.61, f32[2,2,384]{2,0,1:T(2,128)S(1)} %copy.38), kind=kOutput, calls=%fused_computation.10 | convolution fusion | flops 606535680 | bytes 5514240 | tf_op jit(solution)/shard_map/cikmr,kirq->kicmq/dot_general | solution.py:54
  169.5 0.0 copy-done
  169.6 2.3 %bitcast_subtract_fusion = f32[1024,512]{1,0:T(8,128)} fusion(f32[1024,512]{1,0:T(8,128)S(1)} %copy-done, bf16[1024,2,384]{2,0,1:T(8,128)(2,1)S(1)} %bitcast.58, bf16[2,512,384]{2,1,0:T(8,128)(2,1)S(1)} %bitcast.56), kind=kOutput, calls=%fused_computation.5 | convolution fusion | flops 805830656 | bytes 6553600 | tf_op jit(solution)/shard_map/kicmq,knq->icmn/dot_general | solution.py:56
  (10 shorter events, 0.2 us)
Async XLA Ops:
  9.9 80.3 %all-to-all-start = ((bf16[16,192,384]{2,1,0:T(8,128)(2,1)}), bf16[16,192,384]{2,1,0:T(8,128)(2,1)}, u32[]{:S(2)}, u32[]{:S(2)}) async-start(bf16[16,192,384]{2,1,0:T(8,128)(2,1)} %broadcast_in_dim.20), calls=%async_computation | async-start | bytes 4718592 | tf_op jit(solution)/shard_map/all_to_all | solution.py:30
  23.4 139.6 %all-gather.3.cloned.1.call-start = ((), (), s32[]{:S(2)}) async-start(), calls=%async_computation.2 | async-start | bytes 4866048 | tf_op jit(solution)/shard_map/all_gather | solution.py:23
  90.2 10.5 %copy-start.4 = (s32[2,32]{1,0:T(2,128)S(1)}, s32[2,32]{1,0:T(2,128)}, u32[]{:S(2)}) copy-start(s32[2,32]{1,0:T(2,128)} %param.12) | copy-start | bytes 772
  90.2 10.6 %copy-start.1 = (f32[2,32,384]{2,1,0:T(8,128)S(1)}, f32[2,32,384]{2,1,0:T(8,128)}, u32[]{:S(2)}) copy-start(f32[2,32,384]{2,1,0:T(8,128)} %param.11) | copy-start | bytes 294916
  90.2 10.6 %copy-start.2 = (f32[2,32,384]{2,1,0:T(8,128)S(1)}, f32[2,32,384]{2,1,0:T(8,128)}, u32[]{:S(2)}) copy-start(f32[2,32,384]{2,1,0:T(8,128)} %param.10) | copy-start | bytes 294916
  90.2 10.7 %copy-start.3 = (f32[2,2,2,512]{3,2,1,0:T(2,128)S(1)}, f32[2,2,2,512]{3,2,1,0:T(2,128)}, u32[]{:S(2)}) copy-start(f32[2,2,2,512]{3,2,1,0:T(2,128)} %param.13) | copy-start | bytes 49156
  90.2 68.8 %all-to-all-start.1 = ((bf16[32,96,384]{2,1,0:T(8,128)(2,1)}), bf16[32,96,384]{2,1,0:T(8,128)(2,1)S(1)}, u32[]{:S(2)}, u32[]{:S(2)}) async-start(bf16[32,96,384]{2,1,0:T(8,128)(2,1)} %bitcast.8), calls=%async_computation.1 | async-start | bytes 4718592 | tf_op jit(solution)/shard_map/all_to_all | solution.py:32
  166.7 2.8 %copy-start = (f32[1024,512]{1,0:T(8,128)S(1)}, f32[1024,512]{1,0:T(8,128)}, u32[]{:S(2)}) copy-start(f32[1024,512]{1,0:T(8,128)} %param.7) | copy-start | bytes 6291460
Sparse Core Ops, SparseCore 0:
  26.3 93.2 all-gather.2

commit v6 on v5

--- a/solution.py
+++ b/solution.py
@@ -7,6 +7,33 @@
 def column_weight(u_scale_k, v_scale_k, ranks_k):
     position = lax.broadcasted_iota(jnp.int32, u_scale_k.shape, 1)
     return jnp.where(position < ranks_k[:, None], u_scale_k * v_scale_k, jnp.float32(0.0))
+
+
+def ring_gather(block, n_outer, n_inner, outer):
+    n = n_outer if outer else n_inner
+
+    def target(r, step):
+        a, b = divmod(r, n_inner)
+        if outer:
+            return ((a + step) % n_outer) * n_inner + b
+        return a * n_inner + (b + step) % n_inner
+
+    pieces = [block]
+    for d in range(1, n):
+        perm = [(r, target(r, -d)) for r in range(n_outer * n_inner)]
+        pieces.append(lax.ppermute(block, "row", perm))
+    return jnp.stack(pieces)
+
+
+def replicate_over_row(block, n_row):
+    n_x = 4 if n_row % 4 == 0 else n_row
+    n_z = n_row // n_x
+    row = lax.axis_index("row")
+    z, x = row // n_x, row % n_x
+    by_x = ring_gather(block, n_z, n_x, outer=False)
+    by_zx = ring_gather(by_x, n_z, n_x, outer=True)
+    by_zx = jnp.roll(jnp.roll(by_zx, z, axis=0), x, axis=1)
+    return by_zx.reshape((n_row,) + block.shape)
 
 
 def local(slab, u_codes, v_codes, u_scale, v_scale, ranks, d_inverse):
@@ -26,8 +53,7 @@
 
     n_row = lax.axis_size("row")
     flat = shard.reshape(per_row * panels * both, rank_most)
-    spread = jnp.broadcast_to(flat[None], (n_row,) + flat.shape)
-    every_tile = lax.all_to_all(spread, "row", 0, 0, tiled=True)
+    every_tile = replicate_over_row(flat, n_row)
     every_tile = every_tile.reshape(n_row * per_row, panels * both, rank_most)
     col_all = lax.all_to_all(every_tile, "col", 0, 0, tiled=True)
     col_all = col_all.reshape(n_col, panels, both, rank_most)

time: 179 us -> 191 us (1.067)
  starting transfers between devices: 24 us -> 36.8 us
  waiting for transfers between devices: 125 us -> 119 us
  other arithmetic: 3.12 us -> 5.8 us
    all_to_all x1 -> x0, waiting for transfers between devices: 66.1 us -> none  [local(): every_tile = lax.all_to_all(spread, 'row', 0, 0, tiled=True)]
    ppermute x0 -> x6, waiting for transfers between devices: none -> 63.8 us  [ring_gather(): pieces.append(lax.ppermute(block, 'row', perm))]
    ppermute x0 -> x6, starting transfers between devices: none -> 28.8 us  [ring_gather(): pieces.append(lax.ppermute(block, 'row', perm))]
    all_to_all x1 -> x0, starting transfers between devices: 13.5 us -> none  [local(): every_tile = lax.all_to_all(spread, 'row', 0, 0, tiled=True)]
    all_to_all x1, waiting for transfers between devices: 57.8 us -> 55 us  [local(): col_all = lax.all_to_all(every_tile, 'col', 0, 0, tiled=True)]
    all_to_all x1, starting transfers between devices: 10.5 us -> 8 us  [local(): col_all = lax.all_to_all(every_tile, 'col', 0, 0, tiled=True)]
    concatenate x0 -> x1, other arithmetic: none -> 2.43 us  [replicate_over_row(): by_zx = jnp.roll(jnp.roll(by_zx, z, axis=0), x, axis=1)]
  transfers between devices with their start and end apart: 3 -> 8, of which waited for: 2 -> 6; matrix products, arithmetic and copies ran while one was open for 2% -> 5% of each run, Pallas kernels for 0% -> 0%
where the time goes in v6:
time: 191 us; the launch traced here: 189 us
  waiting for transfers between devices  119 us (62%)
  starting transfers between devices  36.8 us (19%)
  between operations  13.8 us (7%)
  matrix products  9.31 us (5%)
  other arithmetic  5.8 us (3%)
  local copies, waits for them, and re-layouts  4.74 us (2%)
    ppermute x6, waiting for transfers between devices, ring_gather(): pieces.append(lax.ppermute(block, 'row', perm))  63.8 us
    all_to_all x1, waiting for transfers between devices, local(): col_all = lax.all_to_all(every_tile, 'col', 0, 0, tiled=True)  55 us
    ppermute x6, starting transfers between devices, ring_gather(): pieces.append(lax.ppermute(block, 'row', perm))  28.8 us
    all_to_all x1, starting transfers between devices, local(): col_all = lax.all_to_all(every_tile, 'col', 0, 0, tiled=True)  8 us
    dot_general x1, matrix products, local(): jnp.einsum('cikbr,ckbq->kirq', row_v, col_scaled, preferred_element_type=...  4.19 us
  transfers between devices with their start and end apart: 8, of which 6 were waited for; matrix products, arithmetic and copies ran while one was open for 5% of the time, Pallas kernels for 0%

profile of v6, /device:TPU:1, one launch (start us, length us, event | category | flops | bytes accessed | tf_op | source)
XLA Modules:
  0.0 189.3 jit_solution(12364128112461028893)
XLA Ops:
  6.5 0.0 all-gather.3.cloned.1.call-start
  6.5 1.6 fusion.16
  8.1 0.0 all-gather.3.cloned.1.call-update
  8.1 5.5 %collective-permute-start.1 = (bf16[192,384]{1,0:T(8,128)(2,1)S(1)}, bf16[192,384]{1,0:T(8,128)(2,1)S(1)}, u32[]{:S(2)}, u32[]{:S(2)}) collective-permute-start(bf16[192,384]{1,0:T(8,128)(2,1)S(1)} %bitcast.75), channel_id=1, source_target_pairs={{0,64},{32,96},{64,0},{96,32},{128,192},{160,224},{192,128},{224,1... | collective-permute-start | bytes 442376 | tf_op jit(solution)/shard_map/ppermute | solution.py:24
  13.6 2.2 %collective-permute-start.2 = (bf16[192,384]{1,0:T(8,128)(2,1)S(1)}, bf16[192,384]{1,0:T(8,128)(2,1)S(1)}, u32[]{:S(2)}, u32[]{:S(2)}) collective-permute-start(bf16[192,384]{1,0:T(8,128)(2,1)S(1)} %bitcast.76), channel_id=1, source_target_pairs={{0,32},{32,64},{64,96},{96,0},{128,160},{160,192},{192,224},{224,1... | collective-permute-start | bytes 442376 | tf_op jit(solution)/shard_map/ppermute | solution.py:24
  15.8 4.3 %collective-permute-start = (bf16[192,384]{1,0:T(8,128)(2,1)S(1)}, bf16[192,384]{1,0:T(8,128)(2,1)S(1)}, u32[]{:S(2)}, u32[]{:S(2)}) collective-permute-start(bf16[192,384]{1,0:T(8,128)(2,1)S(1)} %bitcast.77), channel_id=1, source_target_pairs={{0,96},{32,0},{64,32},{96,64},{128,224},{160,128},{192,160},{224,1... | collective-permute-start | bytes 442376 | tf_op jit(solution)/shard_map/ppermute | solution.py:24
  20.1 0.0 collective-permute-done.1
  20.1 0.6 collective-permute-done.2
  20.7 1.5 collective-permute-done
  22.2 0.1 pad_maximum_fusion.1
  22.3 10.7 %collective-permute-start.3 = (bf16[4,192,384]{2,1,0:T(8,128)(2,1)S(1)}, bf16[4,192,384]{2,1,0:T(8,128)(2,1)S(1)}, u32[]{:S(2)}, u32[]{:S(2)}) collective-permute-start(bf16[4,192,384]{2,1,0:T(8,128)(2,1)S(1)} %pad_maximum_fusion.1), channel_id=1, source_target_pairs={{0,384},{32,416},{64,448},{96,480},{128,0},{160,32},{192,64},{224,... | collective-permute-start | bytes 1769480 | tf_op jit(solution)/shard_map/ppermute | solution.py:24
  33.0 1.9 %collective-permute-start.4 = (bf16[4,192,384]{2,1,0:T(8,128)(2,1)S(1)}, bf16[4,192,384]{2,1,0:T(8,128)(2,1)S(1)}, u32[]{:S(2)}, u32[]{:S(2)}) collective-permute-start(bf16[4,192,384]{2,1,0:T(8,128)(2,1)S(1)} %pad_maximum_fusion.1), channel_id=1, source_target_pairs={{0,256},{32,288},{64,320},{96,352},{128,384},{160,416},{192,448},{... | collective-permute-start | bytes 1769480 | tf_op jit(solution)/shard_map/ppermute | solution.py:24
  35.0 4.2 %collective-permute-start.5 = (bf16[4,192,384]{2,1,0:T(8,128)(2,1)S(1)}, bf16[4,192,384]{2,1,0:T(8,128)(2,1)S(1)}, u32[]{:S(2)}, u32[]{:S(2)}) collective-permute-start(bf16[4,192,384]{2,1,0:T(8,128)(2,1)S(1)} %pad_maximum_fusion.1), channel_id=1, source_target_pairs={{0,128},{32,160},{64,192},{96,224},{128,256},{160,288},{192,320},{... | collective-permute-start | bytes 1769480 | tf_op jit(solution)/shard_map/ppermute | solution.py:24
  39.2 0.1 bitcast_dynamic-update-slice_fusion.6
  39.3 4.6 %collective-permute-done.3 = bf16[4,192,384]{2,1,0:T(8,128)(2,1)S(1)} collective-permute-done((bf16[4,192,384]{2,1,0:T(8,128)(2,1)S(1)}, bf16[4,192,384]{2,1,0:T(8,128)(2,1)S(1)}, u32[]{:S(2)}, u32[]{:S(2)}) %collective-permute-start.3) | collective-permute-done | bytes 589856 | tf_op jit(solution)/shard_map/ppermute | solution.py:24
  43.8 0.1 bitcast_dynamic-update-slice_fusion.4
  43.9 42.8 %collective-permute-done.4 = bf16[4,192,384]{2,1,0:T(8,128)(2,1)S(1)} collective-permute-done((bf16[4,192,384]{2,1,0:T(8,128)(2,1)S(1)}, bf16[4,192,384]{2,1,0:T(8,128)(2,1)S(1)}, u32[]{:S(2)}, u32[]{:S(2)}) %collective-permute-start.4) | collective-permute-done | bytes 589856 | tf_op jit(solution)/shard_map/ppermute | solution.py:24
  86.8 0.1 bitcast_dynamic-update-slice_fusion.2
  86.9 14.3 %collective-permute-done.5 = bf16[4,192,384]{2,1,0:T(8,128)(2,1)S(1)} collective-permute-done((bf16[4,192,384]{2,1,0:T(8,128)(2,1)S(1)}, bf16[4,192,384]{2,1,0:T(8,128)(2,1)S(1)}, u32[]{:S(2)}, u32[]{:S(2)}) %collective-permute-start.5) | collective-permute-done | bytes 589856 | tf_op jit(solution)/shard_map/ppermute | solution.py:24
  101.2 0.1 bitcast_dynamic-update-slice_fusion
  101.3 0.1 bitcast_dynamic-update-slice_fusion.7
  101.4 0.1 bitcast_dynamic-update-slice_fusion.5
  101.5 0.1 bitcast_dynamic-update-slice_fusion.3
  101.6 0.1 bitcast_dynamic-update-slice_fusion.1
  101.7 0.3 constant_dynamic-slice_fusion
  102.0 2.4 %fusion.2 = bf16[4,4,192,384]{3,2,1,0:T(8,128)(2,1)} fusion(s32[]{:T(128)S(6)} %select_n.57, bf16[4,4,192,384]{3,2,1,0:T(8,128)(2,1)S(1)} %constant_dynamic-slice_fusion), kind=kLoop, calls=%fused_computation.4 | loop fusion | flops 1179648 | bytes 4718596 | tf_op jit(solution)/shard_map/jit(_roll_dynamic)/concatenate | solution.py:35
  104.4 8.0 %all-to-all-start = ((bf16[32,96,384]{2,1,0:T(8,128)(2,1)}), bf16[32,96,384]{2,1,0:T(8,128)(2,1)S(1)}, u32[]{:S(2)}, u32[]{:S(2)}) async-start(bf16[32,96,384]{2,1,0:T(8,128)(2,1)} %bitcast.72), calls=%async_computation | async-start | bytes 4718592 | tf_op jit(solution)/shard_map/all_to_all | solution.py:58
  112.4 0.0 copy-done.3
  112.5 0.1 reshape.90
  112.7 0.0 copy-done.4
  112.7 0.0 copy-done.1
  112.8 0.0 copy-done.2
  112.8 0.1 multiply_select_fusion
  112.9 55.0 %all-to-all-done = bf16[32,96,384]{2,1,0:T(8,128)(2,1)S(1)} async-done(((bf16[32,96,384]{2,1,0:T(8,128)(2,1)}), bf16[32,96,384]{2,1,0:T(8,128)(2,1)S(1)}, u32[]{:S(2)}, u32[]{:S(2)}) %all-to-all-start) | async-done | bytes 2359328 | tf_op jit(solution)/shard_map/all_to_all | solution.py:58
  168.0 0.3 slice.73
  168.2 0.9 copy.40
  169.2 0.2 fusion.15
  169.4 1.3 fusion.6
  170.6 0.2 pad_maximum_fusion
  170.8 2.1 %copy.46 = bf16[32,2,16,2,384]{4,0,3,2,1:T(8,128)(2,1)} copy(bf16[32,2,16,2,384]{4,2,3,1,0:T(8,128)(2,1)S(1)} %pad_maximum_fusion) | data formatting | bytes 3145728 | tf_op jit(solution)/shard_map/stack | solution.py:76
  172.9 0.1 slice_bitcast_fusion
  173.0 0.1 copy.49
  173.1 0.0 all-gather.3.cloned.1.call-done
  173.1 4.2 %fusion = f32[2,2,384,384,1]{3,2,1,0,4:T(8,128)S(1)} fusion(bf16[32,2,32,384,1]{3,0,2,1,4:T(8,128)(2,1)} %bitcast.81, bf16[32,2,2,48,384]{4,3,2,1,0:T(8,128)(2,1)} %bitcast.94), kind=kOutput, calls=%fused_computation.2 | convolution fusion | flops 1207959552 | bytes 7077888 | tf_op jit(solution)/shard_map/cikbr,ckbq->kirq/dot_general | solution.py:78
  177.3 0.0 copy-start
  177.3 2.8 %convolution_convert_fusion = bf16[2,2,32,16,384]{4,3,2,1,0:T(8,128)(2,1)S(1)} fusion(bf16[32,2,2,48,384]{4,3,2,1,0:T(8,128)(2,1)} %bitcast.95, f32[2,2,384,384,1]{3,2,1,0,4:T(8,128)S(1)} %fusion, f32[2,384]{1,0:T(2,128)S(1)} %bitcast.93, f32[2,2,384]{2,0,1:T(2,128)S(1)} %copy.38), kind=kOutput, calls=%fused_computation.13 | convolution fusion | flops 606535680 | bytes 5514240 | tf_op jit(solution)/shard_map/cikmr,kirq->kicmq/dot_general | solution.py:80
  180.1 0.0 copy-done
  180.1 2.3 %bitcast_subtract_fusion = f32[1024,512]{1,0:T(8,128)} fusion(f32[1024,512]{1,0:T(8,128)S(1)} %copy-done, bf16[1024,2,384]{2,0,1:T(8,128)(2,1)S(1)} %bitcast.82, bf16[2,512,384]{2,1,0:T(8,128)(2,1)S(1)} %bitcast.74), kind=kOutput, calls=%fused_computation.8 | convolution fusion | flops 805830656 | bytes 6553600 | tf_op jit(solution)/shard_map/kicmq,knq->icmn/dot_general | solution.py:82
  (14 shorter events, 0.2 us)
Async XLA Ops:
  6.5 166.6 %all-gather.3.cloned.1.call-start = ((), (), s32[]{:S(2)}) async-start(), calls=%async_computation.1 | async-start | bytes 4866048 | tf_op jit(solution)/shard_map/all_gather | solution.py:50
  8.1 12.0 %collective-permute-start.1 = (bf16[192,384]{1,0:T(8,128)(2,1)S(1)}, bf16[192,384]{1,0:T(8,128)(2,1)S(1)}, u32[]{:S(2)}, u32[]{:S(2)}) collective-permute-start(bf16[192,384]{1,0:T(8,128)(2,1)S(1)} %bitcast.75), channel_id=1, source_target_pairs={{0,64},{32,96},{64,0},{96,32},{128,192},{160,224},{192,128},{224,1... | collective-permute-start | bytes 442376 | tf_op jit(solution)/shard_map/ppermute | solution.py:24
  13.6 7.1 %collective-permute-start.2 = (bf16[192,384]{1,0:T(8,128)(2,1)S(1)}, bf16[192,384]{1,0:T(8,128)(2,1)S(1)}, u32[]{:S(2)}, u32[]{:S(2)}) collective-permute-start(bf16[192,384]{1,0:T(8,128)(2,1)S(1)} %bitcast.76), channel_id=1, source_target_pairs={{0,32},{32,64},{64,96},{96,0},{128,160},{160,192},{192,224},{224,1... | collective-permute-start | bytes 442376 | tf_op jit(solution)/shard_map/ppermute | solution.py:24
  15.8 6.4 %collective-permute-start = (bf16[192,384]{1,0:T(8,128)(2,1)S(1)}, bf16[192,384]{1,0:T(8,128)(2,1)S(1)}, u32[]{:S(2)}, u32[]{:S(2)}) collective-permute-start(bf16[192,384]{1,0:T(8,128)(2,1)S(1)} %bitcast.77), channel_id=1, source_target_pairs={{0,96},{32,0},{64,32},{96,64},{128,224},{160,128},{192,160},{224,1... | collective-permute-start | bytes 442376 | tf_op jit(solution)/shard_map/ppermute | solution.py:24
  22.3 21.5 %collective-permute-start.3 = (bf16[4,192,384]{2,1,0:T(8,128)(2,1)S(1)}, bf16[4,192,384]{2,1,0:T(8,128)(2,1)S(1)}, u32[]{:S(2)}, u32[]{:S(2)}) collective-permute-start(bf16[4,192,384]{2,1,0:T(8,128)(2,1)S(1)} %pad_maximum_fusion.1), channel_id=1, source_target_pairs={{0,384},{32,416},{64,448},{96,480},{128,0},{160,32},{192,64},{224,... | collective-permute-start | bytes 1769480 | tf_op jit(solution)/shard_map/ppermute | solution.py:24
  33.0 53.8 %collective-permute-start.4 = (bf16[4,192,384]{2,1,0:T(8,128)(2,1)S(1)}, bf16[4,192,384]{2,1,0:T(8,128)(2,1)S(1)}, u32[]{:S(2)}, u32[]{:S(2)}) collective-permute-start(bf16[4,192,384]{2,1,0:T(8,128)(2,1)S(1)} %pad_maximum_fusion.1), channel_id=1, source_target_pairs={{0,256},{32,288},{64,320},{96,352},{128,384},{160,416},{192,448},{... | collective-permute-start | bytes 1769480 | tf_op jit(solution)/shard_map/ppermute | solution.py:24
  35.0 66.2 %collective-permute-start.5 = (bf16[4,192,384]{2,1,0:T(8,128)(2,1)S(1)}, bf16[4,192,384]{2,1,0:T(8,128)(2,1)S(1)}, u32[]{:S(2)}, u32[]{:S(2)}) collective-permute-start(bf16[4,192,384]{2,1,0:T(8,128)(2,1)S(1)} %pad_maximum_fusion.1), channel_id=1, source_target_pairs={{0,128},{32,160},{64,192},{96,224},{128,256},{160,288},{192,320},{... | collective-permute-start | bytes 1769480 | tf_op jit(solution)/shard_map/ppermute | solution.py:24
  104.4 8.0 %copy-start.3 = (f32[2,2,2,512]{3,2,1,0:T(2,128)S(1)}, f32[2,2,2,512]{3,2,1,0:T(2,128)}, u32[]{:S(2)}) copy-start(f32[2,2,2,512]{3,2,1,0:T(2,128)} %param.13) | copy-start | bytes 49156
  104.4 8.3 %copy-start.4 = (s32[2,32]{1,0:T(2,128)S(1)}, s32[2,32]{1,0:T(2,128)}, u32[]{:S(2)}) copy-start(s32[2,32]{1,0:T(2,128)} %param.12) | copy-start | bytes 772
  104.4 8.3 %copy-start.1 = (f32[2,32,384]{2,1,0:T(8,128)S(1)}, f32[2,32,384]{2,1,0:T(8,128)}, u32[]{:S(2)}) copy-start(f32[2,32,384]{2,1,0:T(8,128)} %param.11) | copy-start | bytes 294916
  104.4 8.3 %copy-start.2 = (f32[2,32,384]{2,1,0:T(8,128)S(1)}, f32[2,32,384]{2,1,0:T(8,128)}, u32[]{:S(2)}) copy-start(f32[2,32,384]{2,1,0:T(8,128)} %param.10) | copy-start | bytes 294916
  104.4 63.5 %all-to-all-start = ((bf16[32,96,384]{2,1,0:T(8,128)(2,1)}), bf16[32,96,384]{2,1,0:T(8,128)(2,1)S(1)}, u32[]{:S(2)}, u32[]{:S(2)}) async-start(bf16[32,96,384]{2,1,0:T(8,128)(2,1)} %bitcast.72), calls=%async_computation | async-start | bytes 4718592 | tf_op jit(solution)/shard_map/all_to_all | solution.py:58
  177.3 2.8 %copy-start = (f32[1024,512]{1,0:T(8,128)S(1)}, f32[1024,512]{1,0:T(8,128)}, u32[]{:S(2)}) copy-start(f32[1024,512]{1,0:T(8,128)} %param.7) | copy-start | bytes 6291460
Sparse Core Ops, SparseCore 0:
  9.5 104.8 all-gather.2

commit v7 on v6

--- a/solution.py
+++ b/solution.py
@@ -30,9 +30,9 @@
     n_z = n_row // n_x
     row = lax.axis_index("row")
     z, x = row // n_x, row % n_x
-    by_x = ring_gather(block, n_z, n_x, outer=False)
-    by_zx = ring_gather(by_x, n_z, n_x, outer=True)
-    by_zx = jnp.roll(jnp.roll(by_zx, z, axis=0), x, axis=1)
+    by_z = ring_gather(block, n_z, n_x, outer=True)
+    by_xz = ring_gather(by_z, n_z, n_x, outer=False)
+    by_zx = jnp.roll(jnp.roll(by_xz, x, axis=0), z, axis=1).swapaxes(0, 1)
     return by_zx.reshape((n_row,) + block.shape)
 
 

time: 191 us -> 160 us (0.84)
  waiting for transfers between devices: 119 us -> 85.1 us
  starting transfers between devices: 36.8 us -> 40.7 us
    ppermute x6, waiting for transfers between devices: 63.8 us -> 30 us  [ring_gather(): pieces.append(lax.ppermute(block, 'row', perm))]
    all_to_all x1, starting transfers between devices: 8 us -> 10.7 us  [local(): col_all = lax.all_to_all(every_tile, 'col', 0, 0, tiled=True)]
    concatenate x1 -> x0, other arithmetic: 2.43 us -> none  [replicate_over_row(): by_zx = jnp.roll(jnp.roll(by_zx, z, axis=0), x, axis=1)]
  transfers between devices with their start and end apart: 8 -> 8, of which waited for: 6 -> 5; matrix products, arithmetic and copies ran while one was open for 5% -> 6% of each run, Pallas kernels for 0% -> 0%
where the time goes in v7:
time: 160 us
  waiting for transfers between devices  85.1 us (53%)
  starting transfers between devices  40.7 us (25%)
  between operations  13.8 us (9%)
  matrix products  9.32 us (6%)
  local copies, waits for them, and re-layouts  6.46 us (4%)
  other arithmetic  4.35 us (3%)
    all_to_all x1, waiting for transfers between devices, local(): col_all = lax.all_to_all(every_tile, 'col', 0, 0, tiled=True)  55 us
    ppermute x6, waiting for transfers between devices, ring_gather(): pieces.append(lax.ppermute(block, 'row', perm))  30 us
    ppermute x6, starting transfers between devices, ring_gather(): pieces.append(lax.ppermute(block, 'row', perm))  30 us
    all_to_all x1, starting transfers between devices, local(): col_all = lax.all_to_all(every_tile, 'col', 0, 0, tiled=True)  10.7 us
    dot_general x1, matrix products, local(): jnp.einsum('cikbr,ckbq->kirq', row_v, col_scaled, preferred_element_type=...  4.2 us
  transfers between devices with their start and end apart: 8, of which 5 were waited for; matrix products, arithmetic and copies ran while one was open for 6% of the time, Pallas kernels for 0%

profile of v7, /device:TPU:1, one launch (start us, length us, event | category | flops | bytes accessed | tf_op | source)
XLA Modules:
  0.0 159.8 jit_solution(17271817464519575812)
XLA Ops:
  6.5 0.0 all-gather.3.cloned.1.call-start
  6.5 1.6 fusion.17
  8.1 0.0 all-gather.3.cloned.1.call-update
  8.1 11.5 %collective-permute-start.1 = (bf16[192,384]{1,0:T(8,128)(2,1)S(1)}, bf16[192,384]{1,0:T(8,128)(2,1)S(1)}, u32[]{:S(2)}, u32[]{:S(2)}) collective-permute-start(bf16[192,384]{1,0:T(8,128)(2,1)S(1)} %bitcast.77), channel_id=1, source_target_pairs={{0,256},{32,288},{64,320},{96,352},{128,384},{160,416},{192,448},{... | collective-permute-start | bytes 442376 | tf_op jit(solution)/shard_map/ppermute | solution.py:24
  19.6 4.0 %collective-permute-start.2 = (bf16[192,384]{1,0:T(8,128)(2,1)S(1)}, bf16[192,384]{1,0:T(8,128)(2,1)S(1)}, u32[]{:S(2)}, u32[]{:S(2)}) collective-permute-start(bf16[192,384]{1,0:T(8,128)(2,1)S(1)} %bitcast.78), channel_id=1, source_target_pairs={{0,128},{32,160},{64,192},{96,224},{128,256},{160,288},{192,320},{... | collective-permute-start | bytes 442376 | tf_op jit(solution)/shard_map/ppermute | solution.py:24
  23.6 3.4 %collective-permute-start = (bf16[192,384]{1,0:T(8,128)(2,1)S(1)}, bf16[192,384]{1,0:T(8,128)(2,1)S(1)}, u32[]{:S(2)}, u32[]{:S(2)}) collective-permute-start(bf16[192,384]{1,0:T(8,128)(2,1)S(1)} %bitcast.79), channel_id=1, source_target_pairs={{0,384},{32,416},{64,448},{96,480},{128,0},{160,32},{192,64},{224,... | collective-permute-start | bytes 442376 | tf_op jit(solution)/shard_map/ppermute | solution.py:24
  27.0 0.0 collective-permute-done.1
  27.0 2.9 %collective-permute-done.2 = bf16[192,384]{1,0:T(8,128)(2,1)S(1)} collective-permute-done((bf16[192,384]{1,0:T(8,128)(2,1)S(1)}, bf16[192,384]{1,0:T(8,128)(2,1)S(1)}, u32[]{:S(2)}, u32[]{:S(2)}) %collective-permute-start.2) | collective-permute-done | bytes 147488 | tf_op jit(solution)/shard_map/ppermute | solution.py:24
  30.0 0.6 collective-permute-done
  30.5 0.1 pad_maximum_fusion.1
  30.6 6.7 %collective-permute-start.3 = (bf16[4,192,384]{2,1,0:T(8,128)(2,1)S(1)}, bf16[4,192,384]{2,1,0:T(8,128)(2,1)S(1)}, u32[]{:S(2)}, u32[]{:S(2)}) collective-permute-start(bf16[4,192,384]{2,1,0:T(8,128)(2,1)S(1)} %pad_maximum_fusion.1), channel_id=1, source_target_pairs={{0,96},{32,0},{64,32},{96,64},{128,224},{160,128},{192,160},{224,1... | collective-permute-start | bytes 1769480 | tf_op jit(solution)/shard_map/ppermute | solution.py:24
  37.4 1.9 %collective-permute-start.4 = (bf16[4,192,384]{2,1,0:T(8,128)(2,1)S(1)}, bf16[4,192,384]{2,1,0:T(8,128)(2,1)S(1)}, u32[]{:S(2)}, u32[]{:S(2)}) collective-permute-start(bf16[4,192,384]{2,1,0:T(8,128)(2,1)S(1)} %pad_maximum_fusion.1), channel_id=1, source_target_pairs={{0,64},{32,96},{64,0},{96,32},{128,192},{160,224},{192,128},{224,1... | collective-permute-start | bytes 1769480 | tf_op jit(solution)/shard_map/ppermute | solution.py:24
  39.4 2.5 %collective-permute-start.5 = (bf16[4,192,384]{2,1,0:T(8,128)(2,1)S(1)}, bf16[4,192,384]{2,1,0:T(8,128)(2,1)S(1)}, u32[]{:S(2)}, u32[]{:S(2)}) collective-permute-start(bf16[4,192,384]{2,1,0:T(8,128)(2,1)S(1)} %pad_maximum_fusion.1), channel_id=1, source_target_pairs={{0,32},{32,64},{64,96},{96,0},{128,160},{160,192},{192,224},{224,1... | collective-permute-start | bytes 1769480 | tf_op jit(solution)/shard_map/ppermute | solution.py:24
  41.9 0.1 bitcast_dynamic-update-slice_fusion.6
  41.9 18.2 %collective-permute-done.3 = bf16[4,192,384]{2,1,0:T(8,128)(2,1)S(1)} collective-permute-done((bf16[4,192,384]{2,1,0:T(8,128)(2,1)S(1)}, bf16[4,192,384]{2,1,0:T(8,128)(2,1)S(1)}, u32[]{:S(2)}, u32[]{:S(2)}) %collective-permute-start.3) | collective-permute-done | bytes 589856 | tf_op jit(solution)/shard_map/ppermute | solution.py:24
  60.1 0.1 bitcast_dynamic-update-slice_fusion.4
  60.2 0.0 collective-permute-done.4
  60.2 0.1 bitcast_dynamic-update-slice_fusion.2
  60.3 8.3 %collective-permute-done.5 = bf16[4,192,384]{2,1,0:T(8,128)(2,1)S(1)} collective-permute-done((bf16[4,192,384]{2,1,0:T(8,128)(2,1)S(1)}, bf16[4,192,384]{2,1,0:T(8,128)(2,1)S(1)}, u32[]{:S(2)}, u32[]{:S(2)}) %collective-permute-start.5) | collective-permute-done | bytes 589856 | tf_op jit(solution)/shard_map/ppermute | solution.py:24
  68.7 0.1 bitcast_dynamic-update-slice_fusion
  68.8 0.1 bitcast_dynamic-update-slice_fusion.7
  68.9 0.1 bitcast_dynamic-update-slice_fusion.5
  69.0 0.1 bitcast_dynamic-update-slice_fusion.3
  69.1 0.1 bitcast_dynamic-update-slice_fusion.1
  69.2 0.3 constant_dynamic-slice_fusion
  69.5 1.0 fusion.3
  70.5 1.7 %copy.43 = bf16[4,4,192,384]{3,2,1,0:T(8,128)(2,1)} copy(bf16[4,4,192,384]{3,2,0,1:T(8,128)(2,1)S(1)} %fusion.3) | data formatting | bytes 4718592 | tf_op jit(solution)/shard_map/transpose | solution.py:35
  72.2 10.7 %all-to-all-start = ((bf16[32,96,384]{2,1,0:T(8,128)(2,1)}), bf16[32,96,384]{2,1,0:T(8,128)(2,1)S(1)}, u32[]{:S(2)}, u32[]{:S(2)}) async-start(bf16[32,96,384]{2,1,0:T(8,128)(2,1)} %bitcast.74), calls=%async_computation | async-start | bytes 4718592 | tf_op jit(solution)/shard_map/all_to_all | solution.py:58
  82.9 0.0 copy-done.3
  82.9 0.1 reshape.90
  83.2 0.0 copy-done.4
  83.2 0.0 copy-done.1
  83.2 0.0 copy-done.2
  83.3 0.1 multiply_select_fusion
  83.4 55.0 %all-to-all-done = bf16[32,96,384]{2,1,0:T(8,128)(2,1)S(1)} async-done(((bf16[32,96,384]{2,1,0:T(8,128)(2,1)}), bf16[32,96,384]{2,1,0:T(8,128)(2,1)S(1)}, u32[]{:S(2)}, u32[]{:S(2)}) %all-to-all-start) | async-done | bytes 2359328 | tf_op jit(solution)/shard_map/all_to_all | solution.py:58
  138.4 0.3 slice.73
  138.7 0.9 copy.44
  139.7 0.2 fusion.16
  139.9 1.3 fusion.7
  141.1 0.2 pad_maximum_fusion
  141.3 2.1 %copy.50 = bf16[32,2,16,2,384]{4,0,3,2,1:T(8,128)(2,1)} copy(bf16[32,2,16,2,384]{4,2,3,1,0:T(8,128)(2,1)S(1)} %pad_maximum_fusion) | data formatting | bytes 3145728 | tf_op jit(solution)/shard_map/stack | solution.py:76
  143.4 0.1 slice_bitcast_fusion
  143.5 0.1 copy.53
  143.6 0.0 all-gather.3.cloned.1.call-done
  143.6 4.2 %fusion = f32[2,2,384,384,1]{3,2,1,0,4:T(8,128)S(1)} fusion(bf16[32,2,32,384,1]{3,0,2,1,4:T(8,128)(2,1)} %bitcast.83, bf16[32,2,2,48,384]{4,3,2,1,0:T(8,128)(2,1)} %bitcast.96), kind=kOutput, calls=%fused_computation.2 | convolution fusion | flops 1207959552 | bytes 7077888 | tf_op jit(solution)/shard_map/cikbr,ckbq->kirq/dot_general | solution.py:78
  147.8 0.0 copy-start
  147.8 2.8 %convolution_convert_fusion = bf16[2,2,32,16,384]{4,3,2,1,0:T(8,128)(2,1)S(1)} fusion(bf16[32,2,2,48,384]{4,3,2,1,0:T(8,128)(2,1)} %bitcast.97, f32[2,2,384,384,1]{3,2,1,0,4:T(8,128)S(1)} %fusion, f32[2,384]{1,0:T(2,128)S(1)} %bitcast.95, f32[2,2,384]{2,0,1:T(2,128)S(1)} %copy.41), kind=kOutput, calls=%fused_computation.14 | convolution fusion | flops 606535680 | bytes 5514240 | tf_op jit(solution)/shard_map/cikmr,kirq->kicmq/dot_general | solution.py:80
  150.6 2.3 %bitcast_subtract_fusion = f32[1024,512]{1,0:T(8,128)} fusion(f32[1024,512]{1,0:T(8,128)S(1)} %copy-done, bf16[1024,2,384]{2,0,1:T(8,128)(2,1)S(1)} %bitcast.84, bf16[2,512,384]{2,1,0:T(8,128)(2,1)S(1)} %bitcast.76), kind=kOutput, calls=%fused_computation.9 | convolution fusion | flops 805830656 | bytes 6553600 | tf_op jit(solution)/shard_map/kicmq,knq->icmn/dot_general | solution.py:82
  (15 shorter events, 0.2 us)
Async XLA Ops:
  6.5 137.0 %all-gather.3.cloned.1.call-start = ((), (), s32[]{:S(2)}) async-start(), calls=%async_computation.1 | async-start | bytes 4866048 | tf_op jit(solution)/shard_map/all_gather | solution.py:50
  8.1 18.9 %collective-permute-start.1 = (bf16[192,384]{1,0:T(8,128)(2,1)S(1)}, bf16[192,384]{1,0:T(8,128)(2,1)S(1)}, u32[]{:S(2)}, u32[]{:S(2)}) collective-permute-start(bf16[192,384]{1,0:T(8,128)(2,1)S(1)} %bitcast.77), channel_id=1, source_target_pairs={{0,256},{32,288},{64,320},{96,352},{128,384},{160,416},{192,448},{... | collective-permute-start | bytes 442376 | tf_op jit(solution)/shard_map/ppermute | solution.py:24
  19.6 10.4 %collective-permute-start.2 = (bf16[192,384]{1,0:T(8,128)(2,1)S(1)}, bf16[192,384]{1,0:T(8,128)(2,1)S(1)}, u32[]{:S(2)}, u32[]{:S(2)}) collective-permute-start(bf16[192,384]{1,0:T(8,128)(2,1)S(1)} %bitcast.78), channel_id=1, source_target_pairs={{0,128},{32,160},{64,192},{96,224},{128,256},{160,288},{192,320},{... | collective-permute-start | bytes 442376 | tf_op jit(solution)/shard_map/ppermute | solution.py:24
  23.6 6.9 %collective-permute-start = (bf16[192,384]{1,0:T(8,128)(2,1)S(1)}, bf16[192,384]{1,0:T(8,128)(2,1)S(1)}, u32[]{:S(2)}, u32[]{:S(2)}) collective-permute-start(bf16[192,384]{1,0:T(8,128)(2,1)S(1)} %bitcast.79), channel_id=1, source_target_pairs={{0,384},{32,416},{64,448},{96,480},{128,0},{160,32},{192,64},{224,... | collective-permute-start | bytes 442376 | tf_op jit(solution)/shard_map/ppermute | solution.py:24
  30.6 29.5 %collective-permute-start.3 = (bf16[4,192,384]{2,1,0:T(8,128)(2,1)S(1)}, bf16[4,192,384]{2,1,0:T(8,128)(2,1)S(1)}, u32[]{:S(2)}, u32[]{:S(2)}) collective-permute-start(bf16[4,192,384]{2,1,0:T(8,128)(2,1)S(1)} %pad_maximum_fusion.1), channel_id=1, source_target_pairs={{0,96},{32,0},{64,32},{96,64},{128,224},{160,128},{192,160},{224,1... | collective-permute-start | bytes 1769480 | tf_op jit(solution)/shard_map/ppermute | solution.py:24
  37.4 22.8 %collective-permute-start.4 = (bf16[4,192,384]{2,1,0:T(8,128)(2,1)S(1)}, bf16[4,192,384]{2,1,0:T(8,128)(2,1)S(1)}, u32[]{:S(2)}, u32[]{:S(2)}) collective-permute-start(bf16[4,192,384]{2,1,0:T(8,128)(2,1)S(1)} %pad_maximum_fusion.1), channel_id=1, source_target_pairs={{0,64},{32,96},{64,0},{96,32},{128,192},{160,224},{192,128},{224,1... | collective-permute-start | bytes 1769480 | tf_op jit(solution)/shard_map/ppermute | solution.py:24
  39.4 29.3 %collective-permute-start.5 = (bf16[4,192,384]{2,1,0:T(8,128)(2,1)S(1)}, bf16[4,192,384]{2,1,0:T(8,128)(2,1)S(1)}, u32[]{:S(2)}, u32[]{:S(2)}) collective-permute-start(bf16[4,192,384]{2,1,0:T(8,128)(2,1)S(1)} %pad_maximum_fusion.1), channel_id=1, source_target_pairs={{0,32},{32,64},{64,96},{96,0},{128,160},{160,192},{192,224},{224,1... | collective-permute-start | bytes 1769480 | tf_op jit(solution)/shard_map/ppermute | solution.py:24
  72.2 10.8 %copy-start.3 = (f32[2,2,2,512]{3,2,1,0:T(2,128)S(1)}, f32[2,2,2,512]{3,2,1,0:T(2,128)}, u32[]{:S(2)}) copy-start(f32[2,2,2,512]{3,2,1,0:T(2,128)} %param.13) | copy-start | bytes 49156
  72.2 11.0 %copy-start.4 = (s32[2,32]{1,0:T(2,128)S(1)}, s32[2,32]{1,0:T(2,128)}, u32[]{:S(2)}) copy-start(s32[2,32]{1,0:T(2,128)} %param.12) | copy-start | bytes 772
  72.2 11.1 %copy-start.1 = (f32[2,32,384]{2,1,0:T(8,128)S(1)}, f32[2,32,384]{2,1,0:T(8,128)}, u32[]{:S(2)}) copy-start(f32[2,32,384]{2,1,0:T(8,128)} %param.11) | copy-start | bytes 294916
  72.2 11.1 %copy-start.2 = (f32[2,32,384]{2,1,0:T(8,128)S(1)}, f32[2,32,384]{2,1,0:T(8,128)}, u32[]{:S(2)}) copy-start(f32[2,32,384]{2,1,0:T(8,128)} %param.10) | copy-start | bytes 294916
  72.2 66.3 %all-to-all-start = ((bf16[32,96,384]{2,1,0:T(8,128)(2,1)}), bf16[32,96,384]{2,1,0:T(8,128)(2,1)S(1)}, u32[]{:S(2)}, u32[]{:S(2)}) async-start(bf16[32,96,384]{2,1,0:T(8,128)(2,1)} %bitcast.74), calls=%async_computation | async-start | bytes 4718592 | tf_op jit(solution)/shard_map/all_to_all | solution.py:58
  147.8 2.8 %copy-start = (f32[1024,512]{1,0:T(8,128)S(1)}, f32[1024,512]{1,0:T(8,128)}, u32[]{:S(2)}) copy-start(f32[1024,512]{1,0:T(8,128)} %param.7) | copy-start | bytes 6291460
Sparse Core Ops, SparseCore 0:
  9.5 76.4 all-gather.2

commit v8 on v7

--- a/solution.py
+++ b/solution.py
@@ -10,7 +10,7 @@
 
 
 def ring_gather(block, n_outer, n_inner, outer):
-    n = n_outer if outer else n_inner
+    n_all = n_outer * n_inner
 
     def target(r, step):
         a, b = divmod(r, n_inner)
@@ -18,15 +18,20 @@
             return ((a + step) % n_outer) * n_inner + b
         return a * n_inner + (b + step) % n_inner
 
-    pieces = [block]
-    for d in range(1, n):
-        perm = [(r, target(r, -d)) for r in range(n_outer * n_inner)]
-        pieces.append(lax.ppermute(block, "row", perm))
-    return jnp.stack(pieces)
+    def shift(value, step):
+        return lax.ppermute(value, "row", [(r, target(r, step)) for r in range(n_all)])
+
+    from_behind = shift(block, 1)
+    from_ahead = shift(block, -1)
+    half = block.shape[-2] // 2
+    far = jnp.concatenate(
+        [shift(from_behind[..., :half, :], 1), shift(from_ahead[..., half:, :], -1)], axis=-2
+    )
+    return jnp.stack([block, from_ahead, far, from_behind])
 
 
 def replicate_over_row(block, n_row):
-    n_x = 4 if n_row % 4 == 0 else n_row
+    n_x = 4
     n_z = n_row // n_x
     row = lax.axis_index("row")
     z, x = row // n_x, row % n_x

time: 160 us -> 157 us (0.981)
  waiting for transfers between devices: 85.1 us -> 72.1 us
  starting transfers between devices: 40.7 us -> 49.8 us
    ppermute x6 -> x8, waiting for transfers between devices: 30 us -> 16.8 us  [shift(): lax.ppermute(value, 'row', [(r, target(r, step)) for r in range(n_all)])]
    ppermute x6 -> x8, starting transfers between devices: 30 us -> 36.9 us  [shift(): lax.ppermute(value, 'row', [(r, target(r, step)) for r in range(n_all)])]
    all_to_all x1, starting transfers between devices: 10.7 us -> 12.9 us  [local(): col_all = lax.all_to_all(every_tile, 'col', 0, 0, tiled=True)]
  transfers between devices with their start and end apart: 8 -> 10, of which waited for: 5 -> 7; matrix products, arithmetic and copies ran while one was open for 6% -> 6% of each run, Pallas kernels for 0% -> 0%
where the time goes in v8:
time: 157 us; the launch traced here: 156 us
  waiting for transfers between devices  72.1 us (46%)
  starting transfers between devices  49.8 us (32%)
  between operations  13.8 us (9%)
  matrix products  9.31 us (6%)
  local copies, waits for them, and re-layouts  6.33 us (4%)
  other arithmetic  4.57 us (3%)
    all_to_all x1, waiting for transfers between devices, local(): col_all = lax.all_to_all(every_tile, 'col', 0, 0, tiled=True)  55.3 us
    ppermute x8, starting transfers between devices, shift(): lax.ppermute(value, 'row', [(r, target(r, step)) for r in range(n_all)])  36.9 us
    ppermute x8, waiting for transfers between devices, shift(): lax.ppermute(value, 'row', [(r, target(r, step)) for r in range(n_all)])  16.8 us
    all_to_all x1, starting transfers between devices, local(): col_all = lax.all_to_all(every_tile, 'col', 0, 0, tiled=True)  12.9 us
    dot_general x1, matrix products, local(): jnp.einsum('cikbr,ckbq->kirq', row_v, col_scaled, preferred_element_type=...  4.2 us
  transfers between devices with their start and end apart: 10, of which 7 were waited for; matrix products, arithmetic and copies ran while one was open for 6% of the time, Pallas kernels for 0%

profile of v8, /device:TPU:1, one launch (start us, length us, event | category | flops | bytes accessed | tf_op | source)
XLA Modules:
  0.0 156.0 jit_solution(15520235316791885213)
XLA Ops:
  6.5 0.0 all-gather.3.cloned.1.call-start
  6.5 1.6 %fusion.19 = (bf16[2,2,48,384]{3,2,0,1:T(8,128)(2,1)S(1)}, bf16[2,2,48,384]{3,2,1,0:T(8,128)(2,1)}) fusion(bf16[2,2,32,384]{3,2,1,0:T(8,128)(2,1)} %param.9, bf16[2,2,16,384]{3,2,1,0:T(8,128)(2,1)} %param.8), kind=kLoop, calls=%fused_computation.57 | loop fusion | flops 294912 | bytes 442368 | tf_op jit(solution)/shard_map/concatenate | solution.py:53
  8.1 0.0 all-gather.3.cloned.1.call-update
  8.1 6.6 %collective-permute-start.1 = (bf16[192,384]{1,0:T(8,128)(2,1)S(1)}, bf16[192,384]{1,0:T(8,128)(2,1)S(1)}, u32[]{:S(2)}, u32[]{:S(2)}) collective-permute-start(bf16[192,384]{1,0:T(8,128)(2,1)S(1)} %bitcast.81), channel_id=1, source_target_pairs={{0,128},{32,160},{64,192},{96,224},{128,256},{160,288},{192,320},{... | collective-permute-start | bytes 442376 | tf_op jit(solution)/shard_map/ppermute | solution.py:22
  14.8 6.8 %collective-permute-start = (bf16[192,384]{1,0:T(8,128)(2,1)S(1)}, bf16[192,384]{1,0:T(8,128)(2,1)S(1)}, u32[]{:S(2)}, u32[]{:S(2)}) collective-permute-start(bf16[192,384]{1,0:T(8,128)(2,1)S(1)} %bitcast.82), channel_id=1, source_target_pairs={{0,384},{32,416},{64,448},{96,480},{128,0},{160,32},{192,64},{224,... | collective-permute-start | bytes 442376 | tf_op jit(solution)/shard_map/ppermute | solution.py:22
  21.6 1.1 collective-permute-done.1
  22.7 4.0 %collective-permute-start.2 = (bf16[96,384]{1,0:T(8,128)(2,1)S(1)}, bf16[96,384]{1,0:T(8,128)(2,1)S(1)}, u32[]{:S(2)}, u32[]{:S(2)}) collective-permute-start(bf16[96,384]{1,0:T(8,128)(2,1)S(1)} %slice.89), channel_id=1, source_target_pairs={{0,128},{32,160},{64,192},{96,224},{128,256},{160,288},{192,320},{... | collective-permute-start | bytes 221192 | tf_op jit(solution)/shard_map/ppermute | solution.py:22
  26.7 1.0 collective-permute-done
  27.7 5.1 %collective-permute-start.3 = (bf16[96,384]{1,0:T(8,128)(2,1)S(1)}, bf16[96,384]{1,0:T(8,128)(2,1)S(1)}, u32[]{:S(2)}, u32[]{:S(2)}) collective-permute-start(bf16[96,384]{1,0:T(8,128)(2,1)S(1)} %slice.90), channel_id=1, source_target_pairs={{0,384},{32,416},{64,448},{96,480},{128,0},{160,32},{192,64},{224,... | collective-permute-start | bytes 221192 | tf_op jit(solution)/shard_map/ppermute | solution.py:22
  32.7 0.0 collective-permute-done.2
  32.8 1.9 %collective-permute-done.3 = bf16[96,384]{1,0:T(8,128)(2,1)S(1)} collective-permute-done((bf16[96,384]{1,0:T(8,128)(2,1)S(1)}, bf16[96,384]{1,0:T(8,128)(2,1)S(1)}, u32[]{:S(2)}, u32[]{:S(2)}) %collective-permute-start.3) | collective-permute-done | bytes 73760 | tf_op jit(solution)/shard_map/ppermute | solution.py:22
  34.7 0.1 pad_maximum_fusion.1
  34.8 4.8 %collective-permute-start.5 = (bf16[4,192,384]{2,1,0:T(8,128)(2,1)S(1)}, bf16[4,192,384]{2,1,0:T(8,128)(2,1)S(1)}, u32[]{:S(2)}, u32[]{:S(2)}) collective-permute-start(bf16[4,192,384]{2,1,0:T(8,128)(2,1)S(1)} %pad_maximum_fusion.1), channel_id=1, source_target_pairs={{0,32},{32,64},{64,96},{96,0},{128,160},{160,192},{192,224},{224,1... | collective-permute-start | bytes 1769480 | tf_op jit(solution)/shard_map/ppermute | solution.py:22
  39.6 3.2 %collective-permute-start.4 = (bf16[4,192,384]{2,1,0:T(8,128)(2,1)S(1)}, bf16[4,192,384]{2,1,0:T(8,128)(2,1)S(1)}, u32[]{:S(2)}, u32[]{:S(2)}) collective-permute-start(bf16[4,192,384]{2,1,0:T(8,128)(2,1)S(1)} %pad_maximum_fusion.1), channel_id=1, source_target_pairs={{0,96},{32,0},{64,32},{96,64},{128,224},{160,128},{192,160},{224,1... | collective-permute-start | bytes 1769480 | tf_op jit(solution)/shard_map/ppermute | solution.py:22
  42.8 9.3 %collective-permute-done.5 = bf16[4,192,384]{2,1,0:T(8,128)(2,1)S(1)} collective-permute-done((bf16[4,192,384]{2,1,0:T(8,128)(2,1)S(1)}, bf16[4,192,384]{2,1,0:T(8,128)(2,1)S(1)}, u32[]{:S(2)}, u32[]{:S(2)}) %collective-permute-start.5) | collective-permute-done | bytes 589856 | tf_op jit(solution)/shard_map/ppermute | solution.py:22
  52.2 1.9 %collective-permute-start.6 = (bf16[4,96,384]{2,1,0:T(8,128)(2,1)S(1)}, bf16[4,96,384]{2,1,0:T(8,128)(2,1)S(1)}, u32[]{:S(2)}, u32[]{:S(2)}) collective-permute-start(bf16[4,96,384]{2,1,0:T(8,128)(2,1)S(1)} %slice.91), channel_id=1, source_target_pairs={{0,32},{32,64},{64,96},{96,0},{128,160},{160,192},{192,224},{224,1... | collective-permute-start | bytes 884744 | tf_op jit(solution)/shard_map/ppermute | solution.py:22
  54.1 0.0 collective-permute-done.4
  54.1 4.6 %collective-permute-start.7 = (bf16[4,96,384]{2,1,0:T(8,128)(2,1)S(1)}, bf16[4,96,384]{2,1,0:T(8,128)(2,1)S(1)}, u32[]{:S(2)}, u32[]{:S(2)}) collective-permute-start(bf16[4,96,384]{2,1,0:T(8,128)(2,1)S(1)} %slice.92), channel_id=1, source_target_pairs={{0,96},{32,0},{64,32},{96,64},{128,224},{160,128},{192,160},{224,1... | collective-permute-start | bytes 884744 | tf_op jit(solution)/shard_map/ppermute | solution.py:22
  58.7 0.1 bitcast_dynamic-update-slice_fusion.4
  58.8 0.1 bitcast_dynamic-update-slice_fusion.2
  58.9 1.9 %collective-permute-done.6 = bf16[4,96,384]{2,1,0:T(8,128)(2,1)S(1)} collective-permute-done((bf16[4,96,384]{2,1,0:T(8,128)(2,1)S(1)}, bf16[4,96,384]{2,1,0:T(8,128)(2,1)S(1)}, u32[]{:S(2)}, u32[]{:S(2)}) %collective-permute-start.6) | collective-permute-done | bytes 294944 | tf_op jit(solution)/shard_map/ppermute | solution.py:22
  60.8 1.5 collective-permute-done.7
  62.4 0.1 fusion.14
  62.5 0.1 bitcast_dynamic-update-slice_fusion
  62.6 0.1 bitcast_dynamic-update-slice_fusion.5
  62.7 0.1 bitcast_dynamic-update-slice_fusion.3
  62.8 0.1 fusion.15
  62.9 0.1 bitcast_dynamic-update-slice_fusion.1
  63.0 0.3 constant_dynamic-slice_fusion
  63.3 1.0 fusion.3
  64.3 1.7 %copy.43 = bf16[4,4,192,384]{3,2,1,0:T(8,128)(2,1)} copy(bf16[4,4,192,384]{3,2,0,1:T(8,128)(2,1)S(1)} %fusion.3) | data formatting | bytes 4718592 | tf_op jit(solution)/shard_map/transpose | solution.py:40
  66.0 12.9 %all-to-all-start = ((bf16[32,96,384]{2,1,0:T(8,128)(2,1)}), bf16[32,96,384]{2,1,0:T(8,128)(2,1)S(1)}, u32[]{:S(2)}, u32[]{:S(2)}) async-start(bf16[32,96,384]{2,1,0:T(8,128)(2,1)} %bitcast.78), calls=%async_computation | async-start | bytes 4718592 | tf_op jit(solution)/shard_map/all_to_all | solution.py:63
  79.0 0.1 reshape.90
  79.3 0.1 multiply_select_fusion
  79.4 55.3 %all-to-all-done = bf16[32,96,384]{2,1,0:T(8,128)(2,1)S(1)} async-done(((bf16[32,96,384]{2,1,0:T(8,128)(2,1)}), bf16[32,96,384]{2,1,0:T(8,128)(2,1)S(1)}, u32[]{:S(2)}, u32[]{:S(2)}) %all-to-all-start) | async-done | bytes 2359328 | tf_op jit(solution)/shard_map/all_to_all | solution.py:63
  134.7 0.3 slice.93
  135.0 0.9 copy.44
  135.9 0.2 fusion.18
  136.1 1.3 fusion.7
  137.4 0.2 pad_maximum_fusion
  137.6 2.1 %copy.50 = bf16[32,2,16,2,384]{4,0,3,2,1:T(8,128)(2,1)} copy(bf16[32,2,16,2,384]{4,2,3,1,0:T(8,128)(2,1)S(1)} %pad_maximum_fusion) | data formatting | bytes 3145728 | tf_op jit(solution)/shard_map/stack | solution.py:81
  139.7 0.1 slice_bitcast_fusion
  139.7 0.1 copy.53
  139.8 0.0 all-gather.3.cloned.1.call-done
  139.9 4.2 %fusion = f32[2,2,384,384,1]{3,2,1,0,4:T(8,128)S(1)} fusion(bf16[32,2,32,384,1]{3,0,2,1,4:T(8,128)(2,1)} %bitcast.92, bf16[32,2,2,48,384]{4,3,2,1,0:T(8,128)(2,1)} %bitcast.96), kind=kOutput, calls=%fused_computation.2 | convolution fusion | flops 1207959552 | bytes 7077888 | tf_op jit(solution)/shard_map/cikbr,ckbq->kirq/dot_general | solution.py:83
  144.1 0.0 copy-start
  144.1 2.8 %convolution_convert_fusion = bf16[2,2,32,16,384]{4,3,2,1,0:T(8,128)(2,1)S(1)} fusion(bf16[32,2,2,48,384]{4,3,2,1,0:T(8,128)(2,1)} %bitcast.97, f32[2,2,384,384,1]{3,2,1,0,4:T(8,128)S(1)} %fusion, f32[2,384]{1,0:T(2,128)S(1)} %bitcast.95, f32[2,2,384]{2,0,1:T(2,128)S(1)} %copy.41), kind=kOutput, calls=%fused_computation.14 | convolution fusion | flops 606535680 | bytes 5514240 | tf_op jit(solution)/shard_map/cikmr,kirq->kicmq/dot_general | solution.py:85
  146.9 2.3 %bitcast_subtract_fusion = f32[1024,512]{1,0:T(8,128)} fusion(f32[1024,512]{1,0:T(8,128)S(1)} %copy-done, bf16[1024,2,384]{2,0,1:T(8,128)(2,1)S(1)} %bitcast.93, bf16[2,512,384]{2,1,0:T(8,128)(2,1)S(1)} %bitcast.80), kind=kOutput, calls=%fused_computation.9 | convolution fusion | flops 805830656 | bytes 6553600 | tf_op jit(solution)/shard_map/kicmq,knq->icmn/dot_general | solution.py:87
  (24 shorter events, 0.3 us)
Async XLA Ops:
  6.5 133.3 %all-gather.3.cloned.1.call-start = ((), (), s32[]{:S(2)}) async-start(), calls=%async_computation.1 | async-start | bytes 4866048 | tf_op jit(solution)/shard_map/all_gather | solution.py:55
  8.1 14.5 %collective-permute-start.1 = (bf16[192,384]{1,0:T(8,128)(2,1)S(1)}, bf16[192,384]{1,0:T(8,128)(2,1)S(1)}, u32[]{:S(2)}, u32[]{:S(2)}) collective-permute-start(bf16[192,384]{1,0:T(8,128)(2,1)S(1)} %bitcast.81), channel_id=1, source_target_pairs={{0,128},{32,160},{64,192},{96,224},{128,256},{160,288},{192,320},{... | collective-permute-start | bytes 442376 | tf_op jit(solution)/shard_map/ppermute | solution.py:22
  14.8 12.9 %collective-permute-start = (bf16[192,384]{1,0:T(8,128)(2,1)S(1)}, bf16[192,384]{1,0:T(8,128)(2,1)S(1)}, u32[]{:S(2)}, u32[]{:S(2)}) collective-permute-start(bf16[192,384]{1,0:T(8,128)(2,1)S(1)} %bitcast.82), channel_id=1, source_target_pairs={{0,384},{32,416},{64,448},{96,480},{128,0},{160,32},{192,64},{224,... | collective-permute-start | bytes 442376 | tf_op jit(solution)/shard_map/ppermute | solution.py:22
  22.7 10.1 %collective-permute-start.2 = (bf16[96,384]{1,0:T(8,128)(2,1)S(1)}, bf16[96,384]{1,0:T(8,128)(2,1)S(1)}, u32[]{:S(2)}, u32[]{:S(2)}) collective-permute-start(bf16[96,384]{1,0:T(8,128)(2,1)S(1)} %slice.89), channel_id=1, source_target_pairs={{0,128},{32,160},{64,192},{96,224},{128,256},{160,288},{192,320},{... | collective-permute-start | bytes 221192 | tf_op jit(solution)/shard_map/ppermute | solution.py:22
  27.7 7.0 %collective-permute-start.3 = (bf16[96,384]{1,0:T(8,128)(2,1)S(1)}, bf16[96,384]{1,0:T(8,128)(2,1)S(1)}, u32[]{:S(2)}, u32[]{:S(2)}) collective-permute-start(bf16[96,384]{1,0:T(8,128)(2,1)S(1)} %slice.90), channel_id=1, source_target_pairs={{0,384},{32,416},{64,448},{96,480},{128,0},{160,32},{192,64},{224,... | collective-permute-start | bytes 221192 | tf_op jit(solution)/shard_map/ppermute | solution.py:22
  34.8 17.3 %collective-permute-start.5 = (bf16[4,192,384]{2,1,0:T(8,128)(2,1)S(1)}, bf16[4,192,384]{2,1,0:T(8,128)(2,1)S(1)}, u32[]{:S(2)}, u32[]{:S(2)}) collective-permute-start(bf16[4,192,384]{2,1,0:T(8,128)(2,1)S(1)} %pad_maximum_fusion.1), channel_id=1, source_target_pairs={{0,32},{32,64},{64,96},{96,0},{128,160},{160,192},{192,224},{224,1... | collective-permute-start | bytes 1769480 | tf_op jit(solution)/shard_map/ppermute | solution.py:22
  39.6 14.5 %collective-permute-start.4 = (bf16[4,192,384]{2,1,0:T(8,128)(2,1)S(1)}, bf16[4,192,384]{2,1,0:T(8,128)(2,1)S(1)}, u32[]{:S(2)}, u32[]{:S(2)}) collective-permute-start(bf16[4,192,384]{2,1,0:T(8,128)(2,1)S(1)} %pad_maximum_fusion.1), channel_id=1, source_target_pairs={{0,96},{32,0},{64,32},{96,64},{128,224},{160,128},{192,160},{224,1... | collective-permute-start | bytes 1769480 | tf_op jit(solution)/shard_map/ppermute | solution.py:22
  52.2 8.7 %collective-permute-start.6 = (bf16[4,96,384]{2,1,0:T(8,128)(2,1)S(1)}, bf16[4,96,384]{2,1,0:T(8,128)(2,1)S(1)}, u32[]{:S(2)}, u32[]{:S(2)}) collective-permute-start(bf16[4,96,384]{2,1,0:T(8,128)(2,1)S(1)} %slice.91), channel_id=1, source_target_pairs={{0,32},{32,64},{64,96},{96,0},{128,160},{160,192},{192,224},{224,1... | collective-permute-start | bytes 884744 | tf_op jit(solution)/shard_map/ppermute | solution.py:22
  54.1 8.2 %collective-permute-start.7 = (bf16[4,96,384]{2,1,0:T(8,128)(2,1)S(1)}, bf16[4,96,384]{2,1,0:T(8,128)(2,1)S(1)}, u32[]{:S(2)}, u32[]{:S(2)}) collective-permute-start(bf16[4,96,384]{2,1,0:T(8,128)(2,1)S(1)} %slice.92), channel_id=1, source_target_pairs={{0,96},{32,0},{64,32},{96,64},{128,224},{160,128},{192,160},{224,1... | collective-permute-start | bytes 884744 | tf_op jit(solution)/shard_map/ppermute | solution.py:22
  66.0 13.0 %copy-start.3 = (f32[2,2,2,512]{3,2,1,0:T(2,128)S(1)}, f32[2,2,2,512]{3,2,1,0:T(2,128)}, u32[]{:S(2)}) copy-start(f32[2,2,2,512]{3,2,1,0:T(2,128)} %param.13) | copy-start | bytes 49156
  66.0 13.2 %copy-start.4 = (s32[2,32]{1,0:T(2,128)S(1)}, s32[2,32]{1,0:T(2,128)}, u32[]{:S(2)}) copy-start(s32[2,32]{1,0:T(2,128)} %param.12) | copy-start | bytes 772
  66.0 13.3 %copy-start.1 = (f32[2,32,384]{2,1,0:T(8,128)S(1)}, f32[2,32,384]{2,1,0:T(8,128)}, u32[]{:S(2)}) copy-start(f32[2,32,384]{2,1,0:T(8,128)} %param.11) | copy-start | bytes 294916
  66.0 13.3 %copy-start.2 = (f32[2,32,384]{2,1,0:T(8,128)S(1)}, f32[2,32,384]{2,1,0:T(8,128)}, u32[]{:S(2)}) copy-start(f32[2,32,384]{2,1,0:T(8,128)} %param.10) | copy-start | bytes 294916
  66.0 68.7 %all-to-all-start = ((bf16[32,96,384]{2,1,0:T(8,128)(2,1)}), bf16[32,96,384]{2,1,0:T(8,128)(2,1)S(1)}, u32[]{:S(2)}, u32[]{:S(2)}) async-start(bf16[32,96,384]{2,1,0:T(8,128)(2,1)} %bitcast.78), calls=%async_computation | async-start | bytes 4718592 | tf_op jit(solution)/shard_map/all_to_all | solution.py:63
  144.1 2.8 %copy-start = (f32[1024,512]{1,0:T(8,128)S(1)}, f32[1024,512]{1,0:T(8,128)}, u32[]{:S(2)}) copy-start(f32[1024,512]{1,0:T(8,128)} %param.7) | copy-start | bytes 6291460
Sparse Core Ops, SparseCore 0:
  9.5 76.9 all-gather.2

commit v9 on v8

--- a/solution.py
+++ b/solution.py
@@ -9,7 +9,7 @@
     return jnp.where(position < ranks_k[:, None], u_scale_k * v_scale_k, jnp.float32(0.0))
 
 
-def ring_gather(block, n_outer, n_inner, outer):
+def ring_gather(block, n_outer, n_inner, outer, forward=True):
     n_all = n_outer * n_inner
 
     def target(r, step):
@@ -21,6 +21,8 @@
     def shift(value, step):
         return lax.ppermute(value, "row", [(r, target(r, step)) for r in range(n_all)])
 
+    if not forward:
+        return jnp.stack([block] + [shift(block, -d) for d in range(1, 4)])
     from_behind = shift(block, 1)
     from_ahead = shift(block, -1)
     half = block.shape[-2] // 2
@@ -35,7 +37,7 @@
     n_z = n_row // n_x
     row = lax.axis_index("row")
     z, x = row // n_x, row % n_x
-    by_z = ring_gather(block, n_z, n_x, outer=True)
+    by_z = ring_gather(block, n_z, n_x, outer=True, forward=False)
     by_xz = ring_gather(by_z, n_z, n_x, outer=False)
     by_zx = jnp.roll(jnp.roll(by_xz, x, axis=0), z, axis=1).swapaxes(0, 1)
     return by_zx.reshape((n_row,) + block.shape)
@@ -56,8 +58,19 @@
     row_u = row_all[:, :, :, :u_rows]
     row_v = row_all[:, :, :, u_rows:]
 
+    half = v_rows // 2
+    d_own = lax.dynamic_slice_in_dim(d_inverse, column * half, half, 3)
+    d_own = d_own.transpose(1, 2, 0, 3)[:, :, :, None, :, None]
+    pairs = v_codes.reshape(panels, per_row, half, 2, rank_most)
+    even = pairs[..., 0, :].astype(jnp.float32)
+    odd = pairs[..., 1, :].astype(jnp.float32)
+    first = d_own[0, 0] * even + d_own[0, 1] * odd
+    second = d_own[1, 0] * even + d_own[1, 1] * odd
+    v_scaled = jnp.stack([first, second], axis=-2).reshape(v_codes.shape).astype(jnp.bfloat16)
+    col_shard = jnp.concatenate([u_codes, v_scaled], axis=2).transpose(1, 0, 2, 3)
+
     n_row = lax.axis_size("row")
-    flat = shard.reshape(per_row * panels * both, rank_most)
+    flat = col_shard.reshape(per_row * panels * both, rank_most)
     every_tile = replicate_over_row(flat, n_row)
     every_tile = every_tile.reshape(n_row * per_row, panels * both, rank_most)
     col_all = lax.all_to_all(every_tile, "col", 0, 0, tiled=True)
@@ -71,15 +84,7 @@
     row_weight = lax.dynamic_slice_in_dim(weight, first_tile, per_row, 1)
     col_weight = lax.dynamic_index_in_dim(weight, column, 1, keepdims=False)
 
-    half = v_rows // 2
-    d_blocks = d_inverse.reshape(panels, 2, 2, n_col, half).transpose(1, 2, 3, 0, 4)[..., None]
-    pairs = col_v.reshape(n_col, panels, half, 2, rank_most)
-    even = pairs[..., 0, :].astype(jnp.float32)
-    odd = pairs[..., 1, :].astype(jnp.float32)
-    first = d_blocks[0, 0] * even + d_blocks[0, 1] * odd
-    second = d_blocks[1, 0] * even + d_blocks[1, 1] * odd
-    col_scaled = jnp.stack([first, second], axis=-2).reshape(col_v.shape).astype(jnp.bfloat16)
-
+    col_scaled = col_v
     inner = jnp.einsum("cikbr,ckbq->kirq", row_v, col_scaled, preferred_element_type=jnp.float32)
     core = (row_weight[:, :, :, None] * inner * col_weight[:, None, None, :]).astype(jnp.bfloat16)
     left = jnp.einsum("cikmr,kirq->kicmq", row_u, core, preferred_element_type=jnp.float32)

time: 157 us -> 156 us (level)
  waiting for transfers between devices: 72.1 us -> 79.3 us
  starting transfers between devices: 49.8 us -> 44.8 us
  local copies, waits for them, and re-layouts: 6.33 us -> 4.7 us
    ppermute x8 -> x7, waiting for transfers between devices: 16.8 us -> 24 us  [shift(): lax.ppermute(value, 'row', [(r, target(r, step)) for r in range(n_all)])]
    ppermute x8 -> x7, starting transfers between devices: 36.9 us -> 30.6 us  [shift(): lax.ppermute(value, 'row', [(r, target(r, step)) for r in range(n_all)])]
    another operation x1, local copies, waits for them, and re-layouts: 2.06 us -> 0.08 us  [local(): jnp.stack([first, second], axis=-2).reshape(v_codes.shape)]
    unnamed x14 -> x16, local copies, waits for them, and re-layouts: 0.32 us -> 2.14 us
    transpose x0 -> x2, other arithmetic: none -> 1.78 us  [the longest x1 1.58 us: local(): shard = jnp.concatenate([u_codes, v_codes], axis=2).transpose(1, 0, 2, 3)]
    concatenate x1 -> x0, other arithmetic: 1.57 us -> none  [local(): shard = jnp.concatenate([u_codes, v_codes], axis=2).transpose(1, 0, 2, 3)]
  transfers between devices with their start and end apart: 10 -> 9, of which waited for: 7 -> 7; matrix products, arithmetic and copies ran while one was open for 6% -> 4% of each run, Pallas kernels for 0% -> 0%
where the time goes in v9:
time: 156 us; the launch traced here: 155 us
  waiting for transfers between devices  79.3 us (51%)
  starting transfers between devices  44.8 us (29%)
  between operations  13.8 us (9%)
  matrix products  8.85 us (6%)
  local copies, waits for them, and re-layouts  4.7 us (3%)
  other arithmetic  3.43 us (2%)
    all_to_all x1, waiting for transfers between devices, local(): col_all = lax.all_to_all(every_tile, 'col', 0, 0, tiled=True)  55.3 us
    ppermute x7, starting transfers between devices, shift(): lax.ppermute(value, 'row', [(r, target(r, step)) for r in range(n_all)])  30.6 us
    ppermute x7, waiting for transfers between devices, shift(): lax.ppermute(value, 'row', [(r, target(r, step)) for r in range(n_all)])  24 us
    all_to_all x1, starting transfers between devices, local(): col_all = lax.all_to_all(every_tile, 'col', 0, 0, tiled=True)  14.1 us
    dot_general x1, matrix products, local(): jnp.einsum('cikbr,ckbq->kirq', row_v, col_scaled, preferred_element_type=...  3.75 us
  transfers between devices with their start and end apart: 9, of which 7 were waited for; matrix products, arithmetic and copies ran while one was open for 4% of the time, Pallas kernels for 0%

profile of v9, /device:TPU:1, one launch (start us, length us, event | category | flops | bytes accessed | tf_op | source)
XLA Modules:
  0.0 154.9 jit_solution(10371598149043878195)
XLA Ops:
  6.5 0.0 copy-start
  6.5 0.0 all-gather.3.cloned.1.call-start
  6.5 1.6 %copy_bitcast_fusion = bf16[2,2,48,384]{3,2,1,0:T(8,128)(2,1)} fusion(bf16[2,2,32,384]{3,2,1,0:T(8,128)(2,1)} %param.9, bf16[2,2,16,384]{3,2,1,0:T(8,128)(2,1)} %param.8), kind=kLoop, calls=%fused_computation.28 | loop fusion | flops 294912 | bytes 294912 | tf_op jit(solution)/shard_map/transpose | solution.py:55
  8.1 0.0 all-gather.3.cloned.1.call-update
  8.1 1.0 copy.42
  9.1 0.8 copy.46
  10.0 0.0 copy-done
  10.0 0.1 dynamic-slice_bitcast_fusion
  10.1 0.1 fusion.17
  10.1 0.1 fusion.12
  10.3 0.1 copy.45
  10.4 0.2 maximum_bitcast_fusion.1
  10.6 11.5 %collective-permute-start = (bf16[192,384]{1,0:T(8,128)(2,1)S(1)}, bf16[192,384]{1,0:T(8,128)(2,1)S(1)}, u32[]{:S(2)}, u32[]{:S(2)}) collective-permute-start(bf16[192,384]{1,0:T(8,128)(2,1)S(1)} %bitcast.83), channel_id=1, source_target_pairs={{0,384},{32,416},{64,448},{96,480},{128,0},{160,32},{192,64},{224,... | collective-permute-start | bytes 442376 | tf_op jit(solution)/shard_map/ppermute | solution.py:22
  22.1 1.9 %collective-permute-start.1 = (bf16[192,384]{1,0:T(8,128)(2,1)S(1)}, bf16[192,384]{1,0:T(8,128)(2,1)S(1)}, u32[]{:S(2)}, u32[]{:S(2)}) collective-permute-start(bf16[192,384]{1,0:T(8,128)(2,1)S(1)} %bitcast.84), channel_id=1, source_target_pairs={{0,256},{32,288},{64,320},{96,352},{128,384},{160,416},{192,448},{... | collective-permute-start | bytes 442376 | tf_op jit(solution)/shard_map/ppermute | solution.py:22
  24.0 4.2 %collective-permute-start.2 = (bf16[192,384]{1,0:T(8,128)(2,1)S(1)}, bf16[192,384]{1,0:T(8,128)(2,1)S(1)}, u32[]{:S(2)}, u32[]{:S(2)}) collective-permute-start(bf16[192,384]{1,0:T(8,128)(2,1)S(1)} %bitcast.85), channel_id=1, source_target_pairs={{0,128},{32,160},{64,192},{96,224},{128,256},{160,288},{192,320},{... | collective-permute-start | bytes 442376 | tf_op jit(solution)/shard_map/ppermute | solution.py:22
  28.3 4.5 %collective-permute-done = bf16[192,384]{1,0:T(8,128)(2,1)S(1)} collective-permute-done((bf16[192,384]{1,0:T(8,128)(2,1)S(1)}, bf16[192,384]{1,0:T(8,128)(2,1)S(1)}, u32[]{:S(2)}, u32[]{:S(2)}) %collective-permute-start) | collective-permute-done | bytes 147488 | tf_op jit(solution)/shard_map/ppermute | solution.py:22
  32.7 5.7 %collective-permute-done.1 = bf16[192,384]{1,0:T(8,128)(2,1)S(1)} collective-permute-done((bf16[192,384]{1,0:T(8,128)(2,1)S(1)}, bf16[192,384]{1,0:T(8,128)(2,1)S(1)}, u32[]{:S(2)}, u32[]{:S(2)}) %collective-permute-start.1) | collective-permute-done | bytes 147488 | tf_op jit(solution)/shard_map/ppermute | solution.py:22
  38.5 1.3 collective-permute-done.2
  39.7 0.1 pad_maximum_fusion
  39.8 2.7 %collective-permute-start.4 = (bf16[4,192,384]{2,1,0:T(8,128)(2,1)S(1)}, bf16[4,192,384]{2,1,0:T(8,128)(2,1)S(1)}, u32[]{:S(2)}, u32[]{:S(2)}) collective-permute-start(bf16[4,192,384]{2,1,0:T(8,128)(2,1)S(1)} %pad_maximum_fusion), channel_id=1, source_target_pairs={{0,32},{32,64},{64,96},{96,0},{128,160},{160,192},{192,224},{224,1... | collective-permute-start | bytes 1769480 | tf_op jit(solution)/shard_map/ppermute | solution.py:22
  42.5 3.8 %collective-permute-start.3 = (bf16[4,192,384]{2,1,0:T(8,128)(2,1)S(1)}, bf16[4,192,384]{2,1,0:T(8,128)(2,1)S(1)}, u32[]{:S(2)}, u32[]{:S(2)}) collective-permute-start(bf16[4,192,384]{2,1,0:T(8,128)(2,1)S(1)} %pad_maximum_fusion), channel_id=1, source_target_pairs={{0,96},{32,0},{64,32},{96,64},{128,224},{160,128},{192,160},{224,1... | collective-permute-start | bytes 1769480 | tf_op jit(solution)/shard_map/ppermute | solution.py:22
  46.4 8.6 %collective-permute-done.4 = bf16[4,192,384]{2,1,0:T(8,128)(2,1)S(1)} collective-permute-done((bf16[4,192,384]{2,1,0:T(8,128)(2,1)S(1)}, bf16[4,192,384]{2,1,0:T(8,128)(2,1)S(1)}, u32[]{:S(2)}, u32[]{:S(2)}) %collective-permute-start.4) | collective-permute-done | bytes 589856 | tf_op jit(solution)/shard_map/ppermute | solution.py:22
  55.0 2.7 %collective-permute-start.5 = (bf16[4,96,384]{2,1,0:T(8,128)(2,1)S(1)}, bf16[4,96,384]{2,1,0:T(8,128)(2,1)S(1)}, u32[]{:S(2)}, u32[]{:S(2)}) collective-permute-start(bf16[4,96,384]{2,1,0:T(8,128)(2,1)S(1)} %slice.86), channel_id=1, source_target_pairs={{0,32},{32,64},{64,96},{96,0},{128,160},{160,192},{192,224},{224,1... | collective-permute-start | bytes 884744 | tf_op jit(solution)/shard_map/ppermute | solution.py:22
  57.7 0.0 collective-permute-done.3
  57.7 3.8 %collective-permute-start.6 = (bf16[4,96,384]{2,1,0:T(8,128)(2,1)S(1)}, bf16[4,96,384]{2,1,0:T(8,128)(2,1)S(1)}, u32[]{:S(2)}, u32[]{:S(2)}) collective-permute-start(bf16[4,96,384]{2,1,0:T(8,128)(2,1)S(1)} %slice.87), channel_id=1, source_target_pairs={{0,96},{32,0},{64,32},{96,64},{128,224},{160,128},{192,160},{224,1... | collective-permute-start | bytes 884744 | tf_op jit(solution)/shard_map/ppermute | solution.py:22
  61.6 0.1 bitcast_dynamic-update-slice_fusion.4
  61.6 0.1 bitcast_dynamic-update-slice_fusion.2
  61.8 1.9 %collective-permute-done.5 = bf16[4,96,384]{2,1,0:T(8,128)(2,1)S(1)} collective-permute-done((bf16[4,96,384]{2,1,0:T(8,128)(2,1)S(1)}, bf16[4,96,384]{2,1,0:T(8,128)(2,1)S(1)}, u32[]{:S(2)}, u32[]{:S(2)}) %collective-permute-start.5) | collective-permute-done | bytes 294944 | tf_op jit(solution)/shard_map/ppermute | solution.py:22
  63.7 2.0 %collective-permute-done.6 = bf16[4,96,384]{2,1,0:T(8,128)(2,1)S(1)} collective-permute-done((bf16[4,96,384]{2,1,0:T(8,128)(2,1)S(1)}, bf16[4,96,384]{2,1,0:T(8,128)(2,1)S(1)}, u32[]{:S(2)}, u32[]{:S(2)}) %collective-permute-start.6) | collective-permute-done | bytes 294944 | tf_op jit(solution)/shard_map/ppermute | solution.py:22
  65.7 0.1 fusion.9
  65.8 0.1 bitcast_dynamic-update-slice_fusion
  65.9 0.1 bitcast_dynamic-update-slice_fusion.5
  66.0 0.1 bitcast_dynamic-update-slice_fusion.3
  66.1 0.1 fusion.10
  66.2 0.1 bitcast_dynamic-update-slice_fusion.1
  66.3 0.3 constant_dynamic-slice_fusion
  66.6 1.0 fusion.3
  67.6 1.7 %copy.49 = bf16[4,4,192,384]{3,2,1,0:T(8,128)(2,1)} copy(bf16[4,4,192,384]{3,2,0,1:T(8,128)(2,1)S(1)} %fusion.3) | data formatting | bytes 4718592 | tf_op jit(solution)/shard_map/transpose | solution.py:42
  69.3 14.1 %all-to-all-start = ((bf16[32,96,384]{2,1,0:T(8,128)(2,1)}), bf16[32,96,384]{2,1,0:T(8,128)(2,1)S(1)}, u32[]{:S(2)}, u32[]{:S(2)}) async-start(bf16[32,96,384]{2,1,0:T(8,128)(2,1)} %bitcast.23), calls=%async_computation | async-start | bytes 4718592 | tf_op jit(solution)/shard_map/all_to_all | solution.py:76
  83.5 0.1 multiply_select_fusion
  83.6 55.3 %all-to-all-done = bf16[32,96,384]{2,1,0:T(8,128)(2,1)S(1)} async-done(((bf16[32,96,384]{2,1,0:T(8,128)(2,1)}), bf16[32,96,384]{2,1,0:T(8,128)(2,1)S(1)}, u32[]{:S(2)}, u32[]{:S(2)}) %all-to-all-start) | async-done | bytes 2359328 | tf_op jit(solution)/shard_map/all_to_all | solution.py:76
  138.9 0.1 slice_bitcast_fusion.2
  139.0 0.1 copy.51
  139.1 0.0 all-gather.3.cloned.1.call-done
  139.1 3.7 %fusion = f32[2,2,384,384,1]{3,2,1,0,4:T(8,128)S(1)} fusion(bf16[32,2,48,384]{3,2,1,0:T(8,128)(2,1)S(1)} %bitcast.81, bf16[32,2,2,48,384]{4,3,2,1,0:T(8,128)(2,1)} %bitcast.103), kind=kOutput, calls=%fused_computation.2 | convolution fusion | flops 1207959552 | bytes 7077888 | tf_op jit(solution)/shard_map/cikbr,ckbq->kirq/dot_general | solution.py:88
  142.9 0.0 copy-start.1
  142.9 2.8 %convolution_convert_fusion = bf16[2,2,32,16,384]{4,3,2,1,0:T(8,128)(2,1)S(1)} fusion(bf16[32,2,2,48,384]{4,3,2,1,0:T(8,128)(2,1)} %bitcast.104, f32[2,2,384,384,1]{3,2,1,0,4:T(8,128)S(1)} %fusion, f32[2,384]{1,0:T(2,128)S(1)} %bitcast.102, f32[2,2,384]{2,0,1:T(2,128)S(1)} %copy.40), kind=kOutput, calls=%fused_computation.10 | convolution fusion | flops 606535680 | bytes 5514240 | tf_op jit(solution)/shard_map/cikmr,kirq->kicmq/dot_general | solution.py:90
  145.7 2.3 %bitcast_subtract_fusion = f32[1024,512]{1,0:T(8,128)} fusion(f32[1024,512]{1,0:T(8,128)S(1)} %copy-done.1, bf16[1024,2,384]{2,0,1:T(8,128)(2,1)S(1)} %bitcast.89, bf16[2,512,384]{2,1,0:T(8,128)(2,1)S(1)} %bitcast.82), kind=kOutput, calls=%fused_computation.9 | convolution fusion | flops 805830656 | bytes 6553600 | tf_op jit(solution)/shard_map/kicmq,knq->icmn/dot_general | solution.py:92
  (18 shorter events, 0.2 us)
Async XLA Ops:
  6.5 3.4 %copy-start = (f32[2,2,2,512]{3,2,1,0:T(2,128)S(1)}, f32[2,2,2,512]{3,2,1,0:T(2,128)}, u32[]{:S(2)}) copy-start(f32[2,2,2,512]{3,2,1,0:T(2,128)} %param.13) | copy-start | bytes 49156
  6.5 132.6 %all-gather.3.cloned.1.call-start = ((), (), s32[]{:S(2)}) async-start(), calls=%async_computation.1 | async-start | bytes 4866048 | tf_op jit(solution)/shard_map/all_gather | solution.py:57
  10.6 22.1 %collective-permute-start = (bf16[192,384]{1,0:T(8,128)(2,1)S(1)}, bf16[192,384]{1,0:T(8,128)(2,1)S(1)}, u32[]{:S(2)}, u32[]{:S(2)}) collective-permute-start(bf16[192,384]{1,0:T(8,128)(2,1)S(1)} %bitcast.83), channel_id=1, source_target_pairs={{0,384},{32,416},{64,448},{96,480},{128,0},{160,32},{192,64},{224,... | collective-permute-start | bytes 442376 | tf_op jit(solution)/shard_map/ppermute | solution.py:22
  22.1 16.4 %collective-permute-start.1 = (bf16[192,384]{1,0:T(8,128)(2,1)S(1)}, bf16[192,384]{1,0:T(8,128)(2,1)S(1)}, u32[]{:S(2)}, u32[]{:S(2)}) collective-permute-start(bf16[192,384]{1,0:T(8,128)(2,1)S(1)} %bitcast.84), channel_id=1, source_target_pairs={{0,256},{32,288},{64,320},{96,352},{128,384},{160,416},{192,448},{... | collective-permute-start | bytes 442376 | tf_op jit(solution)/shard_map/ppermute | solution.py:22
  24.0 15.7 %collective-permute-start.2 = (bf16[192,384]{1,0:T(8,128)(2,1)S(1)}, bf16[192,384]{1,0:T(8,128)(2,1)S(1)}, u32[]{:S(2)}, u32[]{:S(2)}) collective-permute-start(bf16[192,384]{1,0:T(8,128)(2,1)S(1)} %bitcast.85), channel_id=1, source_target_pairs={{0,128},{32,160},{64,192},{96,224},{128,256},{160,288},{192,320},{... | collective-permute-start | bytes 442376 | tf_op jit(solution)/shard_map/ppermute | solution.py:22
  39.8 15.2 %collective-permute-start.4 = (bf16[4,192,384]{2,1,0:T(8,128)(2,1)S(1)}, bf16[4,192,384]{2,1,0:T(8,128)(2,1)S(1)}, u32[]{:S(2)}, u32[]{:S(2)}) collective-permute-start(bf16[4,192,384]{2,1,0:T(8,128)(2,1)S(1)} %pad_maximum_fusion), channel_id=1, source_target_pairs={{0,32},{32,64},{64,96},{96,0},{128,160},{160,192},{192,224},{224,1... | collective-permute-start | bytes 1769480 | tf_op jit(solution)/shard_map/ppermute | solution.py:22
  42.5 15.2 %collective-permute-start.3 = (bf16[4,192,384]{2,1,0:T(8,128)(2,1)S(1)}, bf16[4,192,384]{2,1,0:T(8,128)(2,1)S(1)}, u32[]{:S(2)}, u32[]{:S(2)}) collective-permute-start(bf16[4,192,384]{2,1,0:T(8,128)(2,1)S(1)} %pad_maximum_fusion), channel_id=1, source_target_pairs={{0,96},{32,0},{64,32},{96,64},{128,224},{160,128},{192,160},{224,1... | collective-permute-start | bytes 1769480 | tf_op jit(solution)/shard_map/ppermute | solution.py:22
  55.0 8.7 %collective-permute-start.5 = (bf16[4,96,384]{2,1,0:T(8,128)(2,1)S(1)}, bf16[4,96,384]{2,1,0:T(8,128)(2,1)S(1)}, u32[]{:S(2)}, u32[]{:S(2)}) collective-permute-start(bf16[4,96,384]{2,1,0:T(8,128)(2,1)S(1)} %slice.86), channel_id=1, source_target_pairs={{0,32},{32,64},{64,96},{96,0},{128,160},{160,192},{192,224},{224,1... | collective-permute-start | bytes 884744 | tf_op jit(solution)/shard_map/ppermute | solution.py:22
  57.7 7.9 %collective-permute-start.6 = (bf16[4,96,384]{2,1,0:T(8,128)(2,1)S(1)}, bf16[4,96,384]{2,1,0:T(8,128)(2,1)S(1)}, u32[]{:S(2)}, u32[]{:S(2)}) collective-permute-start(bf16[4,96,384]{2,1,0:T(8,128)(2,1)S(1)} %slice.87), channel_id=1, source_target_pairs={{0,96},{32,0},{64,32},{96,64},{128,224},{160,128},{192,160},{224,1... | collective-permute-start | bytes 884744 | tf_op jit(solution)/shard_map/ppermute | solution.py:22
  69.3 14.1 %copy-start.4 = (s32[2,32]{1,0:T(2,128)S(1)}, s32[2,32]{1,0:T(2,128)}, u32[]{:S(2)}) copy-start(s32[2,32]{1,0:T(2,128)} %param.12) | copy-start | bytes 772
  69.3 14.2 %copy-start.2 = (f32[2,32,384]{2,1,0:T(8,128)S(1)}, f32[2,32,384]{2,1,0:T(8,128)}, u32[]{:S(2)}) copy-start(f32[2,32,384]{2,1,0:T(8,128)} %param.11) | copy-start | bytes 294916
  69.3 14.2 %copy-start.3 = (f32[2,32,384]{2,1,0:T(8,128)S(1)}, f32[2,32,384]{2,1,0:T(8,128)}, u32[]{:S(2)}) copy-start(f32[2,32,384]{2,1,0:T(8,128)} %param.10) | copy-start | bytes 294916
  69.3 69.6 %all-to-all-start = ((bf16[32,96,384]{2,1,0:T(8,128)(2,1)}), bf16[32,96,384]{2,1,0:T(8,128)(2,1)S(1)}, u32[]{:S(2)}, u32[]{:S(2)}) async-start(bf16[32,96,384]{2,1,0:T(8,128)(2,1)} %bitcast.23), calls=%async_computation | async-start | bytes 4718592 | tf_op jit(solution)/shard_map/all_to_all | solution.py:76
  142.9 2.8 %copy-start.1 = (f32[1024,512]{1,0:T(8,128)S(1)}, f32[1024,512]{1,0:T(8,128)}, u32[]{:S(2)}) copy-start(f32[1024,512]{1,0:T(8,128)} %param.7) | copy-start | bytes 6291460
Sparse Core Ops, SparseCore 0:
  9.5 77.8 all-gather.2

commit v10 on v9

--- a/solution.py
+++ b/solution.py
@@ -37,7 +37,7 @@
     n_z = n_row // n_x
     row = lax.axis_index("row")
     z, x = row // n_x, row % n_x
-    by_z = ring_gather(block, n_z, n_x, outer=True, forward=False)
+    by_z = ring_gather(block, n_z, n_x, outer=True)
     by_xz = ring_gather(by_z, n_z, n_x, outer=False)
     by_zx = jnp.roll(jnp.roll(by_xz, x, axis=0), z, axis=1).swapaxes(0, 1)
     return by_zx.reshape((n_row,) + block.shape)

time: 156 us -> 155 us (level)
  waiting for transfers between devices: 79.3 us -> 71.8 us
  starting transfers between devices: 44.8 us -> 50 us
    ppermute x7 -> x8, waiting for transfers between devices: 24 us -> 16.5 us  [shift(): lax.ppermute(value, 'row', [(r, target(r, step)) for r in range(n_all)])]
    ppermute x7 -> x8, starting transfers between devices: 30.6 us -> 36.8 us  [shift(): lax.ppermute(value, 'row', [(r, target(r, step)) for r in range(n_all)])]
  transfers between devices with their start and end apart: 9 -> 10, of which waited for: 7 -> 7; matrix products, arithmetic and copies ran while one was open for 4% -> 4% of each run, Pallas kernels for 0% -> 0%
where the time goes in v10:
time: 155 us; the launch traced here: 153 us
  waiting for transfers between devices  71.8 us (46%)
  starting transfers between devices  50 us (32%)
  between operations  13.8 us (9%)
  matrix products  8.85 us (6%)
  local copies, waits for them, and re-layouts  4.71 us (3%)
  other arithmetic  3.45 us (2%)
    all_to_all x1, waiting for transfers between devices, local(): col_all = lax.all_to_all(every_tile, 'col', 0, 0, tiled=True)  55.3 us
    ppermute x8, starting transfers between devices, shift(): lax.ppermute(value, 'row', [(r, target(r, step)) for r in range(n_all)])  36.8 us
    ppermute x8, waiting for transfers between devices, shift(): lax.ppermute(value, 'row', [(r, target(r, step)) for r in range(n_all)])  16.5 us
    all_to_all x1, starting transfers between devices, local(): col_all = lax.all_to_all(every_tile, 'col', 0, 0, tiled=True)  13.1 us
    dot_general x1, matrix products, local(): jnp.einsum('cikbr,ckbq->kirq', row_v, col_scaled, preferred_element_type=...  3.75 us
  transfers between devices with their start and end apart: 10, of which 7 were waited for; matrix products, arithmetic and copies ran while one was open for 4% of the time, Pallas kernels for 0%

profile of v10, /device:TPU:1, one launch (start us, length us, event | category | flops | bytes accessed | tf_op | source)
XLA Modules:
  0.0 152.6 jit_solution(4886117272332604851)
XLA Ops:
  6.5 1.6 %copy_bitcast_fusion = bf16[2,2,48,384]{3,2,1,0:T(8,128)(2,1)} fusion(bf16[2,2,32,384]{3,2,1,0:T(8,128)(2,1)} %param.9, bf16[2,2,16,384]{3,2,1,0:T(8,128)(2,1)} %param.8), kind=kLoop, calls=%fused_computation.29 | loop fusion | flops 294912 | bytes 294912 | tf_op jit(solution)/shard_map/transpose | solution.py:55
  8.1 0.0 all-gather.3.cloned.1.call-update
  8.1 1.0 copy.42
  9.1 0.8 copy.46
  10.0 0.1 dynamic-slice_bitcast_fusion
  10.1 0.1 fusion.17
  10.1 0.1 fusion.12
  10.3 0.1 copy.45
  10.4 0.2 maximum_bitcast_fusion.1
  10.6 6.6 %collective-permute-start.1 = (bf16[192,384]{1,0:T(8,128)(2,1)S(1)}, bf16[192,384]{1,0:T(8,128)(2,1)S(1)}, u32[]{:S(2)}, u32[]{:S(2)}) collective-permute-start(bf16[192,384]{1,0:T(8,128)(2,1)S(1)} %bitcast.84), channel_id=1, source_target_pairs={{0,128},{32,160},{64,192},{96,224},{128,256},{160,288},{192,320},{... | collective-permute-start | bytes 442376 | tf_op jit(solution)/shard_map/ppermute | solution.py:22
  17.2 6.8 %collective-permute-start = (bf16[192,384]{1,0:T(8,128)(2,1)S(1)}, bf16[192,384]{1,0:T(8,128)(2,1)S(1)}, u32[]{:S(2)}, u32[]{:S(2)}) collective-permute-start(bf16[192,384]{1,0:T(8,128)(2,1)S(1)} %bitcast.85), channel_id=1, source_target_pairs={{0,384},{32,416},{64,448},{96,480},{128,0},{160,32},{192,64},{224,... | collective-permute-start | bytes 442376 | tf_op jit(solution)/shard_map/ppermute | solution.py:22
  24.0 1.1 collective-permute-done.1
  25.2 4.0 %collective-permute-start.2 = (bf16[96,384]{1,0:T(8,128)(2,1)S(1)}, bf16[96,384]{1,0:T(8,128)(2,1)S(1)}, u32[]{:S(2)}, u32[]{:S(2)}) collective-permute-start(bf16[96,384]{1,0:T(8,128)(2,1)S(1)} %slice.94), channel_id=1, source_target_pairs={{0,128},{32,160},{64,192},{96,224},{128,256},{160,288},{192,320},{... | collective-permute-start | bytes 221192 | tf_op jit(solution)/shard_map/ppermute | solution.py:22
  29.1 1.0 collective-permute-done
  30.1 5.1 %collective-permute-start.3 = (bf16[96,384]{1,0:T(8,128)(2,1)S(1)}, bf16[96,384]{1,0:T(8,128)(2,1)S(1)}, u32[]{:S(2)}, u32[]{:S(2)}) collective-permute-start(bf16[96,384]{1,0:T(8,128)(2,1)S(1)} %slice.95), channel_id=1, source_target_pairs={{0,384},{32,416},{64,448},{96,480},{128,0},{160,32},{192,64},{224,... | collective-permute-start | bytes 221192 | tf_op jit(solution)/shard_map/ppermute | solution.py:22
  35.2 0.0 collective-permute-done.2
  35.2 2.2 %collective-permute-done.3 = bf16[96,384]{1,0:T(8,128)(2,1)S(1)} collective-permute-done((bf16[96,384]{1,0:T(8,128)(2,1)S(1)}, bf16[96,384]{1,0:T(8,128)(2,1)S(1)}, u32[]{:S(2)}, u32[]{:S(2)}) %collective-permute-start.3) | collective-permute-done | bytes 73760 | tf_op jit(solution)/shard_map/ppermute | solution.py:22
  37.4 0.1 pad_maximum_fusion
  37.5 4.7 %collective-permute-start.5 = (bf16[4,192,384]{2,1,0:T(8,128)(2,1)S(1)}, bf16[4,192,384]{2,1,0:T(8,128)(2,1)S(1)}, u32[]{:S(2)}, u32[]{:S(2)}) collective-permute-start(bf16[4,192,384]{2,1,0:T(8,128)(2,1)S(1)} %pad_maximum_fusion), channel_id=1, source_target_pairs={{0,32},{32,64},{64,96},{96,0},{128,160},{160,192},{192,224},{224,1... | collective-permute-start | bytes 1769480 | tf_op jit(solution)/shard_map/ppermute | solution.py:22
  42.2 3.2 %collective-permute-start.4 = (bf16[4,192,384]{2,1,0:T(8,128)(2,1)S(1)}, bf16[4,192,384]{2,1,0:T(8,128)(2,1)S(1)}, u32[]{:S(2)}, u32[]{:S(2)}) collective-permute-start(bf16[4,192,384]{2,1,0:T(8,128)(2,1)S(1)} %pad_maximum_fusion), channel_id=1, source_target_pairs={{0,96},{32,0},{64,32},{96,64},{128,224},{160,128},{192,160},{224,1... | collective-permute-start | bytes 1769480 | tf_op jit(solution)/shard_map/ppermute | solution.py:22
  45.5 8.7 %collective-permute-done.5 = bf16[4,192,384]{2,1,0:T(8,128)(2,1)S(1)} collective-permute-done((bf16[4,192,384]{2,1,0:T(8,128)(2,1)S(1)}, bf16[4,192,384]{2,1,0:T(8,128)(2,1)S(1)}, u32[]{:S(2)}, u32[]{:S(2)}) %collective-permute-start.5) | collective-permute-done | bytes 589856 | tf_op jit(solution)/shard_map/ppermute | solution.py:22
  54.2 1.9 %collective-permute-start.6 = (bf16[4,96,384]{2,1,0:T(8,128)(2,1)S(1)}, bf16[4,96,384]{2,1,0:T(8,128)(2,1)S(1)}, u32[]{:S(2)}, u32[]{:S(2)}) collective-permute-start(bf16[4,96,384]{2,1,0:T(8,128)(2,1)S(1)} %slice.96), channel_id=1, source_target_pairs={{0,32},{32,64},{64,96},{96,0},{128,160},{160,192},{192,224},{224,1... | collective-permute-start | bytes 884744 | tf_op jit(solution)/shard_map/ppermute | solution.py:22
  56.2 0.0 collective-permute-done.4
  56.2 4.6 %collective-permute-start.7 = (bf16[4,96,384]{2,1,0:T(8,128)(2,1)S(1)}, bf16[4,96,384]{2,1,0:T(8,128)(2,1)S(1)}, u32[]{:S(2)}, u32[]{:S(2)}) collective-permute-start(bf16[4,96,384]{2,1,0:T(8,128)(2,1)S(1)} %slice.97), channel_id=1, source_target_pairs={{0,96},{32,0},{64,32},{96,64},{128,224},{160,128},{192,160},{224,1... | collective-permute-start | bytes 884744 | tf_op jit(solution)/shard_map/ppermute | solution.py:22
  60.8 0.1 bitcast_dynamic-update-slice_fusion.4
  60.9 0.1 bitcast_dynamic-update-slice_fusion.2
  61.0 1.9 %collective-permute-done.6 = bf16[4,96,384]{2,1,0:T(8,128)(2,1)S(1)} collective-permute-done((bf16[4,96,384]{2,1,0:T(8,128)(2,1)S(1)}, bf16[4,96,384]{2,1,0:T(8,128)(2,1)S(1)}, u32[]{:S(2)}, u32[]{:S(2)}) %collective-permute-start.6) | collective-permute-done | bytes 294944 | tf_op jit(solution)/shard_map/ppermute | solution.py:22
  62.9 1.5 %collective-permute-done.7 = bf16[4,96,384]{2,1,0:T(8,128)(2,1)S(1)} collective-permute-done((bf16[4,96,384]{2,1,0:T(8,128)(2,1)S(1)}, bf16[4,96,384]{2,1,0:T(8,128)(2,1)S(1)}, u32[]{:S(2)}, u32[]{:S(2)}) %collective-permute-start.7) | collective-permute-done | bytes 294944 | tf_op jit(solution)/shard_map/ppermute | solution.py:22
  64.4 0.1 fusion.9
  64.5 0.1 bitcast_dynamic-update-slice_fusion
  64.7 0.1 bitcast_dynamic-update-slice_fusion.5
  64.8 0.1 bitcast_dynamic-update-slice_fusion.3
  64.9 0.1 fusion.10
  65.0 0.1 bitcast_dynamic-update-slice_fusion.1
  65.1 0.3 constant_dynamic-slice_fusion
  65.3 1.0 fusion.3
  66.3 1.7 %copy.49 = bf16[4,4,192,384]{3,2,1,0:T(8,128)(2,1)} copy(bf16[4,4,192,384]{3,2,0,1:T(8,128)(2,1)S(1)} %fusion.3) | data formatting | bytes 4718592 | tf_op jit(solution)/shard_map/transpose | solution.py:42
  68.1 13.1 %all-to-all-start = ((bf16[32,96,384]{2,1,0:T(8,128)(2,1)}), bf16[32,96,384]{2,1,0:T(8,128)(2,1)S(1)}, u32[]{:S(2)}, u32[]{:S(2)}) async-start(bf16[32,96,384]{2,1,0:T(8,128)(2,1)} %bitcast.23), calls=%async_computation | async-start | bytes 4718592 | tf_op jit(solution)/shard_map/all_to_all | solution.py:76
  81.2 0.0 copy-done.4
  81.3 0.1 multiply_select_fusion
  81.4 55.3 %all-to-all-done = bf16[32,96,384]{2,1,0:T(8,128)(2,1)S(1)} async-done(((bf16[32,96,384]{2,1,0:T(8,128)(2,1)}), bf16[32,96,384]{2,1,0:T(8,128)(2,1)S(1)}, u32[]{:S(2)}, u32[]{:S(2)}) %all-to-all-start) | async-done | bytes 2359328 | tf_op jit(solution)/shard_map/all_to_all | solution.py:76
  136.7 0.1 slice_bitcast_fusion.2
  136.8 0.1 copy.51
  136.8 0.0 all-gather.3.cloned.1.call-done
  136.9 3.7 %fusion = f32[2,2,384,384,1]{3,2,1,0,4:T(8,128)S(1)} fusion(bf16[32,2,48,384]{3,2,1,0:T(8,128)(2,1)S(1)} %bitcast.82, bf16[32,2,2,48,384]{4,3,2,1,0:T(8,128)(2,1)} %bitcast.100), kind=kOutput, calls=%fused_computation.2 | convolution fusion | flops 1207959552 | bytes 7077888 | tf_op jit(solution)/shard_map/cikbr,ckbq->kirq/dot_general | solution.py:88
  140.6 0.0 copy-start.1
  140.6 2.8 %convolution_convert_fusion = bf16[2,2,32,16,384]{4,3,2,1,0:T(8,128)(2,1)S(1)} fusion(bf16[32,2,2,48,384]{4,3,2,1,0:T(8,128)(2,1)} %bitcast.101, f32[2,2,384,384,1]{3,2,1,0,4:T(8,128)S(1)} %fusion, f32[2,384]{1,0:T(2,128)S(1)} %bitcast.99, f32[2,2,384]{2,0,1:T(2,128)S(1)} %copy.40), kind=kOutput, calls=%fused_computation.10 | convolution fusion | flops 606535680 | bytes 5514240 | tf_op jit(solution)/shard_map/cikmr,kirq->kicmq/dot_general | solution.py:90
  143.4 2.3 %bitcast_subtract_fusion = f32[1024,512]{1,0:T(8,128)} fusion(f32[1024,512]{1,0:T(8,128)S(1)} %copy-done.1, bf16[1024,2,384]{2,0,1:T(8,128)(2,1)S(1)} %bitcast.95, bf16[2,512,384]{2,1,0:T(8,128)(2,1)S(1)} %bitcast.83), kind=kOutput, calls=%fused_computation.9 | convolution fusion | flops 805830656 | bytes 6553600 | tf_op jit(solution)/shard_map/kicmq,knq->icmn/dot_general | solution.py:92
  (23 shorter events, 0.2 us)
Async XLA Ops:
  6.5 3.4 %copy-start = (f32[2,2,2,512]{3,2,1,0:T(2,128)S(1)}, f32[2,2,2,512]{3,2,1,0:T(2,128)}, u32[]{:S(2)}) copy-start(f32[2,2,2,512]{3,2,1,0:T(2,128)} %param.13) | copy-start | bytes 49156
  6.5 130.3 %all-gather.3.cloned.1.call-start = ((), (), s32[]{:S(2)}) async-start(), calls=%async_computation.1 | async-start | bytes 4866048 | tf_op jit(solution)/shard_map/all_gather | solution.py:57
  10.6 14.5 %collective-permute-start.1 = (bf16[192,384]{1,0:T(8,128)(2,1)S(1)}, bf16[192,384]{1,0:T(8,128)(2,1)S(1)}, u32[]{:S(2)}, u32[]{:S(2)}) collective-permute-start(bf16[192,384]{1,0:T(8,128)(2,1)S(1)} %bitcast.84), channel_id=1, source_target_pairs={{0,128},{32,160},{64,192},{96,224},{128,256},{160,288},{192,320},{... | collective-permute-start | bytes 442376 | tf_op jit(solution)/shard_map/ppermute | solution.py:22
  17.2 12.9 %collective-permute-start = (bf16[192,384]{1,0:T(8,128)(2,1)S(1)}, bf16[192,384]{1,0:T(8,128)(2,1)S(1)}, u32[]{:S(2)}, u32[]{:S(2)}) collective-permute-start(bf16[192,384]{1,0:T(8,128)(2,1)S(1)} %bitcast.85), channel_id=1, source_target_pairs={{0,384},{32,416},{64,448},{96,480},{128,0},{160,32},{192,64},{224,... | collective-permute-start | bytes 442376 | tf_op jit(solution)/shard_map/ppermute | solution.py:22
  25.2 10.1 %collective-permute-start.2 = (bf16[96,384]{1,0:T(8,128)(2,1)S(1)}, bf16[96,384]{1,0:T(8,128)(2,1)S(1)}, u32[]{:S(2)}, u32[]{:S(2)}) collective-permute-start(bf16[96,384]{1,0:T(8,128)(2,1)S(1)} %slice.94), channel_id=1, source_target_pairs={{0,128},{32,160},{64,192},{96,224},{128,256},{160,288},{192,320},{... | collective-permute-start | bytes 221192 | tf_op jit(solution)/shard_map/ppermute | solution.py:22
  30.1 7.3 %collective-permute-start.3 = (bf16[96,384]{1,0:T(8,128)(2,1)S(1)}, bf16[96,384]{1,0:T(8,128)(2,1)S(1)}, u32[]{:S(2)}, u32[]{:S(2)}) collective-permute-start(bf16[96,384]{1,0:T(8,128)(2,1)S(1)} %slice.95), channel_id=1, source_target_pairs={{0,384},{32,416},{64,448},{96,480},{128,0},{160,32},{192,64},{224,... | collective-permute-start | bytes 221192 | tf_op jit(solution)/shard_map/ppermute | solution.py:22
  37.5 16.7 %collective-permute-start.5 = (bf16[4,192,384]{2,1,0:T(8,128)(2,1)S(1)}, bf16[4,192,384]{2,1,0:T(8,128)(2,1)S(1)}, u32[]{:S(2)}, u32[]{:S(2)}) collective-permute-start(bf16[4,192,384]{2,1,0:T(8,128)(2,1)S(1)} %pad_maximum_fusion), channel_id=1, source_target_pairs={{0,32},{32,64},{64,96},{96,0},{128,160},{160,192},{192,224},{224,1... | collective-permute-start | bytes 1769480 | tf_op jit(solution)/shard_map/ppermute | solution.py:22
  42.2 13.9 %collective-permute-start.4 = (bf16[4,192,384]{2,1,0:T(8,128)(2,1)S(1)}, bf16[4,192,384]{2,1,0:T(8,128)(2,1)S(1)}, u32[]{:S(2)}, u32[]{:S(2)}) collective-permute-start(bf16[4,192,384]{2,1,0:T(8,128)(2,1)S(1)} %pad_maximum_fusion), channel_id=1, source_target_pairs={{0,96},{32,0},{64,32},{96,64},{128,224},{160,128},{192,160},{224,1... | collective-permute-start | bytes 1769480 | tf_op jit(solution)/shard_map/ppermute | solution.py:22
  54.2 8.7 %collective-permute-start.6 = (bf16[4,96,384]{2,1,0:T(8,128)(2,1)S(1)}, bf16[4,96,384]{2,1,0:T(8,128)(2,1)S(1)}, u32[]{:S(2)}, u32[]{:S(2)}) collective-permute-start(bf16[4,96,384]{2,1,0:T(8,128)(2,1)S(1)} %slice.96), channel_id=1, source_target_pairs={{0,32},{32,64},{64,96},{96,0},{128,160},{160,192},{192,224},{224,1... | collective-permute-start | bytes 884744 | tf_op jit(solution)/shard_map/ppermute | solution.py:22
  56.2 8.2 %collective-permute-start.7 = (bf16[4,96,384]{2,1,0:T(8,128)(2,1)S(1)}, bf16[4,96,384]{2,1,0:T(8,128)(2,1)S(1)}, u32[]{:S(2)}, u32[]{:S(2)}) collective-permute-start(bf16[4,96,384]{2,1,0:T(8,128)(2,1)S(1)} %slice.97), channel_id=1, source_target_pairs={{0,96},{32,0},{64,32},{96,64},{128,224},{160,128},{192,160},{224,1... | collective-permute-start | bytes 884744 | tf_op jit(solution)/shard_map/ppermute | solution.py:22
  68.1 13.2 %copy-start.4 = (s32[2,32]{1,0:T(2,128)S(1)}, s32[2,32]{1,0:T(2,128)}, u32[]{:S(2)}) copy-start(s32[2,32]{1,0:T(2,128)} %param.12) | copy-start | bytes 772
  68.1 13.2 %copy-start.2 = (f32[2,32,384]{2,1,0:T(8,128)S(1)}, f32[2,32,384]{2,1,0:T(8,128)}, u32[]{:S(2)}) copy-start(f32[2,32,384]{2,1,0:T(8,128)} %param.11) | copy-start | bytes 294916
  68.1 13.2 %copy-start.3 = (f32[2,32,384]{2,1,0:T(8,128)S(1)}, f32[2,32,384]{2,1,0:T(8,128)}, u32[]{:S(2)}) copy-start(f32[2,32,384]{2,1,0:T(8,128)} %param.10) | copy-start | bytes 294916
  68.1 68.6 %all-to-all-start = ((bf16[32,96,384]{2,1,0:T(8,128)(2,1)}), bf16[32,96,384]{2,1,0:T(8,128)(2,1)S(1)}, u32[]{:S(2)}, u32[]{:S(2)}) async-start(bf16[32,96,384]{2,1,0:T(8,128)(2,1)} %bitcast.23), calls=%async_computation | async-start | bytes 4718592 | tf_op jit(solution)/shard_map/all_to_all | solution.py:76
  140.6 2.8 %copy-start.1 = (f32[1024,512]{1,0:T(8,128)S(1)}, f32[1024,512]{1,0:T(8,128)}, u32[]{:S(2)}) copy-start(f32[1024,512]{1,0:T(8,128)} %param.7) | copy-start | bytes 6291460
Sparse Core Ops, SparseCore 0:
  9.5 76.5 all-gather.2

commit v11 on v10

--- a/solution.py
+++ b/solution.py
@@ -1,7 +1,7 @@
 import jax
 import jax.numpy as jnp
 from jax import lax
-from jax.sharding import PartitionSpec as P
+from jax.sharding import Mesh, PartitionSpec as P
 
 
 def column_weight(u_scale_k, v_scale_k, ranks_k):
@@ -46,15 +46,21 @@
 def local(slab, u_codes, v_codes, u_scale, v_scale, ranks, d_inverse):
     panels, per_row, u_rows, rank_most = u_codes.shape
     v_rows = v_codes.shape[2]
-    n_col = lax.axis_size("col")
-    column = lax.axis_index("col")
+    n_core = lax.axis_size("core")
+    n_col = lax.axis_size("yz") * n_core
+    core = lax.axis_index("core")
+    column = lax.axis_index("yz") * n_core + core
     first_tile = lax.axis_index("row") * per_row
     tile_order = n_col * u_rows
     both = u_rows + v_rows
 
     shard = jnp.concatenate([u_codes, v_codes], axis=2).transpose(1, 0, 2, 3)
 
-    row_all = lax.all_gather(shard, "col", axis=0, tiled=False)
+    mine = lax.all_gather(shard, "yz", axis=0, tiled=False)
+    other = lax.ppermute(mine, "core", [(0, 1), (1, 0)])
+    first = jnp.where(core == 0, mine, other)
+    second = jnp.where(core == 0, other, mine)
+    row_all = jnp.stack([first, second], axis=1).reshape((n_col,) + shard.shape)
     row_u = row_all[:, :, :, :u_rows]
     row_v = row_all[:, :, :, u_rows:]
 
@@ -73,7 +79,7 @@
     flat = col_shard.reshape(per_row * panels * both, rank_most)
     every_tile = replicate_over_row(flat, n_row)
     every_tile = every_tile.reshape(n_row * per_row, panels * both, rank_most)
-    col_all = lax.all_to_all(every_tile, "col", 0, 0, tiled=True)
+    col_all = lax.all_to_all(every_tile, ("yz", "core"), 0, 0, tiled=True)
     col_all = col_all.reshape(n_col, panels, both, rank_most)
     col_u = col_all[:, :, :u_rows].transpose(1, 0, 2, 3).reshape(panels, tile_order, rank_most)
     col_v = col_all[:, :, u_rows:]
@@ -94,14 +100,17 @@
 
 
 def solution(mesh):
+    n_row, n_col = mesh.devices.shape
+    split = Mesh(mesh.devices.reshape(n_row, n_col // 2, 2), ("row", "yz", "core"))
+    cols = ("yz", "core")
     in_specs = (
-        P("row", "col"),
-        P(None, "row", "col", None),
-        P(None, "row", "col", None),
+        P("row", cols),
+        P(None, "row", cols, None),
+        P(None, "row", cols, None),
         P(),
         P(),
         P(),
         P(),
     )
-    out_specs = P("row", "col")
-    return jax.shard_map(local, mesh=mesh, in_specs=in_specs, out_specs=out_specs, check_vma=False)
+    out_specs = P("row", cols)
+    return jax.shard_map(local, mesh=split, in_specs=in_specs, out_specs=out_specs, check_vma=False)

time: 155 us -> 186 us (1.20)
  waiting for transfers between devices: 71.8 us -> 85.1 us
  starting transfers between devices: 50 us -> 57.8 us
  local copies, waits for them, and re-layouts: 4.71 us -> 9.94 us
  other arithmetic: 3.45 us -> 7.31 us
  matrix products: 8.85 us -> 10.8 us
    all_gather x1, waiting for transfers between devices: 0.02 us -> 66.9 us  [local(): mine = lax.all_gather(shard, 'yz', axis=0, tiled=False)]
    all_to_all x1, waiting for transfers between devices: 55.3 us -> 0.01 us  [local(): col_all = lax.all_to_all(every_tile, ('yz', 'core'), 0, 0, tiled=True)]
    ppermute x0 -> x1, starting transfers between devices: none -> 7.35 us  [local(): other = lax.ppermute(mine, 'core', [(0, 1), (1, 0)])]
    another operation x1 -> x3, other arithmetic: 0.1 us -> 4.86 us  [the longest x2 4.76 us: local(): row_all = jnp.stack([first, second], axis=1).reshape((n_col,) + shard.shape)]
    dot_general x1, matrix products: 2.77 us -> 7.05 us  [local(): jnp.einsum('cikmr,kirq->kicmq', row_u, core, preferred_element_type=jnp.f...]
    dot_general x1 -> x0, matrix products: 3.75 us -> none  [local(): jnp.einsum('cikbr,ckbq->kirq', row_v, col_scaled, preferred_element_type=...]
    all_gather x0 -> x1, local copies, waits for them, and re-layouts: none -> 3.34 us  [local(): mine = lax.all_gather(shard, 'yz', axis=0, tiled=False)]
    ppermute x0 -> x1, waiting for transfers between devices: none -> 2.97 us  [local(): other = lax.ppermute(mine, 'core', [(0, 1), (1, 0)])]
  transfers between devices with their start and end apart: 10 -> 11, of which waited for: 7 -> 8; matrix products, arithmetic and copies ran while one was open for 4% -> 5% of each run, Pallas kernels for 0% -> 0%
where the time goes in v11:
time: 186 us; the launch traced here: 185 us
  waiting for transfers between devices  85.1 us (46%)
  starting transfers between devices  57.8 us (31%)
  between operations  13.8 us (7%)
  matrix products  10.8 us (6%)
  local copies, waits for them, and re-layouts  9.94 us (5%)
  other arithmetic  7.31 us (4%)
    all_gather x1, waiting for transfers between devices, local(): mine = lax.all_gather(shard, 'yz', axis=0, tiled=False)  66.9 us
    ppermute x8, starting transfers between devices, shift(): lax.ppermute(value, 'row', [(r, target(r, step)) for r in range(n_all)])  36.8 us
    ppermute x8, waiting for transfers between devices, shift(): lax.ppermute(value, 'row', [(r, target(r, step)) for r in range(n_all)])  15.2 us
    all_to_all x1, starting transfers between devices, local(): col_all = lax.all_to_all(every_tile, ('yz', 'core'), 0, 0, tiled=True)  13.6 us
    ppermute x1, starting transfers between devices, local(): other = lax.ppermute(mine, 'core', [(0, 1), (1, 0)])  7.35 us
    dot_general x1, matrix products, local(): jnp.einsum('cikmr,kirq->kicmq', row_u, core, preferred_element_type=jnp.f...  7.05 us
    another operation x2, other arithmetic, local(): row_all = jnp.stack([first, second], axis=1).reshape((n_col,) + shard.shape)  4.76 us
    dot_general x1, matrix products, local(): jnp.einsum('kicmq,knq->icmn', left, col_u, preferred_element_type=jnp.flo...  3.73 us
  transfers between devices with their start and end apart: 11, of which 8 were waited for; matrix products, arithmetic and copies ran while one was open for 5% of the time, Pallas kernels for 0%

profile of v11, /device:TPU:1, one launch (start us, length us, event | category | flops | bytes accessed | tf_op | source)
XLA Modules:
  0.0 184.8 jit_solution(4781796835192604409)
XLA Ops:
  6.6 0.7 copy-done
  7.3 0.1 dynamic-slice_bitcast_fusion
  7.3 1.0 copy.37
  8.3 0.1 fusion.24
  8.4 0.1 fusion.19
  8.5 0.1 copy.40
  8.6 0.8 copy.41
  9.4 0.2 maximum_bitcast_fusion.2
  9.7 6.6 %collective-permute-start.2 = (bf16[192,384]{1,0:T(8,128)(2,1)S(1)}, bf16[192,384]{1,0:T(8,128)(2,1)S(1)}, u32[]{:S(2)}, u32[]{:S(2)}) collective-permute-start(bf16[192,384]{1,0:T(8,128)(2,1)S(1)} %bitcast.99), channel_id=1, source_target_pairs={{0,128},{32,160},{64,192},{96,224},{128,256},{160,288},{192,320},{... | collective-permute-start | bytes 442376 | tf_op jit(solution)/shard_map/ppermute | solution.py:22
  16.3 6.8 %collective-permute-start.1 = (bf16[192,384]{1,0:T(8,128)(2,1)S(1)}, bf16[192,384]{1,0:T(8,128)(2,1)S(1)}, u32[]{:S(2)}, u32[]{:S(2)}) collective-permute-start(bf16[192,384]{1,0:T(8,128)(2,1)S(1)} %bitcast.100), channel_id=1, source_target_pairs={{0,384},{32,416},{64,448},{96,480},{128,0},{160,32},{192,64},{224,... | collective-permute-start | bytes 442376 | tf_op jit(solution)/shard_map/ppermute | solution.py:22
  23.1 1.1 collective-permute-done.2
  24.2 4.0 %collective-permute-start.3 = (bf16[96,384]{1,0:T(8,128)(2,1)S(1)}, bf16[96,384]{1,0:T(8,128)(2,1)S(1)}, u32[]{:S(2)}, u32[]{:S(2)}) collective-permute-start(bf16[96,384]{1,0:T(8,128)(2,1)S(1)} %slice.94), channel_id=1, source_target_pairs={{0,128},{32,160},{64,192},{96,224},{128,256},{160,288},{192,320},{... | collective-permute-start | bytes 221192 | tf_op jit(solution)/shard_map/ppermute | solution.py:22
  28.2 1.0 collective-permute-done.1
  29.2 5.1 %collective-permute-start.4 = (bf16[96,384]{1,0:T(8,128)(2,1)S(1)}, bf16[96,384]{1,0:T(8,128)(2,1)S(1)}, u32[]{:S(2)}, u32[]{:S(2)}) collective-permute-start(bf16[96,384]{1,0:T(8,128)(2,1)S(1)} %slice.95), channel_id=1, source_target_pairs={{0,384},{32,416},{64,448},{96,480},{128,0},{160,32},{192,64},{224,... | collective-permute-start | bytes 221192 | tf_op jit(solution)/shard_map/ppermute | solution.py:22
  34.3 1.9 %collective-permute-done.4 = bf16[96,384]{1,0:T(8,128)(2,1)S(1)} collective-permute-done((bf16[96,384]{1,0:T(8,128)(2,1)S(1)}, bf16[96,384]{1,0:T(8,128)(2,1)S(1)}, u32[]{:S(2)}, u32[]{:S(2)}) %collective-permute-start.4) | collective-permute-done | bytes 73760 | tf_op jit(solution)/shard_map/ppermute | solution.py:22
  36.2 0.1 pad_maximum_fusion.1
  36.3 4.7 %collective-permute-start.6 = (bf16[4,192,384]{2,1,0:T(8,128)(2,1)S(1)}, bf16[4,192,384]{2,1,0:T(8,128)(2,1)S(1)}, u32[]{:S(2)}, u32[]{:S(2)}) collective-permute-start(bf16[4,192,384]{2,1,0:T(8,128)(2,1)S(1)} %pad_maximum_fusion.1), channel_id=1, source_target_pairs={{0,32},{32,64},{64,96},{96,0},{128,160},{160,192},{192,224},{224,1... | collective-permute-start | bytes 1769480 | tf_op jit(solution)/shard_map/ppermute | solution.py:22
  41.0 3.2 %collective-permute-start.5 = (bf16[4,192,384]{2,1,0:T(8,128)(2,1)S(1)}, bf16[4,192,384]{2,1,0:T(8,128)(2,1)S(1)}, u32[]{:S(2)}, u32[]{:S(2)}) collective-permute-start(bf16[4,192,384]{2,1,0:T(8,128)(2,1)S(1)} %pad_maximum_fusion.1), channel_id=1, source_target_pairs={{0,96},{32,0},{64,32},{96,64},{128,224},{160,128},{192,160},{224,1... | collective-permute-start | bytes 1769480 | tf_op jit(solution)/shard_map/ppermute | solution.py:22
  44.2 0.7 maximum_bitcast_fusion.1
  44.9 0.0 all-gather.3.cloned.1.call-update
  45.0 7.7 %collective-permute-done.6 = bf16[4,192,384]{2,1,0:T(8,128)(2,1)S(1)} collective-permute-done((bf16[4,192,384]{2,1,0:T(8,128)(2,1)S(1)}, bf16[4,192,384]{2,1,0:T(8,128)(2,1)S(1)}, u32[]{:S(2)}, u32[]{:S(2)}) %collective-permute-start.6) | collective-permute-done | bytes 589856 | tf_op jit(solution)/shard_map/ppermute | solution.py:22
  52.7 1.9 %collective-permute-start.7 = (bf16[4,96,384]{2,1,0:T(8,128)(2,1)S(1)}, bf16[4,96,384]{2,1,0:T(8,128)(2,1)S(1)}, u32[]{:S(2)}, u32[]{:S(2)}) collective-permute-start(bf16[4,96,384]{2,1,0:T(8,128)(2,1)S(1)} %slice.96), channel_id=1, source_target_pairs={{0,32},{32,64},{64,96},{96,0},{128,160},{160,192},{192,224},{224,1... | collective-permute-start | bytes 884744 | tf_op jit(solution)/shard_map/ppermute | solution.py:22
  54.7 4.6 %collective-permute-start.8 = (bf16[4,96,384]{2,1,0:T(8,128)(2,1)S(1)}, bf16[4,96,384]{2,1,0:T(8,128)(2,1)S(1)}, u32[]{:S(2)}, u32[]{:S(2)}) collective-permute-start(bf16[4,96,384]{2,1,0:T(8,128)(2,1)S(1)} %slice.97), channel_id=1, source_target_pairs={{0,96},{32,0},{64,32},{96,64},{128,224},{160,128},{192,160},{224,1... | collective-permute-start | bytes 884744 | tf_op jit(solution)/shard_map/ppermute | solution.py:22
  59.3 0.1 bitcast_dynamic-update-slice_fusion.4
  59.4 0.1 bitcast_dynamic-update-slice_fusion.2
  59.5 1.9 %collective-permute-done.7 = bf16[4,96,384]{2,1,0:T(8,128)(2,1)S(1)} collective-permute-done((bf16[4,96,384]{2,1,0:T(8,128)(2,1)S(1)}, bf16[4,96,384]{2,1,0:T(8,128)(2,1)S(1)}, u32[]{:S(2)}, u32[]{:S(2)}) %collective-permute-start.7) | collective-permute-done | bytes 294944 | tf_op jit(solution)/shard_map/ppermute | solution.py:22
  61.4 1.5 collective-permute-done.8
  62.9 0.1 fusion.16
  63.1 0.1 bitcast_dynamic-update-slice_fusion
  63.2 0.1 bitcast_dynamic-update-slice_fusion.5
  63.3 0.1 bitcast_dynamic-update-slice_fusion.3
  63.4 0.1 fusion.17
  63.5 0.1 bitcast_dynamic-update-slice_fusion.1
  63.6 0.3 constant_dynamic-slice_fusion
  63.9 1.0 fusion.3
  64.8 1.8 copy.44
  66.6 13.6 %all-to-all-start = ((bf16[32,96,384]{2,1,0:T(8,128)(2,1)}), bf16[32,96,384]{2,1,0:T(8,128)(2,1)}, u32[]{:S(2)}, u32[]{:S(2)}) async-start(bf16[32,96,384]{2,1,0:T(8,128)(2,1)} %bitcast.27), calls=%async_computation | async-start | bytes 4718592 | tf_op jit(solution)/shard_map/all_to_all | solution.py:82
  80.2 66.9 %all-gather.3.cloned.1.call-done = bf16[32,2,48,384]{3,2,0,1:T(8,128)(2,1)} async-done(((bf16[2,2,48,384]{3,2,0,1:T(8,128)(2,1)}), bf16[32,2,48,384]{3,2,0,1:T(8,128)(2,1)}) %all-gather.3.cloned.1.call-update) | async-done | bytes 2359312 | tf_op jit(solution)/shard_map/all_gather | solution.py:59
  147.2 3.3 %copy.33 = bf16[16,2,2,48,384]{4,3,0,1,2:T(8,128)(2,1)} copy(bf16[16,2,2,48,384]{4,3,1,0,2:T(8,128)(2,1)} %bitcast.95) | data formatting | bytes 4718592 | tf_op jit(solution)/shard_map/all_gather | solution.py:59
  150.5 7.3 %collective-permute-start = (bf16[16,2,2,48,384]{4,3,0,1,2:T(8,128)(2,1)}, bf16[16,2,2,48,384]{4,3,0,1,2:T(8,128)(2,1)}, u32[]{:S(2)}, u32[]{:S(2)}) collective-permute-start(bf16[16,2,2,48,384]{4,3,0,1,2:T(8,128)(2,1)} %copy.33), channel_id=1, source_target_pairs={{0,1},{1,0},{2,3},{3,2},{4,5},{5,4},{6,7},{7,6},{8,9},{9,8},{10,11... | collective-permute-start | bytes 7077896 | tf_op jit(solution)/shard_map/ppermute | solution.py:60
  157.9 0.1 multiply_select_fusion
  158.1 1.2 slice_bitcast_fusion
  159.3 0.1 copy.46
  159.4 3.0 %collective-permute-done = bf16[16,2,2,48,384]{4,3,0,1,2:T(8,128)(2,1)} collective-permute-done((bf16[16,2,2,48,384]{4,3,0,1,2:T(8,128)(2,1)}, bf16[16,2,2,48,384]{4,3,0,1,2:T(8,128)(2,1)}, u32[]{:S(2)}, u32[]{:S(2)}) %collective-permute-start) | collective-permute-done | bytes 2359328 | tf_op jit(solution)/shard_map/ppermute | solution.py:60
  162.4 2.1 %select_bitcast_fusion.1 = (bf16[16,1,2,2,48,384]{5,4,1,0,2,3:T(8,128)(2,1)S(1)}, bf16[16,1,2,2,48,384]{5,4,1,0,2,3:T(8,128)(2,1)S(1)}) fusion(bf16[16,2,2,48,384]{4,3,0,1,2:T(8,128)(2,1)} %collective-permute-done, pred[]{:T(512)S(6)} %eq.11, bf16[16,2,2,48,384]{4,3,1,0,2:T(8,128)(2,1)S(1)} %bitcast.96), kind=kLoop, calls=%fused_computation.11 | loop fusion | flops 2359296 | bytes 9437185 | tf_op jit(solution)/shard_map/stack | solution.py:63
  164.5 2.7 %pad_maximum_fusion = bf16[16,2,2,2,48,384]{5,4,1,0,2,3:T(8,128)(2,1)} fusion(bf16[16,1,2,2,48,384]{5,4,1,0,2,3:T(8,128)(2,1)S(1)} %get-tuple-element.6, bf16[16,1,2,2,48,384]{5,4,1,0,2,3:T(8,128)(2,1)S(1)} %get-tuple-element.5), kind=kLoop, calls=%fused_computation | loop fusion | flops 2359296 | bytes 9437184 | tf_op jit(solution)/shard_map/stack | solution.py:63
  167.1 7.1 %convolution_convert_fusion = bf16[2,2,32,16,384]{4,3,2,1,0:T(8,128)(2,1)} fusion(bf16[32,2,2,48,384]{4,3,0,1,2:T(8,128)(2,1)} %bitcast.97, f32[2,384]{1,0:T(2,128)S(1)} %bitcast.114, f32[2,2,384]{2,1,0:T(2,128)S(1)} %fusion.22, bf16[32,2,48,384]{3,2,1,0:T(8,128)(2,1)} %bitcast.28), kind=kOutput, calls=%fused_computation.13 | convolution fusion | flops 1814495232 | bytes 7873536 | tf_op jit(solution)/shard_map/cikmr,kirq->kicmq/dot_general | solution.py:96
  174.2 3.7 %bitcast_subtract_fusion = f32[1024,512]{1,0:T(8,128)} fusion(f32[1024,512]{1,0:T(8,128)S(1)} %copy-done.2, bf16[1024,2,384]{2,0,1:T(8,128)(2,1)} %bitcast.110, bf16[2,512,384]{2,1,0:T(8,128)(2,1)S(1)} %bitcast.98), kind=kOutput, calls=%fused_computation.12 | convolution fusion | flops 805830656 | bytes 6553600 | tf_op jit(solution)/shard_map/kicmq,knq->icmn/dot_general | solution.py:98
  (32 shorter events, 0.2 us)
Async XLA Ops:
  6.5 0.7 copy-start
  6.5 37.7 %copy-start.3 = (bf16[2,2,32,384]{3,2,1,0:T(8,128)(2,1)S(1)}, bf16[2,2,32,384]{3,2,1,0:T(8,128)(2,1)}, u32[]{:S(2)}) copy-start(bf16[2,2,32,384]{3,2,1,0:T(8,128)(2,1)} %param.9) | copy-start | bytes 294916
  6.5 37.7 %copy-start.4 = (bf16[2,2,16,384]{3,2,1,0:T(8,128)(2,1)S(1)}, bf16[2,2,16,384]{3,2,1,0:T(8,128)(2,1)}, u32[]{:S(2)}) copy-start(bf16[2,2,16,384]{3,2,1,0:T(8,128)(2,1)} %param.8) | copy-start | bytes 147460
  6.5 140.6 %all-gather.3.cloned.1.call-start = ((), (), s32[]{:S(2)}) async-start(), calls=%async_computation.1 | async-start | bytes 2506752 | tf_op jit(solution)/shard_map/all_gather | solution.py:59
  9.7 14.5 %collective-permute-start.2 = (bf16[192,384]{1,0:T(8,128)(2,1)S(1)}, bf16[192,384]{1,0:T(8,128)(2,1)S(1)}, u32[]{:S(2)}, u32[]{:S(2)}) collective-permute-start(bf16[192,384]{1,0:T(8,128)(2,1)S(1)} %bitcast.99), channel_id=1, source_target_pairs={{0,128},{32,160},{64,192},{96,224},{128,256},{160,288},{192,320},{... | collective-permute-start | bytes 442376 | tf_op jit(solution)/shard_map/ppermute | solution.py:22
  16.3 12.9 %collective-permute-start.1 = (bf16[192,384]{1,0:T(8,128)(2,1)S(1)}, bf16[192,384]{1,0:T(8,128)(2,1)S(1)}, u32[]{:S(2)}, u32[]{:S(2)}) collective-permute-start(bf16[192,384]{1,0:T(8,128)(2,1)S(1)} %bitcast.100), channel_id=1, source_target_pairs={{0,384},{32,416},{64,448},{96,480},{128,0},{160,32},{192,64},{224,... | collective-permute-start | bytes 442376 | tf_op jit(solution)/shard_map/ppermute | solution.py:22
  24.2 10.1 %collective-permute-start.3 = (bf16[96,384]{1,0:T(8,128)(2,1)S(1)}, bf16[96,384]{1,0:T(8,128)(2,1)S(1)}, u32[]{:S(2)}, u32[]{:S(2)}) collective-permute-start(bf16[96,384]{1,0:T(8,128)(2,1)S(1)} %slice.94), channel_id=1, source_target_pairs={{0,128},{32,160},{64,192},{96,224},{128,256},{160,288},{192,320},{... | collective-permute-start | bytes 221192 | tf_op jit(solution)/shard_map/ppermute | solution.py:22
  29.2 7.0 %collective-permute-start.4 = (bf16[96,384]{1,0:T(8,128)(2,1)S(1)}, bf16[96,384]{1,0:T(8,128)(2,1)S(1)}, u32[]{:S(2)}, u32[]{:S(2)}) collective-permute-start(bf16[96,384]{1,0:T(8,128)(2,1)S(1)} %slice.95), channel_id=1, source_target_pairs={{0,384},{32,416},{64,448},{96,480},{128,0},{160,32},{192,64},{224,... | collective-permute-start | bytes 221192 | tf_op jit(solution)/shard_map/ppermute | solution.py:22
  36.3 16.4 %collective-permute-start.6 = (bf16[4,192,384]{2,1,0:T(8,128)(2,1)S(1)}, bf16[4,192,384]{2,1,0:T(8,128)(2,1)S(1)}, u32[]{:S(2)}, u32[]{:S(2)}) collective-permute-start(bf16[4,192,384]{2,1,0:T(8,128)(2,1)S(1)} %pad_maximum_fusion.1), channel_id=1, source_target_pairs={{0,32},{32,64},{64,96},{96,0},{128,160},{160,192},{192,224},{224,1... | collective-permute-start | bytes 1769480 | tf_op jit(solution)/shard_map/ppermute | solution.py:22
  41.0 13.7 %collective-permute-start.5 = (bf16[4,192,384]{2,1,0:T(8,128)(2,1)S(1)}, bf16[4,192,384]{2,1,0:T(8,128)(2,1)S(1)}, u32[]{:S(2)}, u32[]{:S(2)}) collective-permute-start(bf16[4,192,384]{2,1,0:T(8,128)(2,1)S(1)} %pad_maximum_fusion.1), channel_id=1, source_target_pairs={{0,96},{32,0},{64,32},{96,64},{128,224},{160,128},{192,160},{224,1... | collective-permute-start | bytes 1769480 | tf_op jit(solution)/shard_map/ppermute | solution.py:22
  52.7 8.7 %collective-permute-start.7 = (bf16[4,96,384]{2,1,0:T(8,128)(2,1)S(1)}, bf16[4,96,384]{2,1,0:T(8,128)(2,1)S(1)}, u32[]{:S(2)}, u32[]{:S(2)}) collective-permute-start(bf16[4,96,384]{2,1,0:T(8,128)(2,1)S(1)} %slice.96), channel_id=1, source_target_pairs={{0,32},{32,64},{64,96},{96,0},{128,160},{160,192},{192,224},{224,1... | collective-permute-start | bytes 884744 | tf_op jit(solution)/shard_map/ppermute | solution.py:22
  54.7 8.2 %collective-permute-start.8 = (bf16[4,96,384]{2,1,0:T(8,128)(2,1)S(1)}, bf16[4,96,384]{2,1,0:T(8,128)(2,1)S(1)}, u32[]{:S(2)}, u32[]{:S(2)}) collective-permute-start(bf16[4,96,384]{2,1,0:T(8,128)(2,1)S(1)} %slice.97), channel_id=1, source_target_pairs={{0,96},{32,0},{64,32},{96,64},{128,224},{160,128},{192,160},{224,1... | collective-permute-start | bytes 884744 | tf_op jit(solution)/shard_map/ppermute | solution.py:22
  66.6 91.5 %all-to-all-start = ((bf16[32,96,384]{2,1,0:T(8,128)(2,1)}), bf16[32,96,384]{2,1,0:T(8,128)(2,1)}, u32[]{:S(2)}, u32[]{:S(2)}) async-start(bf16[32,96,384]{2,1,0:T(8,128)(2,1)} %bitcast.27), calls=%async_computation | async-start | bytes 4718592 | tf_op jit(solution)/shard_map/all_to_all | solution.py:82
  147.2 10.7 %copy-start.7 = (s32[2,32]{1,0:T(2,128)S(1)}, s32[2,32]{1,0:T(2,128)}, u32[]{:S(2)}) copy-start(s32[2,32]{1,0:T(2,128)} %param.12) | copy-start | bytes 772
  147.2 10.7 %copy-start.5 = (f32[2,32,384]{2,1,0:T(8,128)S(1)}, f32[2,32,384]{2,1,0:T(8,128)}, u32[]{:S(2)}) copy-start(f32[2,32,384]{2,1,0:T(8,128)} %param.11) | copy-start | bytes 294916
  147.2 10.7 %copy-start.6 = (f32[2,32,384]{2,1,0:T(8,128)S(1)}, f32[2,32,384]{2,1,0:T(8,128)}, u32[]{:S(2)}) copy-start(f32[2,32,384]{2,1,0:T(8,128)} %param.10) | copy-start | bytes 294916
  150.5 11.8 %copy-start.1 = (bf16[32,2,48,384]{3,2,0,1:T(8,128)(2,1)S(1)}, bf16[32,2,48,384]{3,2,0,1:T(8,128)(2,1)}, u32[]{:S(2)}) copy-start(bf16[32,2,48,384]{3,2,0,1:T(8,128)(2,1)} %all-gather.3.cloned.1.call-done) | copy-start | bytes 7077892
  150.5 11.8 %collective-permute-start = (bf16[16,2,2,48,384]{4,3,0,1,2:T(8,128)(2,1)}, bf16[16,2,2,48,384]{4,3,0,1,2:T(8,128)(2,1)}, u32[]{:S(2)}, u32[]{:S(2)}) collective-permute-start(bf16[16,2,2,48,384]{4,3,0,1,2:T(8,128)(2,1)} %copy.33), channel_id=1, source_target_pairs={{0,1},{1,0},{2,3},{3,2},{4,5},{5,4},{6,7},{7,6},{8,9},{9,8},{10,11... | collective-permute-start | bytes 7077896 | tf_op jit(solution)/shard_map/ppermute | solution.py:60
  167.1 7.1 %copy-start.2 = (f32[1024,512]{1,0:T(8,128)S(1)}, f32[1024,512]{1,0:T(8,128)}, u32[]{:S(2)}) copy-start(f32[1024,512]{1,0:T(8,128)} %param.7) | copy-start | bytes 6291460
Sparse Core Ops, SparseCore 0:
  45.1 102.0 all-gather.2

commit v12 on v10

--- a/solution.py
+++ b/solution.py
@@ -60,13 +60,18 @@
 
     half = v_rows // 2
     d_own = lax.dynamic_slice_in_dim(d_inverse, column * half, half, 3)
-    d_own = d_own.transpose(1, 2, 0, 3)[:, :, :, None, :, None]
-    pairs = v_codes.reshape(panels, per_row, half, 2, rank_most)
-    even = pairs[..., 0, :].astype(jnp.float32)
-    odd = pairs[..., 1, :].astype(jnp.float32)
-    first = d_own[0, 0] * even + d_own[0, 1] * odd
-    second = d_own[1, 0] * even + d_own[1, 1] * odd
-    v_scaled = jnp.stack([first, second], axis=-2).reshape(v_codes.shape).astype(jnp.bfloat16)
+    d_own = jnp.repeat(d_own, 2, axis=3)
+    parity = lax.broadcasted_iota(jnp.int32, (v_rows,), 0) % 2
+    even_row = parity == 0
+    own_scale = jnp.where(even_row, d_own[:, 0, 0], d_own[:, 1, 1])
+    partner_scale = jnp.where(even_row, d_own[:, 0, 1], d_own[:, 1, 0])
+    codes = v_codes.astype(jnp.float32)
+    partner = jnp.where(
+        even_row[:, None], jnp.roll(codes, -1, axis=2), jnp.roll(codes, 1, axis=2)
+    )
+    v_scaled = (
+        own_scale[:, None, :, None] * codes + partner_scale[:, None, :, None] * partner
+    ).astype(jnp.bfloat16)
     col_shard = jnp.concatenate([u_codes, v_scaled], axis=2).transpose(1, 0, 2, 3)
 
     n_row = lax.axis_size("row")

time: 155 us -> 154 us (level)
  local copies, waits for them, and re-layouts: 4.71 us -> 2.94 us
  other arithmetic: 3.45 us -> 5.09 us
    convert_element_type x0 -> x2, other arithmetic: none -> 1.91 us  [the longest x1 1 us: local(): v_scaled = (own_scale[:, None, :, None] * codes + partner_scale[:, None,...]
    unnamed x16, local copies, waits for them, and re-layouts: 2.14 us -> 0.33 us
where the time goes in v12:
time: 154 us; the launch traced here: 153 us
  waiting for transfers between devices  71.6 us (46%)
  starting transfers between devices  50.2 us (33%)
  between operations  13.8 us (9%)
  matrix products  8.85 us (6%)
  other arithmetic  5.09 us (3%)
  local copies, waits for them, and re-layouts  2.94 us (2%)
    all_to_all x1, waiting for transfers between devices, local(): col_all = lax.all_to_all(every_tile, 'col', 0, 0, tiled=True)  55.3 us
    ppermute x8, starting transfers between devices, shift(): lax.ppermute(value, 'row', [(r, target(r, step)) for r in range(n_all)])  36.8 us
    ppermute x8, waiting for transfers between devices, shift(): lax.ppermute(value, 'row', [(r, target(r, step)) for r in range(n_all)])  16.3 us
    all_to_all x1, starting transfers between devices, local(): col_all = lax.all_to_all(every_tile, 'col', 0, 0, tiled=True)  13.4 us
    dot_general x1, matrix products, local(): jnp.einsum('cikbr,ckbq->kirq', row_v, col_scaled, preferred_element_type=...  3.74 us
  transfers between devices with their start and end apart: 10, of which 7 were waited for; matrix products, arithmetic and copies ran while one was open for 4% of the time, Pallas kernels for 0%

profile of v12, /device:TPU:1, one launch (start us, length us, event | category | flops | bytes accessed | tf_op | source)
XLA Modules:
  0.0 152.6 jit_solution(9243177704275336087)
XLA Ops:
  6.5 0.0 copy-start
  6.5 0.0 all-gather.3.cloned.1.call-start
  6.5 1.6 %copy_bitcast_fusion = bf16[2,2,48,384]{3,2,1,0:T(8,128)(2,1)} fusion(bf16[2,2,32,384]{3,2,1,0:T(8,128)(2,1)} %param.9, bf16[2,2,16,384]{3,2,1,0:T(8,128)(2,1)} %param.8), kind=kLoop, calls=%fused_computation.33 | loop fusion | flops 294912 | bytes 294912 | tf_op jit(solution)/shard_map/transpose | solution.py:55
  8.1 0.0 all-gather.3.cloned.1.call-update
  8.2 0.0 copy-done
  8.2 0.1 constant_dynamic-slice_fusion.1
  8.2 0.1 broadcast_in_dim.30
  8.3 0.1 reshape.117
  8.5 0.9 copy_convert_fusion
  9.4 1.0 fusion.13
  10.5 6.6 %collective-permute-start.1 = (bf16[192,384]{1,0:T(8,128)(2,1)S(1)}, bf16[192,384]{1,0:T(8,128)(2,1)S(1)}, u32[]{:S(2)}, u32[]{:S(2)}) collective-permute-start(bf16[192,384]{1,0:T(8,128)(2,1)S(1)} %bitcast.76), channel_id=1, source_target_pairs={{0,128},{32,160},{64,192},{96,224},{128,256},{160,288},{192,320},{... | collective-permute-start | bytes 442376 | tf_op jit(solution)/shard_map/ppermute | solution.py:22
  17.1 6.8 %collective-permute-start = (bf16[192,384]{1,0:T(8,128)(2,1)S(1)}, bf16[192,384]{1,0:T(8,128)(2,1)S(1)}, u32[]{:S(2)}, u32[]{:S(2)}) collective-permute-start(bf16[192,384]{1,0:T(8,128)(2,1)S(1)} %bitcast.77), channel_id=1, source_target_pairs={{0,384},{32,416},{64,448},{96,480},{128,0},{160,32},{192,64},{224,... | collective-permute-start | bytes 442376 | tf_op jit(solution)/shard_map/ppermute | solution.py:22
  23.9 1.1 collective-permute-done.1
  25.1 4.0 %collective-permute-start.2 = (bf16[96,384]{1,0:T(8,128)(2,1)S(1)}, bf16[96,384]{1,0:T(8,128)(2,1)S(1)}, u32[]{:S(2)}, u32[]{:S(2)}) collective-permute-start(bf16[96,384]{1,0:T(8,128)(2,1)S(1)} %slice.108), channel_id=1, source_target_pairs={{0,128},{32,160},{64,192},{96,224},{128,256},{160,288},{192,320},{... | collective-permute-start | bytes 221192 | tf_op jit(solution)/shard_map/ppermute | solution.py:22
  29.0 1.0 collective-permute-done
  30.0 5.1 %collective-permute-start.3 = (bf16[96,384]{1,0:T(8,128)(2,1)S(1)}, bf16[96,384]{1,0:T(8,128)(2,1)S(1)}, u32[]{:S(2)}, u32[]{:S(2)}) collective-permute-start(bf16[96,384]{1,0:T(8,128)(2,1)S(1)} %slice.109), channel_id=1, source_target_pairs={{0,384},{32,416},{64,448},{96,480},{128,0},{160,32},{192,64},{224,... | collective-permute-start | bytes 221192 | tf_op jit(solution)/shard_map/ppermute | solution.py:22
  35.1 0.0 collective-permute-done.2
  35.1 2.2 %collective-permute-done.3 = bf16[96,384]{1,0:T(8,128)(2,1)S(1)} collective-permute-done((bf16[96,384]{1,0:T(8,128)(2,1)S(1)}, bf16[96,384]{1,0:T(8,128)(2,1)S(1)}, u32[]{:S(2)}, u32[]{:S(2)}) %collective-permute-start.3) | collective-permute-done | bytes 73760 | tf_op jit(solution)/shard_map/ppermute | solution.py:22
  37.3 0.1 pad_maximum_fusion
  37.4 4.7 %collective-permute-start.5 = (bf16[4,192,384]{2,1,0:T(8,128)(2,1)S(1)}, bf16[4,192,384]{2,1,0:T(8,128)(2,1)S(1)}, u32[]{:S(2)}, u32[]{:S(2)}) collective-permute-start(bf16[4,192,384]{2,1,0:T(8,128)(2,1)S(1)} %pad_maximum_fusion), channel_id=1, source_target_pairs={{0,32},{32,64},{64,96},{96,0},{128,160},{160,192},{192,224},{224,1... | collective-permute-start | bytes 1769480 | tf_op jit(solution)/shard_map/ppermute | solution.py:22
  42.1 3.2 %collective-permute-start.4 = (bf16[4,192,384]{2,1,0:T(8,128)(2,1)S(1)}, bf16[4,192,384]{2,1,0:T(8,128)(2,1)S(1)}, u32[]{:S(2)}, u32[]{:S(2)}) collective-permute-start(bf16[4,192,384]{2,1,0:T(8,128)(2,1)S(1)} %pad_maximum_fusion), channel_id=1, source_target_pairs={{0,96},{32,0},{64,32},{96,64},{128,224},{160,128},{192,160},{224,1... | collective-permute-start | bytes 1769480 | tf_op jit(solution)/shard_map/ppermute | solution.py:22
  45.4 8.6 %collective-permute-done.5 = bf16[4,192,384]{2,1,0:T(8,128)(2,1)S(1)} collective-permute-done((bf16[4,192,384]{2,1,0:T(8,128)(2,1)S(1)}, bf16[4,192,384]{2,1,0:T(8,128)(2,1)S(1)}, u32[]{:S(2)}, u32[]{:S(2)}) %collective-permute-start.5) | collective-permute-done | bytes 589856 | tf_op jit(solution)/shard_map/ppermute | solution.py:22
  54.0 2.0 %collective-permute-start.6 = (bf16[4,96,384]{2,1,0:T(8,128)(2,1)S(1)}, bf16[4,96,384]{2,1,0:T(8,128)(2,1)S(1)}, u32[]{:S(2)}, u32[]{:S(2)}) collective-permute-start(bf16[4,96,384]{2,1,0:T(8,128)(2,1)S(1)} %slice.110), channel_id=1, source_target_pairs={{0,32},{32,64},{64,96},{96,0},{128,160},{160,192},{192,224},{224,1... | collective-permute-start | bytes 884744 | tf_op jit(solution)/shard_map/ppermute | solution.py:22
  55.9 0.0 collective-permute-done.4
  56.0 4.5 %collective-permute-start.7 = (bf16[4,96,384]{2,1,0:T(8,128)(2,1)S(1)}, bf16[4,96,384]{2,1,0:T(8,128)(2,1)S(1)}, u32[]{:S(2)}, u32[]{:S(2)}) collective-permute-start(bf16[4,96,384]{2,1,0:T(8,128)(2,1)S(1)} %slice.111), channel_id=1, source_target_pairs={{0,96},{32,0},{64,32},{96,64},{128,224},{160,128},{192,160},{224,1... | collective-permute-start | bytes 884744 | tf_op jit(solution)/shard_map/ppermute | solution.py:22
  60.5 0.1 bitcast_dynamic-update-slice_fusion.4
  60.6 0.1 bitcast_dynamic-update-slice_fusion.2
  60.7 1.9 %collective-permute-done.6 = bf16[4,96,384]{2,1,0:T(8,128)(2,1)S(1)} collective-permute-done((bf16[4,96,384]{2,1,0:T(8,128)(2,1)S(1)}, bf16[4,96,384]{2,1,0:T(8,128)(2,1)S(1)}, u32[]{:S(2)}, u32[]{:S(2)}) %collective-permute-start.6) | collective-permute-done | bytes 294944 | tf_op jit(solution)/shard_map/ppermute | solution.py:22
  62.7 1.5 %collective-permute-done.7 = bf16[4,96,384]{2,1,0:T(8,128)(2,1)S(1)} collective-permute-done((bf16[4,96,384]{2,1,0:T(8,128)(2,1)S(1)}, bf16[4,96,384]{2,1,0:T(8,128)(2,1)S(1)}, u32[]{:S(2)}, u32[]{:S(2)}) %collective-permute-start.7) | collective-permute-done | bytes 294944 | tf_op jit(solution)/shard_map/ppermute | solution.py:22
  64.2 0.1 fusion.9
  64.3 0.1 bitcast_dynamic-update-slice_fusion
  64.4 0.1 bitcast_dynamic-update-slice_fusion.5
  64.5 0.1 bitcast_dynamic-update-slice_fusion.3
  64.6 0.1 fusion.10
  64.7 0.1 bitcast_dynamic-update-slice_fusion.1
  64.8 0.3 constant_dynamic-slice_fusion
  65.1 1.0 fusion.3
  66.1 1.7 %copy.22 = bf16[4,4,192,384]{3,2,1,0:T(8,128)(2,1)} copy(bf16[4,4,192,384]{3,2,0,1:T(8,128)(2,1)S(1)} %fusion.3) | data formatting | bytes 4718592 | tf_op jit(solution)/shard_map/transpose | solution.py:42
  67.8 13.4 %all-to-all-start = ((bf16[32,96,384]{2,1,0:T(8,128)(2,1)}), bf16[32,96,384]{2,1,0:T(8,128)(2,1)S(1)}, u32[]{:S(2)}, u32[]{:S(2)}) async-start(bf16[32,96,384]{2,1,0:T(8,128)(2,1)} %bitcast.20), calls=%async_computation | async-start | bytes 4718592 | tf_op jit(solution)/shard_map/all_to_all | solution.py:81
  81.2 0.1 multiply_select_fusion
  81.3 55.3 %all-to-all-done = bf16[32,96,384]{2,1,0:T(8,128)(2,1)S(1)} async-done(((bf16[32,96,384]{2,1,0:T(8,128)(2,1)}), bf16[32,96,384]{2,1,0:T(8,128)(2,1)S(1)}, u32[]{:S(2)}, u32[]{:S(2)}) %all-to-all-start) | async-done | bytes 2359328 | tf_op jit(solution)/shard_map/all_to_all | solution.py:81
  136.6 0.1 slice_bitcast_fusion.2
  136.7 0.1 copy.24
  136.8 0.0 all-gather.3.cloned.1.call-done
  136.8 3.7 %fusion = f32[2,2,384,384,1]{3,2,1,0,4:T(8,128)S(1)} fusion(bf16[32,2,48,384]{3,2,1,0:T(8,128)(2,1)S(1)} %bitcast.74, bf16[32,2,2,48,384]{4,3,2,1,0:T(8,128)(2,1)} %bitcast.93), kind=kOutput, calls=%fused_computation.2 | convolution fusion | flops 1207959552 | bytes 7077888 | tf_op jit(solution)/shard_map/cikbr,ckbq->kirq/dot_general | solution.py:93
  140.6 0.0 copy-start.1
  140.6 2.8 %convolution_convert_fusion = bf16[2,2,32,16,384]{4,3,2,1,0:T(8,128)(2,1)S(1)} fusion(bf16[32,2,2,48,384]{4,3,2,1,0:T(8,128)(2,1)} %bitcast.94, f32[2,2,384,384,1]{3,2,1,0,4:T(8,128)S(1)} %fusion, f32[2,384]{1,0:T(2,128)S(1)} %bitcast.92, f32[2,2,384]{2,0,1:T(2,128)S(1)} %copy.19), kind=kOutput, calls=%fused_computation.10 | convolution fusion | flops 606535680 | bytes 5514240 | tf_op jit(solution)/shard_map/cikmr,kirq->kicmq/dot_general | solution.py:95
  143.4 2.3 %bitcast_subtract_fusion = f32[1024,512]{1,0:T(8,128)} fusion(f32[1024,512]{1,0:T(8,128)S(1)} %copy-done.1, bf16[1024,2,384]{2,0,1:T(8,128)(2,1)S(1)} %bitcast.87, bf16[2,512,384]{2,1,0:T(8,128)(2,1)S(1)} %bitcast.75), kind=kOutput, calls=%fused_computation.9 | convolution fusion | flops 805830656 | bytes 6553600 | tf_op jit(solution)/shard_map/kicmq,knq->icmn/dot_general | solution.py:97
  (25 shorter events, 0.2 us)
Async XLA Ops:
  6.5 1.6 %copy-start = (f32[2,2,2,512]{3,2,1,0:T(2,128)S(1)}, f32[2,2,2,512]{3,2,1,0:T(2,128)}, u32[]{:S(2)}) copy-start(f32[2,2,2,512]{3,2,1,0:T(2,128)} %param.13) | copy-start | bytes 49156
  6.5 3.9 %copy-start.2 = (bf16[2,2,16,384]{3,2,1,0:T(8,128)(2,1)S(1)}, bf16[2,2,16,384]{3,2,1,0:T(8,128)(2,1)}, u32[]{:S(2)}) copy-start(bf16[2,2,16,384]{3,2,1,0:T(8,128)(2,1)} %param.8) | copy-start | bytes 147460
  6.5 130.3 %all-gather.3.cloned.1.call-start = ((), (), s32[]{:S(2)}) async-start(), calls=%async_computation.1 | async-start | bytes 4866048 | tf_op jit(solution)/shard_map/all_gather | solution.py:57
  10.5 14.5 %collective-permute-start.1 = (bf16[192,384]{1,0:T(8,128)(2,1)S(1)}, bf16[192,384]{1,0:T(8,128)(2,1)S(1)}, u32[]{:S(2)}, u32[]{:S(2)}) collective-permute-start(bf16[192,384]{1,0:T(8,128)(2,1)S(1)} %bitcast.76), channel_id=1, source_target_pairs={{0,128},{32,160},{64,192},{96,224},{128,256},{160,288},{192,320},{... | collective-permute-start | bytes 442376 | tf_op jit(solution)/shard_map/ppermute | solution.py:22
  17.1 12.9 %collective-permute-start = (bf16[192,384]{1,0:T(8,128)(2,1)S(1)}, bf16[192,384]{1,0:T(8,128)(2,1)S(1)}, u32[]{:S(2)}, u32[]{:S(2)}) collective-permute-start(bf16[192,384]{1,0:T(8,128)(2,1)S(1)} %bitcast.77), channel_id=1, source_target_pairs={{0,384},{32,416},{64,448},{96,480},{128,0},{160,32},{192,64},{224,... | collective-permute-start | bytes 442376 | tf_op jit(solution)/shard_map/ppermute | solution.py:22
  25.1 10.1 %collective-permute-start.2 = (bf16[96,384]{1,0:T(8,128)(2,1)S(1)}, bf16[96,384]{1,0:T(8,128)(2,1)S(1)}, u32[]{:S(2)}, u32[]{:S(2)}) collective-permute-start(bf16[96,384]{1,0:T(8,128)(2,1)S(1)} %slice.108), channel_id=1, source_target_pairs={{0,128},{32,160},{64,192},{96,224},{128,256},{160,288},{192,320},{... | collective-permute-start | bytes 221192 | tf_op jit(solution)/shard_map/ppermute | solution.py:22
  30.0 7.3 %collective-permute-start.3 = (bf16[96,384]{1,0:T(8,128)(2,1)S(1)}, bf16[96,384]{1,0:T(8,128)(2,1)S(1)}, u32[]{:S(2)}, u32[]{:S(2)}) collective-permute-start(bf16[96,384]{1,0:T(8,128)(2,1)S(1)} %slice.109), channel_id=1, source_target_pairs={{0,384},{32,416},{64,448},{96,480},{128,0},{160,32},{192,64},{224,... | collective-permute-start | bytes 221192 | tf_op jit(solution)/shard_map/ppermute | solution.py:22
  37.4 16.5 %collective-permute-start.5 = (bf16[4,192,384]{2,1,0:T(8,128)(2,1)S(1)}, bf16[4,192,384]{2,1,0:T(8,128)(2,1)S(1)}, u32[]{:S(2)}, u32[]{:S(2)}) collective-permute-start(bf16[4,192,384]{2,1,0:T(8,128)(2,1)S(1)} %pad_maximum_fusion), channel_id=1, source_target_pairs={{0,32},{32,64},{64,96},{96,0},{128,160},{160,192},{192,224},{224,1... | collective-permute-start | bytes 1769480 | tf_op jit(solution)/shard_map/ppermute | solution.py:22
  42.1 13.8 %collective-permute-start.4 = (bf16[4,192,384]{2,1,0:T(8,128)(2,1)S(1)}, bf16[4,192,384]{2,1,0:T(8,128)(2,1)S(1)}, u32[]{:S(2)}, u32[]{:S(2)}) collective-permute-start(bf16[4,192,384]{2,1,0:T(8,128)(2,1)S(1)} %pad_maximum_fusion), channel_id=1, source_target_pairs={{0,96},{32,0},{64,32},{96,64},{128,224},{160,128},{192,160},{224,1... | collective-permute-start | bytes 1769480 | tf_op jit(solution)/shard_map/ppermute | solution.py:22
  54.0 8.7 %collective-permute-start.6 = (bf16[4,96,384]{2,1,0:T(8,128)(2,1)S(1)}, bf16[4,96,384]{2,1,0:T(8,128)(2,1)S(1)}, u32[]{:S(2)}, u32[]{:S(2)}) collective-permute-start(bf16[4,96,384]{2,1,0:T(8,128)(2,1)S(1)} %slice.110), channel_id=1, source_target_pairs={{0,32},{32,64},{64,96},{96,0},{128,160},{160,192},{192,224},{224,1... | collective-permute-start | bytes 884744 | tf_op jit(solution)/shard_map/ppermute | solution.py:22
  56.0 8.2 %collective-permute-start.7 = (bf16[4,96,384]{2,1,0:T(8,128)(2,1)S(1)}, bf16[4,96,384]{2,1,0:T(8,128)(2,1)S(1)}, u32[]{:S(2)}, u32[]{:S(2)}) collective-permute-start(bf16[4,96,384]{2,1,0:T(8,128)(2,1)S(1)} %slice.111), channel_id=1, source_target_pairs={{0,96},{32,0},{64,32},{96,64},{128,224},{160,128},{192,160},{224,1... | collective-permute-start | bytes 884744 | tf_op jit(solution)/shard_map/ppermute | solution.py:22
  67.8 13.4 %copy-start.5 = (s32[2,32]{1,0:T(2,128)S(1)}, s32[2,32]{1,0:T(2,128)}, u32[]{:S(2)}) copy-start(s32[2,32]{1,0:T(2,128)} %param.12) | copy-start | bytes 772
  67.8 13.4 %copy-start.3 = (f32[2,32,384]{2,1,0:T(8,128)S(1)}, f32[2,32,384]{2,1,0:T(8,128)}, u32[]{:S(2)}) copy-start(f32[2,32,384]{2,1,0:T(8,128)} %param.11) | copy-start | bytes 294916
  67.8 13.4 %copy-start.4 = (f32[2,32,384]{2,1,0:T(8,128)S(1)}, f32[2,32,384]{2,1,0:T(8,128)}, u32[]{:S(2)}) copy-start(f32[2,32,384]{2,1,0:T(8,128)} %param.10) | copy-start | bytes 294916
  67.8 68.8 %all-to-all-start = ((bf16[32,96,384]{2,1,0:T(8,128)(2,1)}), bf16[32,96,384]{2,1,0:T(8,128)(2,1)S(1)}, u32[]{:S(2)}, u32[]{:S(2)}) async-start(bf16[32,96,384]{2,1,0:T(8,128)(2,1)} %bitcast.20), calls=%async_computation | async-start | bytes 4718592 | tf_op jit(solution)/shard_map/all_to_all | solution.py:81
  140.6 2.8 %copy-start.1 = (f32[1024,512]{1,0:T(8,128)S(1)}, f32[1024,512]{1,0:T(8,128)}, u32[]{:S(2)}) copy-start(f32[1024,512]{1,0:T(8,128)} %param.7) | copy-start | bytes 6291460
Sparse Core Ops, SparseCore 0:
  9.5 76.5 all-gather.2

commit v13 on v12

--- a/solution.py
+++ b/solution.py
@@ -25,6 +25,8 @@
         return jnp.stack([block] + [shift(block, -d) for d in range(1, 4)])
     from_behind = shift(block, 1)
     from_ahead = shift(block, -1)
+    if forward == "whole":
+        return jnp.stack([block, from_ahead, shift(from_behind, 1), from_behind])
     half = block.shape[-2] // 2
     far = jnp.concatenate(
         [shift(from_behind[..., :half, :], 1), shift(from_ahead[..., half:, :], -1)], axis=-2
@@ -37,7 +39,7 @@
     n_z = n_row // n_x
     row = lax.axis_index("row")
     z, x = row // n_x, row % n_x
-    by_z = ring_gather(block, n_z, n_x, outer=True)
+    by_z = ring_gather(block, n_z, n_x, outer=True, forward="whole")
     by_xz = ring_gather(by_z, n_z, n_x, outer=False)
     by_zx = jnp.roll(jnp.roll(by_xz, x, axis=0), z, axis=1).swapaxes(0, 1)
     return by_zx.reshape((n_row,) + block.shape)

time: 154 us -> 155 us (level)
    ppermute x8 -> x7, waiting for transfers between devices: 16.3 us -> 16.8 us  [shift(): lax.ppermute(value, 'row', [(r, target(r, step)) for r in range(n_all)])]
    ppermute x8 -> x7, starting transfers between devices: 36.8 us -> 37.2 us  [shift(): lax.ppermute(value, 'row', [(r, target(r, step)) for r in range(n_all)])]
  transfers between devices with their start and end apart: 10 -> 9, of which waited for: 7 -> 7; matrix products, arithmetic and copies ran while one was open for 4% -> 4% of each run, Pallas kernels for 0% -> 0%
where the time goes in v13:
time: 155 us; the launch traced here: 154 us
  waiting for transfers between devices  72.2 us (47%)
  starting transfers between devices  51 us (33%)
  between operations  13.8 us (9%)
  matrix products  8.85 us (6%)
  other arithmetic  5.08 us (3%)
  local copies, waits for them, and re-layouts  2.93 us (2%)
    all_to_all x1, waiting for transfers between devices, local(): col_all = lax.all_to_all(every_tile, 'col', 0, 0, tiled=True)  55.3 us
    ppermute x7, starting transfers between devices, shift(): lax.ppermute(value, 'row', [(r, target(r, step)) for r in range(n_all)])  37.2 us
    ppermute x7, waiting for transfers between devices, shift(): lax.ppermute(value, 'row', [(r, target(r, step)) for r in range(n_all)])  16.8 us
    all_to_all x1, starting transfers between devices, local(): col_all = lax.all_to_all(every_tile, 'col', 0, 0, tiled=True)  13.8 us
    dot_general x1, matrix products, local(): jnp.einsum('cikbr,ckbq->kirq', row_v, col_scaled, preferred_element_type=...  3.75 us
  transfers between devices with their start and end apart: 9, of which 7 were waited for; matrix products, arithmetic and copies ran while one was open for 4% of the time, Pallas kernels for 0%

profile of v13, /device:TPU:1, one launch (start us, length us, event | category | flops | bytes accessed | tf_op | source)
XLA Modules:
  0.0 153.9 jit_solution(6178853891791425099)
XLA Ops:
  6.5 0.0 copy-start
  6.5 0.0 all-gather.3.cloned.1.call-start
  6.5 1.6 %copy_bitcast_fusion = bf16[2,2,48,384]{3,2,1,0:T(8,128)(2,1)} fusion(bf16[2,2,32,384]{3,2,1,0:T(8,128)(2,1)} %param.9, bf16[2,2,16,384]{3,2,1,0:T(8,128)(2,1)} %param.8), kind=kLoop, calls=%fused_computation.32 | loop fusion | flops 294912 | bytes 294912 | tf_op jit(solution)/shard_map/transpose | solution.py:57
  8.1 0.0 all-gather.3.cloned.1.call-update
  8.2 0.0 copy-done
  8.2 0.1 constant_dynamic-slice_fusion.1
  8.2 0.1 broadcast_in_dim.30
  8.3 0.1 reshape.117
  8.5 0.9 copy_convert_fusion
  9.4 1.0 fusion.13
  10.5 0.0 copy-done.2
  10.5 6.6 %collective-permute-start.1 = (bf16[192,384]{1,0:T(8,128)(2,1)S(1)}, bf16[192,384]{1,0:T(8,128)(2,1)S(1)}, u32[]{:S(2)}, u32[]{:S(2)}) collective-permute-start(bf16[192,384]{1,0:T(8,128)(2,1)S(1)} %bitcast.75), channel_id=1, source_target_pairs={{0,128},{32,160},{64,192},{96,224},{128,256},{160,288},{192,320},{... | collective-permute-start | bytes 442376 | tf_op jit(solution)/shard_map/ppermute | solution.py:22
  17.1 6.8 %collective-permute-start = (bf16[192,384]{1,0:T(8,128)(2,1)S(1)}, bf16[192,384]{1,0:T(8,128)(2,1)S(1)}, u32[]{:S(2)}, u32[]{:S(2)}) collective-permute-start(bf16[192,384]{1,0:T(8,128)(2,1)S(1)} %bitcast.76), channel_id=1, source_target_pairs={{0,384},{32,416},{64,448},{96,480},{128,0},{160,32},{192,64},{224,... | collective-permute-start | bytes 442376 | tf_op jit(solution)/shard_map/ppermute | solution.py:22
  23.9 1.1 collective-permute-done.1
  25.0 3.9 %collective-permute-start.2 = (bf16[192,384]{1,0:T(8,128)(2,1)S(1)}, bf16[192,384]{1,0:T(8,128)(2,1)S(1)}, u32[]{:S(2)}, u32[]{:S(2)}) collective-permute-start(bf16[192,384]{1,0:T(8,128)(2,1)S(1)} %collective-permute-done.1), channel_id=1, source_target_pairs={{0,128},{32,160},{64,192},{96,224},{128,256},{160,288},{192,320},{... | collective-permute-start | bytes 442376 | tf_op jit(solution)/shard_map/ppermute | solution.py:22
  29.0 1.0 collective-permute-done
  30.0 3.2 %collective-permute-done.2 = bf16[192,384]{1,0:T(8,128)(2,1)S(1)} collective-permute-done((bf16[192,384]{1,0:T(8,128)(2,1)S(1)}, bf16[192,384]{1,0:T(8,128)(2,1)S(1)}, u32[]{:S(2)}, u32[]{:S(2)}) %collective-permute-start.2) | collective-permute-done | bytes 147488 | tf_op jit(solution)/shard_map/ppermute | solution.py:22
  33.2 0.1 pad_maximum_fusion
  33.3 10.0 %collective-permute-start.4 = (bf16[4,192,384]{2,1,0:T(8,128)(2,1)S(1)}, bf16[4,192,384]{2,1,0:T(8,128)(2,1)S(1)}, u32[]{:S(2)}, u32[]{:S(2)}) collective-permute-start(bf16[4,192,384]{2,1,0:T(8,128)(2,1)S(1)} %pad_maximum_fusion), channel_id=1, source_target_pairs={{0,32},{32,64},{64,96},{96,0},{128,160},{160,192},{192,224},{224,1... | collective-permute-start | bytes 1769480 | tf_op jit(solution)/shard_map/ppermute | solution.py:22
  43.3 3.3 %collective-permute-start.3 = (bf16[4,192,384]{2,1,0:T(8,128)(2,1)S(1)}, bf16[4,192,384]{2,1,0:T(8,128)(2,1)S(1)}, u32[]{:S(2)}, u32[]{:S(2)}) collective-permute-start(bf16[4,192,384]{2,1,0:T(8,128)(2,1)S(1)} %pad_maximum_fusion), channel_id=1, source_target_pairs={{0,96},{32,0},{64,32},{96,64},{128,224},{160,128},{192,160},{224,1... | collective-permute-start | bytes 1769480 | tf_op jit(solution)/shard_map/ppermute | solution.py:22
  46.7 8.1 %collective-permute-done.4 = bf16[4,192,384]{2,1,0:T(8,128)(2,1)S(1)} collective-permute-done((bf16[4,192,384]{2,1,0:T(8,128)(2,1)S(1)}, bf16[4,192,384]{2,1,0:T(8,128)(2,1)S(1)}, u32[]{:S(2)}, u32[]{:S(2)}) %collective-permute-start.4) | collective-permute-done | bytes 589856 | tf_op jit(solution)/shard_map/ppermute | solution.py:22
  54.8 1.9 %collective-permute-start.5 = (bf16[4,96,384]{2,1,0:T(8,128)(2,1)S(1)}, bf16[4,96,384]{2,1,0:T(8,128)(2,1)S(1)}, u32[]{:S(2)}, u32[]{:S(2)}) collective-permute-start(bf16[4,96,384]{2,1,0:T(8,128)(2,1)S(1)} %slice.100), channel_id=1, source_target_pairs={{0,32},{32,64},{64,96},{96,0},{128,160},{160,192},{192,224},{224,1... | collective-permute-start | bytes 884744 | tf_op jit(solution)/shard_map/ppermute | solution.py:22
  56.7 0.0 collective-permute-done.3
  56.8 4.6 %collective-permute-start.6 = (bf16[4,96,384]{2,1,0:T(8,128)(2,1)S(1)}, bf16[4,96,384]{2,1,0:T(8,128)(2,1)S(1)}, u32[]{:S(2)}, u32[]{:S(2)}) collective-permute-start(bf16[4,96,384]{2,1,0:T(8,128)(2,1)S(1)} %slice.101), channel_id=1, source_target_pairs={{0,96},{32,0},{64,32},{96,64},{128,224},{160,128},{192,160},{224,1... | collective-permute-start | bytes 884744 | tf_op jit(solution)/shard_map/ppermute | solution.py:22
  61.4 0.1 bitcast_dynamic-update-slice_fusion.4
  61.4 0.1 bitcast_dynamic-update-slice_fusion.2
  61.6 1.9 %collective-permute-done.5 = bf16[4,96,384]{2,1,0:T(8,128)(2,1)S(1)} collective-permute-done((bf16[4,96,384]{2,1,0:T(8,128)(2,1)S(1)}, bf16[4,96,384]{2,1,0:T(8,128)(2,1)S(1)}, u32[]{:S(2)}, u32[]{:S(2)}) %collective-permute-start.5) | collective-permute-done | bytes 294944 | tf_op jit(solution)/shard_map/ppermute | solution.py:22
  63.5 1.5 collective-permute-done.6
  65.0 0.1 fusion.9
  65.1 0.1 bitcast_dynamic-update-slice_fusion
  65.2 0.1 bitcast_dynamic-update-slice_fusion.5
  65.3 0.1 bitcast_dynamic-update-slice_fusion.3
  65.4 0.1 fusion.10
  65.6 0.1 bitcast_dynamic-update-slice_fusion.1
  65.7 0.3 constant_dynamic-slice_fusion
  65.9 1.0 fusion.3
  66.9 1.7 %copy.22 = bf16[4,4,192,384]{3,2,1,0:T(8,128)(2,1)} copy(bf16[4,4,192,384]{3,2,0,1:T(8,128)(2,1)S(1)} %fusion.3) | data formatting | bytes 4718592 | tf_op jit(solution)/shard_map/transpose | solution.py:44
  68.6 13.8 %all-to-all-start = ((bf16[32,96,384]{2,1,0:T(8,128)(2,1)}), bf16[32,96,384]{2,1,0:T(8,128)(2,1)S(1)}, u32[]{:S(2)}, u32[]{:S(2)}) async-start(bf16[32,96,384]{2,1,0:T(8,128)(2,1)} %bitcast.20), calls=%async_computation | async-start | bytes 4718592 | tf_op jit(solution)/shard_map/all_to_all | solution.py:83
  82.5 0.0 copy-done.5
  82.5 0.1 multiply_select_fusion
  82.6 55.3 %all-to-all-done = bf16[32,96,384]{2,1,0:T(8,128)(2,1)S(1)} async-done(((bf16[32,96,384]{2,1,0:T(8,128)(2,1)}), bf16[32,96,384]{2,1,0:T(8,128)(2,1)S(1)}, u32[]{:S(2)}, u32[]{:S(2)}) %all-to-all-start) | async-done | bytes 2359328 | tf_op jit(solution)/shard_map/all_to_all | solution.py:83
  138.0 0.1 slice_bitcast_fusion.2
  138.1 0.1 copy.24
  138.1 0.0 all-gather.3.cloned.1.call-done
  138.2 3.7 %fusion = f32[2,2,384,384,1]{3,2,1,0,4:T(8,128)S(1)} fusion(bf16[32,2,48,384]{3,2,1,0:T(8,128)(2,1)S(1)} %bitcast.73, bf16[32,2,2,48,384]{4,3,2,1,0:T(8,128)(2,1)} %bitcast.95), kind=kOutput, calls=%fused_computation.2 | convolution fusion | flops 1207959552 | bytes 7077888 | tf_op jit(solution)/shard_map/cikbr,ckbq->kirq/dot_general | solution.py:95
  141.9 0.0 copy-start.1
  141.9 2.8 %convolution_convert_fusion = bf16[2,2,32,16,384]{4,3,2,1,0:T(8,128)(2,1)S(1)} fusion(bf16[32,2,2,48,384]{4,3,2,1,0:T(8,128)(2,1)} %bitcast.96, f32[2,2,384,384,1]{3,2,1,0,4:T(8,128)S(1)} %fusion, f32[2,384]{1,0:T(2,128)S(1)} %bitcast.94, f32[2,2,384]{2,0,1:T(2,128)S(1)} %copy.19), kind=kOutput, calls=%fused_computation.10 | convolution fusion | flops 606535680 | bytes 5514240 | tf_op jit(solution)/shard_map/cikmr,kirq->kicmq/dot_general | solution.py:97
  144.7 2.3 %bitcast_subtract_fusion = f32[1024,512]{1,0:T(8,128)} fusion(f32[1024,512]{1,0:T(8,128)S(1)} %copy-done.1, bf16[1024,2,384]{2,0,1:T(8,128)(2,1)S(1)} %bitcast.80, bf16[2,512,384]{2,1,0:T(8,128)(2,1)S(1)} %bitcast.74), kind=kOutput, calls=%fused_computation.9 | convolution fusion | flops 805830656 | bytes 6553600 | tf_op jit(solution)/shard_map/kicmq,knq->icmn/dot_general | solution.py:99
  (20 shorter events, 0.2 us)
Async XLA Ops:
  6.5 1.6 %copy-start = (f32[2,2,2,512]{3,2,1,0:T(2,128)S(1)}, f32[2,2,2,512]{3,2,1,0:T(2,128)}, u32[]{:S(2)}) copy-start(f32[2,2,2,512]{3,2,1,0:T(2,128)} %param.13) | copy-start | bytes 49156
  6.5 3.9 %copy-start.2 = (bf16[2,2,16,384]{3,2,1,0:T(8,128)(2,1)S(1)}, bf16[2,2,16,384]{3,2,1,0:T(8,128)(2,1)}, u32[]{:S(2)}) copy-start(bf16[2,2,16,384]{3,2,1,0:T(8,128)(2,1)} %param.8) | copy-start | bytes 147460
  6.5 131.6 %all-gather.3.cloned.1.call-start = ((), (), s32[]{:S(2)}) async-start(), calls=%async_computation.1 | async-start | bytes 4866048 | tf_op jit(solution)/shard_map/all_gather | solution.py:59
  10.5 14.5 %collective-permute-start.1 = (bf16[192,384]{1,0:T(8,128)(2,1)S(1)}, bf16[192,384]{1,0:T(8,128)(2,1)S(1)}, u32[]{:S(2)}, u32[]{:S(2)}) collective-permute-start(bf16[192,384]{1,0:T(8,128)(2,1)S(1)} %bitcast.75), channel_id=1, source_target_pairs={{0,128},{32,160},{64,192},{96,224},{128,256},{160,288},{192,320},{... | collective-permute-start | bytes 442376 | tf_op jit(solution)/shard_map/ppermute | solution.py:22
  17.1 12.9 %collective-permute-start = (bf16[192,384]{1,0:T(8,128)(2,1)S(1)}, bf16[192,384]{1,0:T(8,128)(2,1)S(1)}, u32[]{:S(2)}, u32[]{:S(2)}) collective-permute-start(bf16[192,384]{1,0:T(8,128)(2,1)S(1)} %bitcast.76), channel_id=1, source_target_pairs={{0,384},{32,416},{64,448},{96,480},{128,0},{160,32},{192,64},{224,... | collective-permute-start | bytes 442376 | tf_op jit(solution)/shard_map/ppermute | solution.py:22
  25.0 8.1 %collective-permute-start.2 = (bf16[192,384]{1,0:T(8,128)(2,1)S(1)}, bf16[192,384]{1,0:T(8,128)(2,1)S(1)}, u32[]{:S(2)}, u32[]{:S(2)}) collective-permute-start(bf16[192,384]{1,0:T(8,128)(2,1)S(1)} %collective-permute-done.1), channel_id=1, source_target_pairs={{0,128},{32,160},{64,192},{96,224},{128,256},{160,288},{192,320},{... | collective-permute-start | bytes 442376 | tf_op jit(solution)/shard_map/ppermute | solution.py:22
  33.3 21.5 %collective-permute-start.4 = (bf16[4,192,384]{2,1,0:T(8,128)(2,1)S(1)}, bf16[4,192,384]{2,1,0:T(8,128)(2,1)S(1)}, u32[]{:S(2)}, u32[]{:S(2)}) collective-permute-start(bf16[4,192,384]{2,1,0:T(8,128)(2,1)S(1)} %pad_maximum_fusion), channel_id=1, source_target_pairs={{0,32},{32,64},{64,96},{96,0},{128,160},{160,192},{192,224},{224,1... | collective-permute-start | bytes 1769480 | tf_op jit(solution)/shard_map/ppermute | solution.py:22
  43.3 13.4 %collective-permute-start.3 = (bf16[4,192,384]{2,1,0:T(8,128)(2,1)S(1)}, bf16[4,192,384]{2,1,0:T(8,128)(2,1)S(1)}, u32[]{:S(2)}, u32[]{:S(2)}) collective-permute-start(bf16[4,192,384]{2,1,0:T(8,128)(2,1)S(1)} %pad_maximum_fusion), channel_id=1, source_target_pairs={{0,96},{32,0},{64,32},{96,64},{128,224},{160,128},{192,160},{224,1... | collective-permute-start | bytes 1769480 | tf_op jit(solution)/shard_map/ppermute | solution.py:22
  54.8 8.7 %collective-permute-start.5 = (bf16[4,96,384]{2,1,0:T(8,128)(2,1)S(1)}, bf16[4,96,384]{2,1,0:T(8,128)(2,1)S(1)}, u32[]{:S(2)}, u32[]{:S(2)}) collective-permute-start(bf16[4,96,384]{2,1,0:T(8,128)(2,1)S(1)} %slice.100), channel_id=1, source_target_pairs={{0,32},{32,64},{64,96},{96,0},{128,160},{160,192},{192,224},{224,1... | collective-permute-start | bytes 884744 | tf_op jit(solution)/shard_map/ppermute | solution.py:22
  56.8 8.2 %collective-permute-start.6 = (bf16[4,96,384]{2,1,0:T(8,128)(2,1)S(1)}, bf16[4,96,384]{2,1,0:T(8,128)(2,1)S(1)}, u32[]{:S(2)}, u32[]{:S(2)}) collective-permute-start(bf16[4,96,384]{2,1,0:T(8,128)(2,1)S(1)} %slice.101), channel_id=1, source_target_pairs={{0,96},{32,0},{64,32},{96,64},{128,224},{160,128},{192,160},{224,1... | collective-permute-start | bytes 884744 | tf_op jit(solution)/shard_map/ppermute | solution.py:22
  68.6 13.8 %copy-start.5 = (s32[2,32]{1,0:T(2,128)S(1)}, s32[2,32]{1,0:T(2,128)}, u32[]{:S(2)}) copy-start(s32[2,32]{1,0:T(2,128)} %param.12) | copy-start | bytes 772
  68.6 13.9 %copy-start.3 = (f32[2,32,384]{2,1,0:T(8,128)S(1)}, f32[2,32,384]{2,1,0:T(8,128)}, u32[]{:S(2)}) copy-start(f32[2,32,384]{2,1,0:T(8,128)} %param.11) | copy-start | bytes 294916
  68.6 13.9 %copy-start.4 = (f32[2,32,384]{2,1,0:T(8,128)S(1)}, f32[2,32,384]{2,1,0:T(8,128)}, u32[]{:S(2)}) copy-start(f32[2,32,384]{2,1,0:T(8,128)} %param.10) | copy-start | bytes 294916
  68.6 69.3 %all-to-all-start = ((bf16[32,96,384]{2,1,0:T(8,128)(2,1)}), bf16[32,96,384]{2,1,0:T(8,128)(2,1)S(1)}, u32[]{:S(2)}, u32[]{:S(2)}) async-start(bf16[32,96,384]{2,1,0:T(8,128)(2,1)} %bitcast.20), calls=%async_computation | async-start | bytes 4718592 | tf_op jit(solution)/shard_map/all_to_all | solution.py:83
  141.9 2.8 %copy-start.1 = (f32[1024,512]{1,0:T(8,128)S(1)}, f32[1024,512]{1,0:T(8,128)}, u32[]{:S(2)}) copy-start(f32[1024,512]{1,0:T(8,128)} %param.7) | copy-start | bytes 6291460
Sparse Core Ops, SparseCore 0:
  9.5 76.4 all-gather.2

commit v14 on v12

--- a/solution.py
+++ b/solution.py
@@ -52,7 +52,7 @@
     tile_order = n_col * u_rows
     both = u_rows + v_rows
 
-    shard = jnp.concatenate([u_codes, v_codes], axis=2).transpose(1, 0, 2, 3)
+    shard = jnp.concatenate([u_codes, v_codes], axis=2)
 
     row_all = lax.all_gather(shard, "col", axis=0, tiled=False)
     row_u = row_all[:, :, :, :u_rows]
@@ -90,9 +90,9 @@
     col_weight = lax.dynamic_index_in_dim(weight, column, 1, keepdims=False)
 
     col_scaled = col_v
-    inner = jnp.einsum("cikbr,ckbq->kirq", row_v, col_scaled, preferred_element_type=jnp.float32)
+    inner = jnp.einsum("ckibr,ckbq->kirq", row_v, col_scaled, preferred_element_type=jnp.float32)
     core = (row_weight[:, :, :, None] * inner * col_weight[:, None, None, :]).astype(jnp.bfloat16)
-    left = jnp.einsum("cikmr,kirq->kicmq", row_u, core, preferred_element_type=jnp.float32)
+    left = jnp.einsum("ckimr,kirq->kicmq", row_u, core, preferred_element_type=jnp.float32)
     left = left.astype(jnp.bfloat16)
     update = jnp.einsum("kicmq,knq->icmn", left, col_u, preferred_element_type=jnp.float32)
     return slab - update.reshape(slab.shape)

time: 154 us -> 154 us (level)
    concatenate x0 -> x1, other arithmetic: none -> 1.59 us  [local(): shard = jnp.concatenate([u_codes, v_codes], axis=2)]
    transpose x1 -> x0, other arithmetic: 1.59 us -> none  [local(): shard = jnp.concatenate([u_codes, v_codes], axis=2).transpose(1, 0, 2, 3)]
where the time goes in v14:
time: 154 us; the launch traced here: 153 us
  waiting for transfers between devices  71.6 us (46%)
  starting transfers between devices  50.2 us (33%)
  between operations  13.8 us (9%)
  matrix products  8.85 us (6%)
  other arithmetic  5.09 us (3%)
  local copies, waits for them, and re-layouts  2.94 us (2%)
    all_to_all x1, waiting for transfers between devices, local(): col_all = lax.all_to_all(every_tile, 'col', 0, 0, tiled=True)  55.3 us
    ppermute x8, starting transfers between devices, shift(): lax.ppermute(value, 'row', [(r, target(r, step)) for r in range(n_all)])  36.8 us
    ppermute x8, waiting for transfers between devices, shift(): lax.ppermute(value, 'row', [(r, target(r, step)) for r in range(n_all)])  16.3 us
    all_to_all x1, starting transfers between devices, local(): col_all = lax.all_to_all(every_tile, 'col', 0, 0, tiled=True)  13.4 us
    dot_general x1, matrix products, local(): jnp.einsum('ckibr,ckbq->kirq', row_v, col_scaled, preferred_element_type=...  3.74 us
  transfers between devices with their start and end apart: 10, of which 7 were waited for; matrix products, arithmetic and copies ran while one was open for 4% of the time, Pallas kernels for 0%

profile of v14, /device:TPU:1, one launch (start us, length us, event | category | flops | bytes accessed | tf_op | source)
XLA Modules:
  0.0 152.6 jit_solution(13620025386668787476)
XLA Ops:
  6.5 1.6 %pad_maximum_fusion.1 = bf16[2,2,48,384]{3,2,1,0:T(8,128)(2,1)} fusion(bf16[2,2,32,384]{3,2,1,0:T(8,128)(2,1)} %param.9, bf16[2,2,16,384]{3,2,1,0:T(8,128)(2,1)} %param.8), kind=kLoop, calls=%fused_computation.30 | loop fusion | flops 294912 | bytes 294912 | tf_op jit(solution)/shard_map/concatenate | solution.py:55
  8.1 0.0 all-gather.3.cloned.1.call-update
  8.2 0.0 copy-done
  8.2 0.1 constant_dynamic-slice_fusion.1
  8.2 0.1 broadcast_in_dim.30
  8.3 0.1 reshape.117
  8.5 0.9 copy_convert_fusion
  9.4 1.0 fusion.13
  10.5 6.6 %collective-permute-start.1 = (bf16[192,384]{1,0:T(8,128)(2,1)S(1)}, bf16[192,384]{1,0:T(8,128)(2,1)S(1)}, u32[]{:S(2)}, u32[]{:S(2)}) collective-permute-start(bf16[192,384]{1,0:T(8,128)(2,1)S(1)} %bitcast.74), channel_id=1, source_target_pairs={{0,128},{32,160},{64,192},{96,224},{128,256},{160,288},{192,320},{... | collective-permute-start | bytes 442376 | tf_op jit(solution)/shard_map/ppermute | solution.py:22
  17.1 6.8 %collective-permute-start = (bf16[192,384]{1,0:T(8,128)(2,1)S(1)}, bf16[192,384]{1,0:T(8,128)(2,1)S(1)}, u32[]{:S(2)}, u32[]{:S(2)}) collective-permute-start(bf16[192,384]{1,0:T(8,128)(2,1)S(1)} %bitcast.75), channel_id=1, source_target_pairs={{0,384},{32,416},{64,448},{96,480},{128,0},{160,32},{192,64},{224,... | collective-permute-start | bytes 442376 | tf_op jit(solution)/shard_map/ppermute | solution.py:22
  23.9 1.1 collective-permute-done.1
  25.1 4.0 %collective-permute-start.2 = (bf16[96,384]{1,0:T(8,128)(2,1)S(1)}, bf16[96,384]{1,0:T(8,128)(2,1)S(1)}, u32[]{:S(2)}, u32[]{:S(2)}) collective-permute-start(bf16[96,384]{1,0:T(8,128)(2,1)S(1)} %slice.108), channel_id=1, source_target_pairs={{0,128},{32,160},{64,192},{96,224},{128,256},{160,288},{192,320},{... | collective-permute-start | bytes 221192 | tf_op jit(solution)/shard_map/ppermute | solution.py:22
  29.0 1.0 collective-permute-done
  30.0 5.1 %collective-permute-start.3 = (bf16[96,384]{1,0:T(8,128)(2,1)S(1)}, bf16[96,384]{1,0:T(8,128)(2,1)S(1)}, u32[]{:S(2)}, u32[]{:S(2)}) collective-permute-start(bf16[96,384]{1,0:T(8,128)(2,1)S(1)} %slice.109), channel_id=1, source_target_pairs={{0,384},{32,416},{64,448},{96,480},{128,0},{160,32},{192,64},{224,... | collective-permute-start | bytes 221192 | tf_op jit(solution)/shard_map/ppermute | solution.py:22
  35.1 0.0 collective-permute-done.2
  35.1 2.2 %collective-permute-done.3 = bf16[96,384]{1,0:T(8,128)(2,1)S(1)} collective-permute-done((bf16[96,384]{1,0:T(8,128)(2,1)S(1)}, bf16[96,384]{1,0:T(8,128)(2,1)S(1)}, u32[]{:S(2)}, u32[]{:S(2)}) %collective-permute-start.3) | collective-permute-done | bytes 73760 | tf_op jit(solution)/shard_map/ppermute | solution.py:22
  37.3 0.1 pad_maximum_fusion
  37.4 4.7 %collective-permute-start.5 = (bf16[4,192,384]{2,1,0:T(8,128)(2,1)S(1)}, bf16[4,192,384]{2,1,0:T(8,128)(2,1)S(1)}, u32[]{:S(2)}, u32[]{:S(2)}) collective-permute-start(bf16[4,192,384]{2,1,0:T(8,128)(2,1)S(1)} %pad_maximum_fusion), channel_id=1, source_target_pairs={{0,32},{32,64},{64,96},{96,0},{128,160},{160,192},{192,224},{224,1... | collective-permute-start | bytes 1769480 | tf_op jit(solution)/shard_map/ppermute | solution.py:22
  42.1 3.2 %collective-permute-start.4 = (bf16[4,192,384]{2,1,0:T(8,128)(2,1)S(1)}, bf16[4,192,384]{2,1,0:T(8,128)(2,1)S(1)}, u32[]{:S(2)}, u32[]{:S(2)}) collective-permute-start(bf16[4,192,384]{2,1,0:T(8,128)(2,1)S(1)} %pad_maximum_fusion), channel_id=1, source_target_pairs={{0,96},{32,0},{64,32},{96,64},{128,224},{160,128},{192,160},{224,1... | collective-permute-start | bytes 1769480 | tf_op jit(solution)/shard_map/ppermute | solution.py:22
  45.4 8.6 %collective-permute-done.5 = bf16[4,192,384]{2,1,0:T(8,128)(2,1)S(1)} collective-permute-done((bf16[4,192,384]{2,1,0:T(8,128)(2,1)S(1)}, bf16[4,192,384]{2,1,0:T(8,128)(2,1)S(1)}, u32[]{:S(2)}, u32[]{:S(2)}) %collective-permute-start.5) | collective-permute-done | bytes 589856 | tf_op jit(solution)/shard_map/ppermute | solution.py:22
  54.0 2.0 %collective-permute-start.6 = (bf16[4,96,384]{2,1,0:T(8,128)(2,1)S(1)}, bf16[4,96,384]{2,1,0:T(8,128)(2,1)S(1)}, u32[]{:S(2)}, u32[]{:S(2)}) collective-permute-start(bf16[4,96,384]{2,1,0:T(8,128)(2,1)S(1)} %slice.110), channel_id=1, source_target_pairs={{0,32},{32,64},{64,96},{96,0},{128,160},{160,192},{192,224},{224,1... | collective-permute-start | bytes 884744 | tf_op jit(solution)/shard_map/ppermute | solution.py:22
  55.9 0.0 collective-permute-done.4
  56.0 4.5 %collective-permute-start.7 = (bf16[4,96,384]{2,1,0:T(8,128)(2,1)S(1)}, bf16[4,96,384]{2,1,0:T(8,128)(2,1)S(1)}, u32[]{:S(2)}, u32[]{:S(2)}) collective-permute-start(bf16[4,96,384]{2,1,0:T(8,128)(2,1)S(1)} %slice.111), channel_id=1, source_target_pairs={{0,96},{32,0},{64,32},{96,64},{128,224},{160,128},{192,160},{224,1... | collective-permute-start | bytes 884744 | tf_op jit(solution)/shard_map/ppermute | solution.py:22
  60.5 0.1 bitcast_dynamic-update-slice_fusion.4
  60.6 0.1 bitcast_dynamic-update-slice_fusion.2
  60.7 1.9 %collective-permute-done.6 = bf16[4,96,384]{2,1,0:T(8,128)(2,1)S(1)} collective-permute-done((bf16[4,96,384]{2,1,0:T(8,128)(2,1)S(1)}, bf16[4,96,384]{2,1,0:T(8,128)(2,1)S(1)}, u32[]{:S(2)}, u32[]{:S(2)}) %collective-permute-start.6) | collective-permute-done | bytes 294944 | tf_op jit(solution)/shard_map/ppermute | solution.py:22
  62.7 1.5 %collective-permute-done.7 = bf16[4,96,384]{2,1,0:T(8,128)(2,1)S(1)} collective-permute-done((bf16[4,96,384]{2,1,0:T(8,128)(2,1)S(1)}, bf16[4,96,384]{2,1,0:T(8,128)(2,1)S(1)}, u32[]{:S(2)}, u32[]{:S(2)}) %collective-permute-start.7) | collective-permute-done | bytes 294944 | tf_op jit(solution)/shard_map/ppermute | solution.py:22
  64.2 0.1 fusion.9
  64.3 0.1 bitcast_dynamic-update-slice_fusion
  64.4 0.1 bitcast_dynamic-update-slice_fusion.5
  64.5 0.1 bitcast_dynamic-update-slice_fusion.3
  64.6 0.1 fusion.10
  64.7 0.1 bitcast_dynamic-update-slice_fusion.1
  64.8 0.3 constant_dynamic-slice_fusion
  65.1 1.0 fusion.3
  66.1 1.7 %copy.19 = bf16[4,4,192,384]{3,2,1,0:T(8,128)(2,1)} copy(bf16[4,4,192,384]{3,2,0,1:T(8,128)(2,1)S(1)} %fusion.3) | data formatting | bytes 4718592 | tf_op jit(solution)/shard_map/transpose | solution.py:42
  67.8 13.4 %all-to-all-start = ((bf16[32,96,384]{2,1,0:T(8,128)(2,1)}), bf16[32,96,384]{2,1,0:T(8,128)(2,1)S(1)}, u32[]{:S(2)}, u32[]{:S(2)}) async-start(bf16[32,96,384]{2,1,0:T(8,128)(2,1)} %bitcast.19), calls=%async_computation | async-start | bytes 4718592 | tf_op jit(solution)/shard_map/all_to_all | solution.py:81
  81.2 0.0 copy-done.3
  81.2 0.0 copy-done.4
  81.2 0.1 multiply_select_fusion
  81.3 55.3 %all-to-all-done = bf16[32,96,384]{2,1,0:T(8,128)(2,1)S(1)} async-done(((bf16[32,96,384]{2,1,0:T(8,128)(2,1)}), bf16[32,96,384]{2,1,0:T(8,128)(2,1)S(1)}, u32[]{:S(2)}, u32[]{:S(2)}) %all-to-all-start) | async-done | bytes 2359328 | tf_op jit(solution)/shard_map/all_to_all | solution.py:81
  136.6 0.1 slice_bitcast_fusion.2
  136.7 0.1 copy.21
  136.8 0.0 all-gather.3.cloned.1.call-done
  136.8 3.7 %fusion = f32[2,2,384,384,1]{3,2,1,0,4:T(8,128)S(1)} fusion(bf16[32,2,2,48,384]{4,3,2,1,0:T(8,128)(2,1)} %bitcast.91, bf16[32,2,48,384]{3,2,1,0:T(8,128)(2,1)S(1)} %bitcast.72), kind=kOutput, calls=%fused_computation.2 | convolution fusion | flops 1207959552 | bytes 7077888 | tf_op jit(solution)/shard_map/ckibr,ckbq->kirq/dot_general | solution.py:93
  140.6 0.0 copy-start.1
  140.6 2.8 %convolution_convert_fusion = bf16[2,2,32,16,384]{4,3,2,1,0:T(8,128)(2,1)S(1)} fusion(bf16[32,2,2,48,384]{4,3,2,1,0:T(8,128)(2,1)} %bitcast.92, f32[2,2,384,384,1]{3,2,1,0,4:T(8,128)S(1)} %fusion, f32[2,384]{1,0:T(2,128)S(1)} %bitcast.90, f32[2,2,384]{2,0,1:T(2,128)S(1)} %copy.15), kind=kOutput, calls=%fused_computation.10 | convolution fusion | flops 606535680 | bytes 5514240 | tf_op jit(solution)/shard_map/ckimr,kirq->kicmq/dot_general | solution.py:95
  143.4 2.3 %bitcast_subtract_fusion = f32[1024,512]{1,0:T(8,128)} fusion(f32[1024,512]{1,0:T(8,128)S(1)} %copy-done.1, bf16[1024,2,384]{2,0,1:T(8,128)(2,1)S(1)} %bitcast.85, bf16[2,512,384]{2,1,0:T(8,128)(2,1)S(1)} %bitcast.73), kind=kOutput, calls=%fused_computation.9 | convolution fusion | flops 805830656 | bytes 6553600 | tf_op jit(solution)/shard_map/kicmq,knq->icmn/dot_general | solution.py:97
  (25 shorter events, 0.2 us)
Async XLA Ops:
  6.5 1.6 %copy-start = (f32[2,2,2,512]{3,2,1,0:T(2,128)S(1)}, f32[2,2,2,512]{3,2,1,0:T(2,128)}, u32[]{:S(2)}) copy-start(f32[2,2,2,512]{3,2,1,0:T(2,128)} %param.13) | copy-start | bytes 49156
  6.5 3.9 %copy-start.2 = (bf16[2,2,16,384]{3,2,1,0:T(8,128)(2,1)S(1)}, bf16[2,2,16,384]{3,2,1,0:T(8,128)(2,1)}, u32[]{:S(2)}) copy-start(bf16[2,2,16,384]{3,2,1,0:T(8,128)(2,1)} %param.8) | copy-start | bytes 147460
  6.5 130.3 %all-gather.3.cloned.1.call-start = ((), (), s32[]{:S(2)}) async-start(), calls=%async_computation.1 | async-start | bytes 4866048 | tf_op jit(solution)/shard_map/all_gather | solution.py:57
  10.5 14.5 %collective-permute-start.1 = (bf16[192,384]{1,0:T(8,128)(2,1)S(1)}, bf16[192,384]{1,0:T(8,128)(2,1)S(1)}, u32[]{:S(2)}, u32[]{:S(2)}) collective-permute-start(bf16[192,384]{1,0:T(8,128)(2,1)S(1)} %bitcast.74), channel_id=1, source_target_pairs={{0,128},{32,160},{64,192},{96,224},{128,256},{160,288},{192,320},{... | collective-permute-start | bytes 442376 | tf_op jit(solution)/shard_map/ppermute | solution.py:22
  17.1 12.9 %collective-permute-start = (bf16[192,384]{1,0:T(8,128)(2,1)S(1)}, bf16[192,384]{1,0:T(8,128)(2,1)S(1)}, u32[]{:S(2)}, u32[]{:S(2)}) collective-permute-start(bf16[192,384]{1,0:T(8,128)(2,1)S(1)} %bitcast.75), channel_id=1, source_target_pairs={{0,384},{32,416},{64,448},{96,480},{128,0},{160,32},{192,64},{224,... | collective-permute-start | bytes 442376 | tf_op jit(solution)/shard_map/ppermute | solution.py:22
  25.1 10.1 %collective-permute-start.2 = (bf16[96,384]{1,0:T(8,128)(2,1)S(1)}, bf16[96,384]{1,0:T(8,128)(2,1)S(1)}, u32[]{:S(2)}, u32[]{:S(2)}) collective-permute-start(bf16[96,384]{1,0:T(8,128)(2,1)S(1)} %slice.108), channel_id=1, source_target_pairs={{0,128},{32,160},{64,192},{96,224},{128,256},{160,288},{192,320},{... | collective-permute-start | bytes 221192 | tf_op jit(solution)/shard_map/ppermute | solution.py:22
  30.0 7.3 %collective-permute-start.3 = (bf16[96,384]{1,0:T(8,128)(2,1)S(1)}, bf16[96,384]{1,0:T(8,128)(2,1)S(1)}, u32[]{:S(2)}, u32[]{:S(2)}) collective-permute-start(bf16[96,384]{1,0:T(8,128)(2,1)S(1)} %slice.109), channel_id=1, source_target_pairs={{0,384},{32,416},{64,448},{96,480},{128,0},{160,32},{192,64},{224,... | collective-permute-start | bytes 221192 | tf_op jit(solution)/shard_map/ppermute | solution.py:22
  37.4 16.5 %collective-permute-start.5 = (bf16[4,192,384]{2,1,0:T(8,128)(2,1)S(1)}, bf16[4,192,384]{2,1,0:T(8,128)(2,1)S(1)}, u32[]{:S(2)}, u32[]{:S(2)}) collective-permute-start(bf16[4,192,384]{2,1,0:T(8,128)(2,1)S(1)} %pad_maximum_fusion), channel_id=1, source_target_pairs={{0,32},{32,64},{64,96},{96,0},{128,160},{160,192},{192,224},{224,1... | collective-permute-start | bytes 1769480 | tf_op jit(solution)/shard_map/ppermute | solution.py:22
  42.1 13.8 %collective-permute-start.4 = (bf16[4,192,384]{2,1,0:T(8,128)(2,1)S(1)}, bf16[4,192,384]{2,1,0:T(8,128)(2,1)S(1)}, u32[]{:S(2)}, u32[]{:S(2)}) collective-permute-start(bf16[4,192,384]{2,1,0:T(8,128)(2,1)S(1)} %pad_maximum_fusion), channel_id=1, source_target_pairs={{0,96},{32,0},{64,32},{96,64},{128,224},{160,128},{192,160},{224,1... | collective-permute-start | bytes 1769480 | tf_op jit(solution)/shard_map/ppermute | solution.py:22
  54.0 8.7 %collective-permute-start.6 = (bf16[4,96,384]{2,1,0:T(8,128)(2,1)S(1)}, bf16[4,96,384]{2,1,0:T(8,128)(2,1)S(1)}, u32[]{:S(2)}, u32[]{:S(2)}) collective-permute-start(bf16[4,96,384]{2,1,0:T(8,128)(2,1)S(1)} %slice.110), channel_id=1, source_target_pairs={{0,32},{32,64},{64,96},{96,0},{128,160},{160,192},{192,224},{224,1... | collective-permute-start | bytes 884744 | tf_op jit(solution)/shard_map/ppermute | solution.py:22
  56.0 8.2 %collective-permute-start.7 = (bf16[4,96,384]{2,1,0:T(8,128)(2,1)S(1)}, bf16[4,96,384]{2,1,0:T(8,128)(2,1)S(1)}, u32[]{:S(2)}, u32[]{:S(2)}) collective-permute-start(bf16[4,96,384]{2,1,0:T(8,128)(2,1)S(1)} %slice.111), channel_id=1, source_target_pairs={{0,96},{32,0},{64,32},{96,64},{128,224},{160,128},{192,160},{224,1... | collective-permute-start | bytes 884744 | tf_op jit(solution)/shard_map/ppermute | solution.py:22
  67.8 13.4 %copy-start.5 = (s32[2,32]{1,0:T(2,128)S(1)}, s32[2,32]{1,0:T(2,128)}, u32[]{:S(2)}) copy-start(s32[2,32]{1,0:T(2,128)} %param.12) | copy-start | bytes 772
  67.8 13.4 %copy-start.3 = (f32[2,32,384]{2,1,0:T(8,128)S(1)}, f32[2,32,384]{2,1,0:T(8,128)}, u32[]{:S(2)}) copy-start(f32[2,32,384]{2,1,0:T(8,128)} %param.11) | copy-start | bytes 294916
  67.8 13.4 %copy-start.4 = (f32[2,32,384]{2,1,0:T(8,128)S(1)}, f32[2,32,384]{2,1,0:T(8,128)}, u32[]{:S(2)}) copy-start(f32[2,32,384]{2,1,0:T(8,128)} %param.10) | copy-start | bytes 294916
  67.8 68.8 %all-to-all-start = ((bf16[32,96,384]{2,1,0:T(8,128)(2,1)}), bf16[32,96,384]{2,1,0:T(8,128)(2,1)S(1)}, u32[]{:S(2)}, u32[]{:S(2)}) async-start(bf16[32,96,384]{2,1,0:T(8,128)(2,1)} %bitcast.19), calls=%async_computation | async-start | bytes 4718592 | tf_op jit(solution)/shard_map/all_to_all | solution.py:81
  140.6 2.8 %copy-start.1 = (f32[1024,512]{1,0:T(8,128)S(1)}, f32[1024,512]{1,0:T(8,128)}, u32[]{:S(2)}) copy-start(f32[1024,512]{1,0:T(8,128)} %param.7) | copy-start | bytes 6291460
Sparse Core Ops, SparseCore 0:
  9.5 76.5 all-gather.2

commit v15 on v12

--- a/solution.py
+++ b/solution.py
@@ -22,14 +22,14 @@
         return lax.ppermute(value, "row", [(r, target(r, step)) for r in range(n_all)])
 
     if not forward:
-        return jnp.stack([block] + [shift(block, -d) for d in range(1, 4)])
+        return [block] + [shift(block, -d) for d in range(1, 4)]
     from_behind = shift(block, 1)
     from_ahead = shift(block, -1)
     half = block.shape[-2] // 2
     far = jnp.concatenate(
         [shift(from_behind[..., :half, :], 1), shift(from_ahead[..., half:, :], -1)], axis=-2
     )
-    return jnp.stack([block, from_ahead, far, from_behind])
+    return [block, from_ahead, far, from_behind]
 
 
 def replicate_over_row(block, n_row):
@@ -37,9 +37,11 @@
     n_z = n_row // n_x
     row = lax.axis_index("row")
     z, x = row // n_x, row % n_x
-    by_z = ring_gather(block, n_z, n_x, outer=True)
-    by_xz = ring_gather(by_z, n_z, n_x, outer=False)
-    by_zx = jnp.roll(jnp.roll(by_xz, x, axis=0), z, axis=1).swapaxes(0, 1)
+    by_z = jnp.stack(ring_gather(block, n_z, n_x, outer=True))
+    by_z = jnp.roll(by_z, z, axis=0)
+    by_zx = jnp.zeros((n_z, n_x) + block.shape, block.dtype)
+    for d, piece in enumerate(ring_gather(by_z, n_z, n_x, outer=False)):
+        by_zx = lax.dynamic_update_slice(by_zx, piece[:, None], (0, (x + d) % n_x, 0, 0))
     return by_zx.reshape((n_row,) + block.shape)
 
 

time: 154 us -> 155 us (level)
  local copies, waits for them, and re-layouts: 2.94 us -> 4.49 us
    transpose x1 -> x0, local copies, waits for them, and re-layouts: 1.7 us -> none  [replicate_over_row(): by_zx = jnp.roll(jnp.roll(by_xz, x, axis=0), z, axis=1).swapaxes(0, 1)]
where the time goes in v15:
time: 155 us; the launch traced here: 154 us
  waiting for transfers between devices  72 us (46%)
  starting transfers between devices  50.1 us (32%)
  between operations  13.9 us (9%)
  matrix products  8.85 us (6%)
  other arithmetic  4.85 us (3%)
  local copies, waits for them, and re-layouts  4.49 us (3%)
    all_to_all x1, waiting for transfers between devices, local(): col_all = lax.all_to_all(every_tile, 'col', 0, 0, tiled=True)  55.3 us
    ppermute x8, starting transfers between devices, shift(): lax.ppermute(value, 'row', [(r, target(r, step)) for r in range(n_all)])  36.8 us
    ppermute x8, waiting for transfers between devices, shift(): lax.ppermute(value, 'row', [(r, target(r, step)) for r in range(n_all)])  16.7 us
    all_to_all x1, starting transfers between devices, local(): col_all = lax.all_to_all(every_tile, 'col', 0, 0, tiled=True)  13.3 us
    dot_general x1, matrix products, local(): jnp.einsum('cikbr,ckbq->kirq', row_v, col_scaled, preferred_element_type=...  3.75 us
  transfers between devices with their start and end apart: 10, of which 7 were waited for; matrix products, arithmetic and copies ran while one was open for 4% of the time, Pallas kernels for 0%

profile of v15, /device:TPU:1, one launch (start us, length us, event | category | flops | bytes accessed | tf_op | source)
XLA Modules:
  0.0 154.2 jit_solution(6931311953439940388)
XLA Ops:
  6.5 0.0 copy-start
  6.5 0.0 all-gather.3.cloned.1.call-start
  6.5 1.6 %copy_bitcast_fusion = bf16[2,2,48,384]{3,2,1,0:T(8,128)(2,1)} fusion(bf16[2,2,32,384]{3,2,1,0:T(8,128)(2,1)} %param.9, bf16[2,2,16,384]{3,2,1,0:T(8,128)(2,1)} %param.8), kind=kLoop, calls=%fused_computation.28 | loop fusion | flops 294912 | bytes 294912 | tf_op jit(solution)/shard_map/transpose | solution.py:57
  8.1 0.0 all-gather.3.cloned.1.call-update
  8.2 0.0 copy-done
  8.2 0.1 constant_dynamic-slice_fusion.1
  8.2 0.1 broadcast_in_dim.46
  8.3 0.1 reshape.117
  8.5 0.9 copy_convert_fusion
  9.4 1.0 fusion.10
  10.4 0.0 copy-done.3
  10.5 6.6 %collective-permute-start.1 = (bf16[192,384]{1,0:T(8,128)(2,1)S(1)}, bf16[192,384]{1,0:T(8,128)(2,1)S(1)}, u32[]{:S(2)}, u32[]{:S(2)}) collective-permute-start(bf16[192,384]{1,0:T(8,128)(2,1)S(1)} %bitcast.81), channel_id=1, source_target_pairs={{0,128},{32,160},{64,192},{96,224},{128,256},{160,288},{192,320},{... | collective-permute-start | bytes 442376 | tf_op jit(solution)/shard_map/ppermute | solution.py:22
  17.1 6.8 %collective-permute-start = (bf16[192,384]{1,0:T(8,128)(2,1)S(1)}, bf16[192,384]{1,0:T(8,128)(2,1)S(1)}, u32[]{:S(2)}, u32[]{:S(2)}) collective-permute-start(bf16[192,384]{1,0:T(8,128)(2,1)S(1)} %bitcast.82), channel_id=1, source_target_pairs={{0,384},{32,416},{64,448},{96,480},{128,0},{160,32},{192,64},{224,... | collective-permute-start | bytes 442376 | tf_op jit(solution)/shard_map/ppermute | solution.py:22
  24.0 1.0 collective-permute-done.1
  25.0 4.0 %collective-permute-start.2 = (bf16[96,384]{1,0:T(8,128)(2,1)S(1)}, bf16[96,384]{1,0:T(8,128)(2,1)S(1)}, u32[]{:S(2)}, u32[]{:S(2)}) collective-permute-start(bf16[96,384]{1,0:T(8,128)(2,1)S(1)} %slice.108), channel_id=1, source_target_pairs={{0,128},{32,160},{64,192},{96,224},{128,256},{160,288},{192,320},{... | collective-permute-start | bytes 221192 | tf_op jit(solution)/shard_map/ppermute | solution.py:22
  29.0 1.0 collective-permute-done
  30.0 5.1 %collective-permute-start.3 = (bf16[96,384]{1,0:T(8,128)(2,1)S(1)}, bf16[96,384]{1,0:T(8,128)(2,1)S(1)}, u32[]{:S(2)}, u32[]{:S(2)}) collective-permute-start(bf16[96,384]{1,0:T(8,128)(2,1)S(1)} %slice.109), channel_id=1, source_target_pairs={{0,384},{32,416},{64,448},{96,480},{128,0},{160,32},{192,64},{224,... | collective-permute-start | bytes 221192 | tf_op jit(solution)/shard_map/ppermute | solution.py:22
  35.1 0.0 collective-permute-done.2
  35.1 2.1 %collective-permute-done.3 = bf16[96,384]{1,0:T(8,128)(2,1)S(1)} collective-permute-done((bf16[96,384]{1,0:T(8,128)(2,1)S(1)}, bf16[96,384]{1,0:T(8,128)(2,1)S(1)}, u32[]{:S(2)}, u32[]{:S(2)}) %collective-permute-start.3) | collective-permute-done | bytes 73760 | tf_op jit(solution)/shard_map/ppermute | solution.py:22
  37.5 0.3 broadcast_in_dim.44
  37.8 0.2 bitcast_dynamic-update-slice_fusion.2
  38.0 4.7 %collective-permute-start.5 = (bf16[4,192,384]{2,1,0:T(8,128)(2,1)S(1)}, bf16[4,192,384]{2,1,0:T(8,128)(2,1)S(1)}, u32[]{:S(2)}, u32[]{:S(2)}) collective-permute-start(bf16[4,192,384]{2,1,0:T(8,128)(2,1)S(1)} %get-tuple-element.6), channel_id=1, source_target_pairs={{0,32},{32,64},{64,96},{96,0},{128,160},{160,192},{192,224},{224,1... | collective-permute-start | bytes 1769480 | tf_op jit(solution)/shard_map/ppermute | solution.py:22
  42.7 3.2 %collective-permute-start.4 = (bf16[4,192,384]{2,1,0:T(8,128)(2,1)S(1)}, bf16[4,192,384]{2,1,0:T(8,128)(2,1)S(1)}, u32[]{:S(2)}, u32[]{:S(2)}) collective-permute-start(bf16[4,192,384]{2,1,0:T(8,128)(2,1)S(1)} %get-tuple-element.6), channel_id=1, source_target_pairs={{0,96},{32,0},{64,32},{96,64},{128,224},{160,128},{192,160},{224,1... | collective-permute-start | bytes 1769480 | tf_op jit(solution)/shard_map/ppermute | solution.py:22
  45.9 8.7 %collective-permute-done.5 = bf16[4,192,384]{2,1,0:T(8,128)(2,1)S(1)} collective-permute-done((bf16[4,192,384]{2,1,0:T(8,128)(2,1)S(1)}, bf16[4,192,384]{2,1,0:T(8,128)(2,1)S(1)}, u32[]{:S(2)}, u32[]{:S(2)}) %collective-permute-start.5) | collective-permute-done | bytes 589856 | tf_op jit(solution)/shard_map/ppermute | solution.py:22
  54.6 0.8 slice.110
  55.3 1.9 %collective-permute-start.6 = (bf16[4,96,384]{2,1,0:T(8,128)(2,1)}, bf16[4,96,384]{2,1,0:T(8,128)(2,1)}, u32[]{:S(2)}, u32[]{:S(2)}) collective-permute-start(bf16[4,96,384]{2,1,0:T(8,128)(2,1)} %slice.110), channel_id=1, source_target_pairs={{0,32},{32,64},{64,96},{96,0},{128,160},{160,192},{192,224},{224,1... | collective-permute-start | bytes 884744 | tf_op jit(solution)/shard_map/ppermute | solution.py:22
  57.2 0.0 collective-permute-done.4
  57.3 0.7 slice.111
  58.0 4.6 %collective-permute-start.7 = (bf16[4,96,384]{2,1,0:T(8,128)(2,1)}, bf16[4,96,384]{2,1,0:T(8,128)(2,1)}, u32[]{:S(2)}, u32[]{:S(2)}) collective-permute-start(bf16[4,96,384]{2,1,0:T(8,128)(2,1)} %slice.111), channel_id=1, source_target_pairs={{0,96},{32,0},{64,32},{96,64},{128,224},{160,128},{192,160},{224,1... | collective-permute-start | bytes 884744 | tf_op jit(solution)/shard_map/ppermute | solution.py:22
  62.6 0.1 bitcast_dynamic-update-slice_fusion.1
  62.7 1.6 %collective-permute-done.6 = bf16[4,96,384]{2,1,0:T(8,128)(2,1)} collective-permute-done((bf16[4,96,384]{2,1,0:T(8,128)(2,1)}, bf16[4,96,384]{2,1,0:T(8,128)(2,1)}, u32[]{:S(2)}, u32[]{:S(2)}) %collective-permute-start.6) | collective-permute-done | bytes 294944 | tf_op jit(solution)/shard_map/ppermute | solution.py:22
  64.3 2.2 %collective-permute-done.7 = bf16[4,96,384]{2,1,0:T(8,128)(2,1)} collective-permute-done((bf16[4,96,384]{2,1,0:T(8,128)(2,1)}, bf16[4,96,384]{2,1,0:T(8,128)(2,1)}, u32[]{:S(2)}, u32[]{:S(2)}) %collective-permute-start.7) | collective-permute-done | bytes 294944 | tf_op jit(solution)/shard_map/ppermute | solution.py:22
  66.5 1.2 fusion.7
  67.7 0.2 copy.25
  68.0 0.1 bitcast_dynamic-update-slice_fusion
  68.1 0.0 copy-start.1
  68.1 1.4 copy-done.1
  69.5 13.3 %all-to-all-start = ((bf16[32,96,384]{2,1,0:T(8,128)(2,1)}), bf16[32,96,384]{2,1,0:T(8,128)(2,1)S(1)}, u32[]{:S(2)}, u32[]{:S(2)}) async-start(bf16[32,96,384]{2,1,0:T(8,128)(2,1)} %bitcast.76), calls=%async_computation | async-start | bytes 4718592 | tf_op jit(solution)/shard_map/all_to_all | solution.py:83
  82.8 0.0 copy-done.6
  82.8 0.1 multiply_select_fusion
  83.0 55.3 %all-to-all-done = bf16[32,96,384]{2,1,0:T(8,128)(2,1)S(1)} async-done(((bf16[32,96,384]{2,1,0:T(8,128)(2,1)}), bf16[32,96,384]{2,1,0:T(8,128)(2,1)S(1)}, u32[]{:S(2)}, u32[]{:S(2)}) %all-to-all-start) | async-done | bytes 2359328 | tf_op jit(solution)/shard_map/all_to_all | solution.py:83
  138.3 0.1 slice_bitcast_fusion.2
  138.4 0.1 copy.28
  138.5 0.0 all-gather.3.cloned.1.call-done
  138.5 3.7 %fusion = f32[2,2,384,384,1]{3,2,1,0,4:T(8,128)S(1)} fusion(bf16[32,2,48,384]{3,2,1,0:T(8,128)(2,1)S(1)} %bitcast.78, bf16[32,2,2,48,384]{4,3,2,1,0:T(8,128)(2,1)} %bitcast.90), kind=kOutput, calls=%fused_computation | convolution fusion | flops 1207959552 | bytes 7077888 | tf_op jit(solution)/shard_map/cikbr,ckbq->kirq/dot_general | solution.py:95
  142.2 0.0 copy-start.2
  142.2 2.8 %convolution_convert_fusion = bf16[2,2,32,16,384]{4,3,2,1,0:T(8,128)(2,1)S(1)} fusion(bf16[32,2,2,48,384]{4,3,2,1,0:T(8,128)(2,1)} %bitcast.91, f32[2,2,384,384,1]{3,2,1,0,4:T(8,128)S(1)} %fusion, f32[2,384]{1,0:T(2,128)S(1)} %bitcast.89, f32[2,2,384]{2,0,1:T(2,128)S(1)} %copy.22), kind=kOutput, calls=%fused_computation.6 | convolution fusion | flops 606535680 | bytes 5514240 | tf_op jit(solution)/shard_map/cikmr,kirq->kicmq/dot_general | solution.py:97
  145.0 2.3 %bitcast_subtract_fusion = f32[1024,512]{1,0:T(8,128)} fusion(f32[1024,512]{1,0:T(8,128)S(1)} %copy-done.2, bf16[1024,2,384]{2,0,1:T(8,128)(2,1)S(1)} %bitcast.80, bf16[2,512,384]{2,1,0:T(8,128)(2,1)S(1)} %bitcast.79), kind=kOutput, calls=%fused_computation.5 | convolution fusion | flops 805830656 | bytes 6553600 | tf_op jit(solution)/shard_map/kicmq,knq->icmn/dot_general | solution.py:99
  (28 shorter events, 0.3 us)
Async XLA Ops:
  6.5 1.6 %copy-start = (f32[2,2,2,512]{3,2,1,0:T(2,128)S(1)}, f32[2,2,2,512]{3,2,1,0:T(2,128)}, u32[]{:S(2)}) copy-start(f32[2,2,2,512]{3,2,1,0:T(2,128)} %param.13) | copy-start | bytes 49156
  6.5 3.9 %copy-start.3 = (bf16[2,2,16,384]{3,2,1,0:T(8,128)(2,1)S(1)}, bf16[2,2,16,384]{3,2,1,0:T(8,128)(2,1)}, u32[]{:S(2)}) copy-start(bf16[2,2,16,384]{3,2,1,0:T(8,128)(2,1)} %param.8) | copy-start | bytes 147460
  6.5 131.9 %all-gather.3.cloned.1.call-start = ((), (), s32[]{:S(2)}) async-start(), calls=%async_computation.1 | async-start | bytes 4866048 | tf_op jit(solution)/shard_map/all_gather | solution.py:59
  10.5 14.5 %collective-permute-start.1 = (bf16[192,384]{1,0:T(8,128)(2,1)S(1)}, bf16[192,384]{1,0:T(8,128)(2,1)S(1)}, u32[]{:S(2)}, u32[]{:S(2)}) collective-permute-start(bf16[192,384]{1,0:T(8,128)(2,1)S(1)} %bitcast.81), channel_id=1, source_target_pairs={{0,128},{32,160},{64,192},{96,224},{128,256},{160,288},{192,320},{... | collective-permute-start | bytes 442376 | tf_op jit(solution)/shard_map/ppermute | solution.py:22
  17.1 12.9 %collective-permute-start = (bf16[192,384]{1,0:T(8,128)(2,1)S(1)}, bf16[192,384]{1,0:T(8,128)(2,1)S(1)}, u32[]{:S(2)}, u32[]{:S(2)}) collective-permute-start(bf16[192,384]{1,0:T(8,128)(2,1)S(1)} %bitcast.82), channel_id=1, source_target_pairs={{0,384},{32,416},{64,448},{96,480},{128,0},{160,32},{192,64},{224,... | collective-permute-start | bytes 442376 | tf_op jit(solution)/shard_map/ppermute | solution.py:22
  25.0 10.1 %collective-permute-start.2 = (bf16[96,384]{1,0:T(8,128)(2,1)S(1)}, bf16[96,384]{1,0:T(8,128)(2,1)S(1)}, u32[]{:S(2)}, u32[]{:S(2)}) collective-permute-start(bf16[96,384]{1,0:T(8,128)(2,1)S(1)} %slice.108), channel_id=1, source_target_pairs={{0,128},{32,160},{64,192},{96,224},{128,256},{160,288},{192,320},{... | collective-permute-start | bytes 221192 | tf_op jit(solution)/shard_map/ppermute | solution.py:22
  30.0 7.3 %collective-permute-start.3 = (bf16[96,384]{1,0:T(8,128)(2,1)S(1)}, bf16[96,384]{1,0:T(8,128)(2,1)S(1)}, u32[]{:S(2)}, u32[]{:S(2)}) collective-permute-start(bf16[96,384]{1,0:T(8,128)(2,1)S(1)} %slice.109), channel_id=1, source_target_pairs={{0,384},{32,416},{64,448},{96,480},{128,0},{160,32},{192,64},{224,... | collective-permute-start | bytes 221192 | tf_op jit(solution)/shard_map/ppermute | solution.py:22
  38.0 16.6 %collective-permute-start.5 = (bf16[4,192,384]{2,1,0:T(8,128)(2,1)S(1)}, bf16[4,192,384]{2,1,0:T(8,128)(2,1)S(1)}, u32[]{:S(2)}, u32[]{:S(2)}) collective-permute-start(bf16[4,192,384]{2,1,0:T(8,128)(2,1)S(1)} %get-tuple-element.6), channel_id=1, source_target_pairs={{0,32},{32,64},{64,96},{96,0},{128,160},{160,192},{192,224},{224,1... | collective-permute-start | bytes 1769480 | tf_op jit(solution)/shard_map/ppermute | solution.py:22
  42.7 14.6 %collective-permute-start.4 = (bf16[4,192,384]{2,1,0:T(8,128)(2,1)S(1)}, bf16[4,192,384]{2,1,0:T(8,128)(2,1)S(1)}, u32[]{:S(2)}, u32[]{:S(2)}) collective-permute-start(bf16[4,192,384]{2,1,0:T(8,128)(2,1)S(1)} %get-tuple-element.6), channel_id=1, source_target_pairs={{0,96},{32,0},{64,32},{96,64},{128,224},{160,128},{192,160},{224,1... | collective-permute-start | bytes 1769480 | tf_op jit(solution)/shard_map/ppermute | solution.py:22
  55.3 9.0 %collective-permute-start.6 = (bf16[4,96,384]{2,1,0:T(8,128)(2,1)}, bf16[4,96,384]{2,1,0:T(8,128)(2,1)}, u32[]{:S(2)}, u32[]{:S(2)}) collective-permute-start(bf16[4,96,384]{2,1,0:T(8,128)(2,1)} %slice.110), channel_id=1, source_target_pairs={{0,32},{32,64},{64,96},{96,0},{128,160},{160,192},{192,224},{224,1... | collective-permute-start | bytes 884744 | tf_op jit(solution)/shard_map/ppermute | solution.py:22
  58.0 8.5 %collective-permute-start.7 = (bf16[4,96,384]{2,1,0:T(8,128)(2,1)}, bf16[4,96,384]{2,1,0:T(8,128)(2,1)}, u32[]{:S(2)}, u32[]{:S(2)}) collective-permute-start(bf16[4,96,384]{2,1,0:T(8,128)(2,1)} %slice.111), channel_id=1, source_target_pairs={{0,96},{32,0},{64,32},{96,64},{128,224},{160,128},{192,160},{224,1... | collective-permute-start | bytes 884744 | tf_op jit(solution)/shard_map/ppermute | solution.py:22
  68.1 1.4 copy-start.1
  69.5 13.3 %copy-start.6 = (s32[2,32]{1,0:T(2,128)S(1)}, s32[2,32]{1,0:T(2,128)}, u32[]{:S(2)}) copy-start(s32[2,32]{1,0:T(2,128)} %param.12) | copy-start | bytes 772
  69.5 13.3 %copy-start.4 = (f32[2,32,384]{2,1,0:T(8,128)S(1)}, f32[2,32,384]{2,1,0:T(8,128)}, u32[]{:S(2)}) copy-start(f32[2,32,384]{2,1,0:T(8,128)} %param.11) | copy-start | bytes 294916
  69.5 13.3 %copy-start.5 = (f32[2,32,384]{2,1,0:T(8,128)S(1)}, f32[2,32,384]{2,1,0:T(8,128)}, u32[]{:S(2)}) copy-start(f32[2,32,384]{2,1,0:T(8,128)} %param.10) | copy-start | bytes 294916
  69.5 68.8 %all-to-all-start = ((bf16[32,96,384]{2,1,0:T(8,128)(2,1)}), bf16[32,96,384]{2,1,0:T(8,128)(2,1)S(1)}, u32[]{:S(2)}, u32[]{:S(2)}) async-start(bf16[32,96,384]{2,1,0:T(8,128)(2,1)} %bitcast.76), calls=%async_computation | async-start | bytes 4718592 | tf_op jit(solution)/shard_map/all_to_all | solution.py:83
  142.2 2.8 %copy-start.2 = (f32[1024,512]{1,0:T(8,128)S(1)}, f32[1024,512]{1,0:T(8,128)}, u32[]{:S(2)}) copy-start(f32[1024,512]{1,0:T(8,128)} %param.7) | copy-start | bytes 6291460
Sparse Core Ops, SparseCore 0:
  9.5 76.3 all-gather.2
